TPU v7x, 256 devices: a whole 4x4x8 slice. The times are simulated.
256 devices in a mesh: req: 64 (over y, z, core), tp: 4 (over x).
Axes of the slice: x: 4, y: 4, z: 8, core: 2. Of those that a mesh axis runs over, the one named last changes fastest.
Arguments:
- queries: bfloat16 [64, 1280, 24, 128], P('req', None, 'tp'), may hold values from -25 to 25
- text_kv: bfloat16 [64, 1280, 4, 256], P('req', None, 'tp'), may hold values from -6 to 6
- image_rows: bfloat16 [32768, 6144], P('req', 'tp'), may hold values from -6 to 6
- row_request: int32 [32768], P('req'), may hold values from 0 to 63, as said below
- row_position: int32 [32768], P('req'), may hold values from 8 to 1263, as said below
- prompt_lengths: int32 [64], P('req'), may hold values from 24 to 1280, as said below
- kv_weight: bfloat16 [6144, 4, 256], P('tp'), may hold values from -0.078125 to 0.078125
Outputs:
- attended: bfloat16 [64, 1280, 24, 128], P('req', None, 'tp')
Inputs may be any that keep to these rules, and one draw needn't show every extreme that they name: `row_request`: the rows of one device name one request at most 16 times, and on every device some request is named exactly 16 times. `row_position`: the rows naming one request take distinct positions, 8 or more, that form one run ending at least 16 positions before that request's length. `prompt_lengths`: some request has length exactly 1280.
All inputs are finite; a program needn't handle non-finite values.
Results may differ from a plain program's by a relative error of at most 0.0085.
Values may be sent and summed in bfloat16 or wider, within the bound.
No kernel may reach another device: no remote copies, remote signals or barrier semaphores. Data moves between devices by JAX's collectives and lax.ppermute only.
A program may use at most 128 MiB of HBM per device.

v0:
```python
import math

import jax
import jax.numpy as jnp
from jax import lax
from jax.sharding import PartitionSpec as P


def rotate_keys(summed, positions, head_dim):
    half = head_dim // 2
    freqs = jnp.exp(jnp.arange(half, dtype=jnp.float32) * (-2.0 * math.log(1000000.0) / head_dim))
    angles = positions.astype(jnp.float32)[:, None, None] * freqs[None, None, :]
    cosine = jnp.cos(angles)
    sine = jnp.sin(angles)
    first = summed[..., :half]
    second = summed[..., half:head_dim]
    rotated = jnp.concatenate(
        [first * cosine - second * sine, second * cosine + first * sine, summed[..., head_dim:]],
        axis=-1,
    )
    return rotated.astype(jnp.bfloat16)


def per_device(queries, text_kv, image_rows, row_request, row_position, prompt_lengths, kv_weight):
    groups = lax.axis_size("req")
    own_rows = image_rows.shape[0]
    capacity = 2 * own_rows // groups
    prompt = queries.shape[1]
    head_dim = queries.shape[3]
    local_heads = kv_weight.shape[1] // lax.axis_size("tp")
    one_hot = (row_request[:, None] == jnp.arange(groups, dtype=jnp.int32)[None, :]).astype(
        jnp.int32
    )
    before = jnp.cumsum(one_hot, axis=0) - one_hot
    slot_index = jnp.sum(before * one_hot, axis=1)
    target = row_request * capacity + slot_index
    pos_buffer = (
        jnp.full((groups * capacity,), prompt, jnp.int32)
        .at[target]
        .set(row_position)
        .reshape(groups, capacity)
    )
    row_buffer = (
        jnp.zeros((groups * capacity, image_rows.shape[1]), jnp.bfloat16).at[target].set(image_rows)
    )
    row_buffer = row_buffer.reshape(groups, capacity, image_rows.shape[1])
    got_rows, got_pos = (
        lax.all_to_all(row_buffer, "req", split_axis=0, concat_axis=0, tiled=True),
        lax.all_to_all(pos_buffer, "req", split_axis=0, concat_axis=0, tiled=True),
    )
    flat_rows = got_rows.reshape(groups * capacity, image_rows.shape[1])
    places = got_pos.reshape(groups * capacity)
    summed = lax.psum_scatter(
        jnp.einsum("rd,dhc->hrc", flat_rows, kv_weight, preferred_element_type=jnp.float32),
        "tp",
        scatter_dimension=0,
        tiled=True,
    )
    image_kv = rotate_keys(jnp.transpose(summed, (1, 0, 2)), places, head_dim)
    prompt_kv = text_kv[0].at[places].set(image_kv, mode="drop")
    length = prompt_lengths[0]
    local_query_heads = queries.shape[2]
    group = local_query_heads // local_heads
    grouped = queries[0].reshape(prompt, local_heads, group, head_dim)
    keys = prompt_kv[..., :head_dim]
    values = prompt_kv[..., head_dim:]
    block = prompt // 2
    pieces = []
    for block_index in range(2):
        row_start = block_index * block
        query_block = grouped[row_start : row_start + block]
        scores = jnp.einsum(
            "qhgd,khd->hgqk", query_block, keys, preferred_element_type=jnp.float32
        ) * head_dim ** (-0.5)
        query_index = row_start + jnp.arange(block, dtype=jnp.int32)
        key_index = jnp.arange(prompt, dtype=jnp.int32)
        allowed = (key_index[None, :] <= query_index[:, None]) & (key_index[None, :] < length)
        scores = jnp.where(allowed, scores, jnp.float32(-1e30))
        highest = jnp.max(scores, axis=-1, keepdims=True)
        expo = jnp.exp(scores - highest)
        weights = (expo / jnp.sum(expo, axis=-1, keepdims=True)).astype(jnp.bfloat16)
        result = jnp.einsum("hgqk,khd->qhgd", weights, values, preferred_element_type=jnp.float32)
        result = jnp.where(query_index[:, None, None, None] < length, result, jnp.float32(0.0))
        pieces.append(result.reshape(block, local_query_heads, head_dim).astype(jnp.bfloat16))
    return jnp.concatenate(pieces, axis=0)[None]


def solution(mesh):
    in_specs = (
        P("req", None, "tp", None),
        P("req", None, "tp", None),
        P("req", "tp"),
        P("req"),
        P("req"),
        P("req"),
        P("tp", None, None),
    )
    out_specs = P("req", None, "tp", None)
    return jax.shard_map(
        per_device, mesh=mesh, in_specs=in_specs, out_specs=out_specs, check_vma=False
    )
```

profile of v0, /device:TPU:1, one launch (start us, length us, event | category | flops | bytes accessed | tf_op | source)
XLA Modules:
  0.0 232.7 jit_solution(3321122596609330127)
XLA Ops:
  6.5 0.8 fusion.42
  7.4 1.2 reduce-window.6
  8.9 0.8 fusion.41
  10.4 6.0 %scatter_custom_fusion.1 = bf16[1024,1536]{1,0:T(8,128)(2,1)} fusion(s32[512]{0:T(512)S(1)} %compare_select_fusion.1, bf16[512,1536]{1,0:T(8,128)(2,1)} %param.9, bf16[]{:T(256)} %constant.4.clone.1), kind=kCustom, calls=%fused_computation.27 | custom fusion | bytes 3146240 | tf_op jit(solution)/shard_map/scatter | solution.py:44
  16.3 86.7 %all_to_all.14 = bf16[64,16,1536]{2,1,0:T(8,128)(2,1)S(1)} all-to-all(bf16[64,16,1536]{2,1,0:T(8,128)(2,1)} %bitcast.115), channel_id=1, replica_groups=mesh['req'=64,'tp'=4] {'req'}, dimensions={0} | all-to-all | bytes 6291456 | tf_op jit(solution)/shard_map/all_to_all | solution.py:48
  103.0 5.0 %fusion.10 = f32[4,1024,256]{1,2,0:T(8,128)} fusion(bf16[1024,1536,1]{1,0,2:T(8,128)(2,1)S(1)} %bitcast.116, bf16[1536,4,256]{2,1,0:T(4,128)(2,1)S(1)} %copy-done), kind=kOutput, calls=%fused_computation.21 | convolution fusion | flops 3221225472 | bytes 10485760 | tf_op jit(solution)/shard_map/rd,dhc->hrc/dot_general | solution.py:54
  108.0 2.7 %scatter_custom_fusion = s32[1024]{0:T(1024)S(1)} fusion(s32[512]{0:T(512)S(1)} %compare_select_fusion.1, s32[512]{0:T(512)} %param.11, s32[]{:T(128)} %constant.11.clone.1), kind=kCustom, calls=%fused_computation.64 | custom fusion | bytes 4608 | tf_op jit(solution)/shard_map/scatter | solution.py:40
  111.4 6.2 %all-to-all-start = ((s32[64,1,16]{2,1,0:T(1,128)}), s32[64,1,16]{2,1,0:T(1,128)S(1)}, u32[]{:S(2)}, u32[]{:S(2)}) async-start(s32[64,1,16]{2,1,0:T(1,128)} %bitcast.4), calls=%async_computation | async-start | bytes 65536 | tf_op jit(solution)/shard_map/all_to_all | solution.py:49
  118.3 1.6 fusion.6
  120.0 6.9 %all-to-all-done = s32[64,1,16]{2,1,0:T(1,128)S(1)} async-done(((s32[64,1,16]{2,1,0:T(1,128)}), s32[64,1,16]{2,1,0:T(1,128)S(1)}, u32[]{:S(2)}, u32[]{:S(2)}) %all-to-all-start) | async-done | bytes 4128 | tf_op jit(solution)/shard_map/all_to_all | solution.py:49
  128.4 26.0 %reduce-scatter.2.cloned.1.call-done = f32[1,1024,256]{1,2,0:T(8,128)} async-done(((f32[4,1024,256]{1,2,0:T(8,128)}), f32[1,1024,256]{1,2,0:T(8,128)}) %reduce-scatter.2.cloned.1.call-update) | async-done | bytes 1048592 | tf_op jit(solution)/shard_map/reduce_scatter | solution.py:53
  154.4 1.1 slice.65
  155.5 2.1 fusion.36
  157.6 0.8 maximum_bitcast_fusion.1
  158.4 1.2 copy.42
  159.7 5.5 %scatter_fusion = bf16[1280,256]{1,0:T(8,128)(2,1)S(1)} fusion(bf16[1280,256]{1,0:T(8,128)(2,1)S(1)} %bitcast.114, s32[1024]{0:T(1024)S(1)} %bitcast.120, bf16[1024,256]{1,0:T(8,128)(2,1)S(1)} %copy.42), kind=kCustom, calls=%fused_computation.2 | custom fusion | bytes 1576960 | tf_op jit(solution)/shard_map/scatter | solution.py:60
  165.2 10.0 %fusion.45 = (f32[6,640]{1,0:T(8,128)S(1)}, f32[1,6,640,1280]{2,3,1,0:T(8,128)}) fusion(bf16[1,1280,6,128]{3,1,2,0:T(8,128)(2,1)} %param.7, bf16[1280,1,256]{2,0,1:T(8,128)(2,1)S(1)} %bitcast.110, pred[640,1280]{0,1:T(8,128)(4,1)S(1)} %get-tuple-element.8), kind=kOutput, calls=%fused_computation.68 | convolution fusion | flops 1273032960 | bytes 21806080 | tf_op jit(solution)/shard_map/qhgd,khd->hgqk/dot_general | solution.py:72
  175.1 8.5 %fusion.46 = (f32[6,640]{1,0:T(8,128)S(1)}, f32[1,6,640,1280]{2,3,1,0:T(8,128)}) fusion(bf16[1,1280,6,128]{3,1,2,0:T(8,128)(2,1)S(1)} %copy-done.4, bf16[1280,1,256]{2,0,1:T(8,128)(2,1)S(1)} %bitcast.111, pred[640,1280]{0,1:T(8,128)(4,1)S(1)} %get-tuple-element.7), kind=kOutput, calls=%fused_computation.69 | convolution fusion | flops 1273032960 | bytes 21806080 | tf_op jit(solution)/shard_map/qhgd,khd->hgqk/dot_general | solution.py:72
  183.6 9.2 %fusion.1 = f32[6,640]{1,0:T(8,128)S(1)} fusion(f32[1,6,640,1280]{2,3,1,0:T(8,128)} %get-tuple-element.10, f32[6,640]{1,0:T(8,128)S(1)} %get-tuple-element.9), kind=kLoop, calls=%fused_computation.10 | loop fusion | flops 9826560 | bytes 19691520 | tf_op jit(solution)/shard_map/reduce_sum | solution.py:81
  192.8 9.7 %fusion.24 = bf16[640,6,128]{0,2,1:T(8,128)(2,1)} fusion(f32[6,640]{1,0:T(8,128)S(1)} %fusion.1, f32[1,6,640,1280]{2,3,1,0:T(8,128)} %get-tuple-element.10, f32[6,640]{1,0:T(8,128)S(1)} %get-tuple-element.9, pred[640]{0:T(1024)(128)(4,1)S(1)} %get-tuple-element.14, bf16[1280,1,256]{2,0,1:T(8,128)(2,1)S(1)} %bitcast.112), kind=kOutput, calls=%fused_computation.30 | convolution fusion | flops 1274019840 | bytes 21013504 | tf_op jit(solution)/shard_map/hgqk,khd->qhgd/dot_general | solution.py:82
  202.5 9.2 %fusion = f32[6,640]{1,0:T(8,128)S(1)} fusion(f32[1,6,640,1280]{2,3,1,0:T(8,128)} %get-tuple-element.12, f32[6,640]{1,0:T(8,128)S(1)} %get-tuple-element.11), kind=kLoop, calls=%fused_computation.9 | loop fusion | flops 9826560 | bytes 19691520 | tf_op jit(solution)/shard_map/reduce_sum | solution.py:81
  211.6 8.9 %fusion.21 = bf16[640,6,128]{0,2,1:T(8,128)(2,1)S(1)} fusion(f32[6,640]{1,0:T(8,128)S(1)} %fusion, f32[1,6,640,1280]{2,3,1,0:T(8,128)} %get-tuple-element.12, f32[6,640]{1,0:T(8,128)S(1)} %get-tuple-element.11, pred[640]{0:T(1024)(128)(4,1)S(1)} %get-tuple-element.13, bf16[1280,1,256]{2,0,1:T(8,128)(2,1)} %bitcast.113), kind=kOutput, calls=%fused_computation.29 | convolution fusion | flops 1274019840 | bytes 21002880 | tf_op jit(solution)/shard_map/hgqk,khd->qhgd/dot_general | solution.py:82
  220.5 1.4 maximum_bitcast_fusion
  221.9 3.9 %copy.47 = bf16[1,1280,6,128]{3,1,2,0:T(8,128)(2,1)} copy(bf16[1,1280,6,128]{1,3,2,0:T(8,128)(2,1)} %maximum_bitcast_fusion) | data formatting | bytes 3932160 | tf_op jit(solution)/shard_map/broadcast_in_dim | solution.py:85
  (29 shorter events, 3.2 us)
Async XLA Ops:
  6.5 96.4 %copy-start = (bf16[1536,4,256]{2,1,0:T(4,128)(2,1)S(1)}, bf16[1536,4,256]{2,1,0:T(4,128)(2,1)}, u32[]{:S(2)}) copy-start(bf16[1536,4,256]{2,1,0:T(4,128)(2,1)} %param.13) | copy-start | bytes 9437188
  6.5 147.9 %reduce-scatter.2.cloned.1.call-start = ((), (), s32[]{:S(2)}) async-start(), calls=%async_computation.3 | async-start | bytes 5242880 | tf_op jit(solution)/shard_map/reduce_scatter | solution.py:53
  108.0 51.7 %copy-start.3 = (bf16[1,1280,1,256]{3,1,2,0:T(8,128)(2,1)S(1)}, bf16[1,1280,1,256]{3,1,2,0:T(8,128)(2,1)}, u32[]{:S(2)}) copy-start(bf16[1,1280,1,256]{3,1,2,0:T(8,128)(2,1)} %param.8) | copy-start | bytes 1966084
  111.4 15.4 %all-to-all-start = ((s32[64,1,16]{2,1,0:T(1,128)}), s32[64,1,16]{2,1,0:T(1,128)S(1)}, u32[]{:S(2)}, u32[]{:S(2)}) async-start(s32[64,1,16]{2,1,0:T(1,128)} %bitcast.4), calls=%async_computation | async-start | bytes 65536 | tf_op jit(solution)/shard_map/all_to_all | solution.py:49
  165.2 27.6 %copy-start.2 = (bf16[1280,256]{1,0:T(8,128)(2,1)}, bf16[1280,256]{1,0:T(8,128)(2,1)S(1)}, u32[]{:S(2)}) copy-start(bf16[1280,256]{1,0:T(8,128)(2,1)S(1)} %scatter_fusion) | copy-start | bytes 1966084
  165.2 10.0 %copy-start.4 = (bf16[1,1280,6,128]{3,1,2,0:T(8,128)(2,1)S(1)}, bf16[1,1280,6,128]{3,1,2,0:T(8,128)(2,1)}, u32[]{:S(2)}) copy-start(bf16[1,1280,6,128]{3,1,2,0:T(8,128)(2,1)} %param.7) | copy-start | bytes 5898244
  211.6 8.9 %copy-start.5 = (bf16[640,6,128]{0,2,1:T(8,128)(2,1)S(1)}, bf16[640,6,128]{0,2,1:T(8,128)(2,1)}, u32[]{:S(2)}) copy-start(bf16[640,6,128]{0,2,1:T(8,128)(2,1)} %fusion.24) | copy-start | bytes 2949124
  211.6 14.3 %copy-start.1 = (bf16[1536,4,256]{2,1,0:T(4,128)(2,1)S(1)}, bf16[1536,4,256]{2,1,0:T(4,128)(2,1)}, u32[]{:S(2)}) copy-start(bf16[1536,4,256]{2,1,0:T(4,128)(2,1)} %param.13) | copy-start | bytes 9437188
Sparse Core Ops, SparseCore 0:
  108.1 46.2 reduce-scatter.1
where the time goes:
time: 233 us
  blocking collectives  86.7 us (37%)
  matrix products  41.9 us (18%)
  waiting for transfers between devices  32.9 us (14%)
  other arithmetic  28.8 us (12%)
  local copies, waits for them, and re-layouts  22 us (9%)
  between operations  14.2 us (6%)
  starting transfers between devices  6.2 us (3%)
    all_to_all x1, blocking collectives, per_device(): lax.all_to_all(row_buffer, 'req', split_axis=0, concat_axis=0, tiled=True)  86.7 us
    reduce_scatter x1, waiting for transfers between devices, per_device(): lax.psum_scatter(jnp.einsum('rd,dhc->hrc', flat_rows, kv_weight, preferre...  26 us
    dot_general x2, matrix products, per_device(): jnp.einsum('hgqk,khd->qhgd', weights, values, preferred_element_type=jnp....  18.5 us
    dot_general x2, matrix products, per_device(): jnp.einsum('qhgd,khd->hgqk', query_block, keys, preferred_element_type=jn...  18.4 us
    reduce_sum x2, other arithmetic, per_device(): jnp.sum(expo, axis=-1, keepdims=True)  18.3 us
    all_to_all x1, waiting for transfers between devices, per_device(): lax.all_to_all(pos_buffer, 'req', split_axis=0, concat_axis=0, tiled=True)  6.88 us
    all_to_all x1, starting transfers between devices, per_device(): lax.all_to_all(pos_buffer, 'req', split_axis=0, concat_axis=0, tiled=True)  6.2 us
    scatter x1, local copies, waits for them, and re-layouts, per_device(): jnp.zeros((groups * capacity, image_rows.shape[1]), jnp.bfloat16).at[target]  5.96 us
  transfers between devices with their start and end apart: 2, of which 2 were waited for; matrix products, arithmetic and copies ran while one was open for 3% of the time, Pallas kernels for 0%

commit v1 on v0

v1 whole, which is shorter than its diff:
```python
import functools
import math

import jax
import jax.numpy as jnp
from jax import lax
from jax.experimental import pallas as pl
from jax.experimental.pallas import tpu as pltpu
from jax.sharding import PartitionSpec as P


def rotate_keys(summed, positions, head_dim):
    half = head_dim // 2
    freqs = jnp.exp(jnp.arange(half, dtype=jnp.float32) * (-2.0 * math.log(1000000.0) / head_dim))
    angles = positions.astype(jnp.float32)[:, None] * freqs[None, :]
    cosine = jnp.cos(angles)
    sine = jnp.sin(angles)
    first = summed[..., :half]
    second = summed[..., half:head_dim]
    rotated = jnp.concatenate(
        [first * cosine - second * sine, second * cosine + first * sine, summed[..., head_dim:]],
        axis=-1,
    )
    return rotated.astype(jnp.bfloat16)


def attention_kernel(block, head_dim, len_ref, q_ref, kv_ref, o_ref):
    prompt = q_ref.shape[1]
    length = len_ref[0]
    scale = head_dim ** (-0.5)
    for index in range(prompt // block):
        row_start = index * block
        keys_used = row_start + block
        query = q_ref[0, row_start:keys_used, :]
        keys = kv_ref[0:keys_used, 0:head_dim]
        scores = lax.dot_general(
            query, keys, (((1,), (1,)), ((), ())), preferred_element_type=jnp.float32
        ) * scale
        query_index = row_start + lax.broadcasted_iota(jnp.int32, (block, 1), 0)
        limit = jnp.minimum(query_index, length - 1)
        key_index = lax.broadcasted_iota(jnp.int32, (1, keys_used), 1)
        scores = jnp.where(key_index <= limit, scores, jnp.float32(-1e30))
        highest = jnp.max(scores, axis=-1, keepdims=True)
        expo = jnp.exp(scores - highest)
        total = jnp.sum(expo, axis=-1, keepdims=True)
        weights = (expo * (1.0 / total)).astype(jnp.bfloat16)
        values = kv_ref[0:keys_used, head_dim:]
        result = jnp.dot(weights, values, preferred_element_type=jnp.float32)
        result = jnp.where(query_index < length, result, jnp.float32(0.0))
        o_ref[0, row_start:keys_used, :] = result.astype(o_ref.dtype)


def attend(heads_first, prompt_kv, length, head_dim, block=256):
    heads, prompt, _ = heads_first.shape
    grid_spec = pltpu.PrefetchScalarGridSpec(
        num_scalar_prefetch=1,
        grid=(heads,),
        in_specs=[
            pl.BlockSpec((1, prompt, head_dim), lambda h, lens: (h, 0, 0)),
            pl.BlockSpec((prompt, 2 * head_dim), lambda h, lens: (0, 0)),
        ],
        out_specs=pl.BlockSpec((1, prompt, head_dim), lambda h, lens: (h, 0, 0)),
    )
    return pl.pallas_call(
        functools.partial(attention_kernel, block, head_dim),
        grid_spec=grid_spec,
        out_shape=jax.ShapeDtypeStruct((heads, prompt, head_dim), jnp.bfloat16),
        compiler_params=pltpu.CompilerParams(dimension_semantics=("arbitrary",)),
    )(length, heads_first, prompt_kv)


def per_device(queries, text_kv, image_rows, row_request, row_position, prompt_lengths, kv_weight):
    groups = lax.axis_size("req")
    own_rows = image_rows.shape[0]
    capacity = 2 * own_rows // groups
    prompt = queries.shape[1]
    head_dim = queries.shape[3]
    partial = jnp.einsum("rd,dhc->hrc", image_rows, kv_weight, preferred_element_type=jnp.float32)
    summed = lax.psum_scatter(partial, "tp", scatter_dimension=0, tiled=True)[0]
    image_kv = rotate_keys(summed, row_position, head_dim)
    one_hot = (row_request[:, None] == jnp.arange(groups, dtype=jnp.int32)[None, :]).astype(
        jnp.int32
    )
    before = jnp.cumsum(one_hot, axis=0) - one_hot
    slot_index = jnp.sum(before * one_hot, axis=1)
    target = row_request * capacity + slot_index
    pos_buffer = (
        jnp.full((groups * capacity,), prompt, jnp.int32)
        .at[target]
        .set(row_position)
        .reshape(groups, capacity)
    )
    kv_buffer = (
        jnp.zeros((groups * capacity, image_kv.shape[1]), jnp.bfloat16)
        .at[target]
        .set(image_kv)
        .reshape(groups, capacity, image_kv.shape[1])
    )
    got_kv = lax.all_to_all(kv_buffer, "req", split_axis=0, concat_axis=0, tiled=True)
    got_pos = lax.all_to_all(pos_buffer, "req", split_axis=0, concat_axis=0, tiled=True)
    places = got_pos.reshape(groups * capacity)
    flat_kv = got_kv.reshape(groups * capacity, image_kv.shape[1])
    prompt_kv = text_kv[0, :, 0, :].at[places].set(flat_kv, mode="drop")
    heads_first = jnp.transpose(queries[0], (1, 0, 2))
    out = attend(heads_first, prompt_kv, prompt_lengths, head_dim)
    return jnp.transpose(out, (1, 0, 2))[None]


def solution(mesh):
    in_specs = (
        P("req", None, "tp", None),
        P("req", None, "tp", None),
        P("req", "tp"),
        P("req"),
        P("req"),
        P("req"),
        P("tp", None, None),
    )
    out_specs = P("req", None, "tp", None)
    return jax.shard_map(
        per_device, mesh=mesh, in_specs=in_specs, out_specs=out_specs, check_vma=False
    )
```

time: 233 us -> 118 us (0.51)
  blocking collectives: 86.7 us -> 0 us
  matrix products: 41.9 us -> 5.08 us
  other arithmetic: 28.8 us -> 3.73 us
  Pallas kernels: 0 us -> 21 us
  starting transfers between devices: 6.2 us -> 23.8 us
  local copies, waits for them, and re-layouts: 22 us -> 16.8 us
    all_to_all x1 -> x0, blocking collectives: 86.7 us -> none  [per_device(): lax.all_to_all(row_buffer, 'req', split_axis=0, concat_axis=0, tiled=True)]
    dot_general x5 -> x1, matrix products: 41.9 us -> 5.08 us  [per_device(): jnp.einsum('rd,dhc->hrc', image_rows, kv_weight, preferred_element_type=j...]
    pallas_call x0 -> x1, Pallas kernels: none -> 21 us  [attend(): pl.pallas_call(functools.partial(attention_kernel, block, head_dim), grid...]
    reduce_sum x2 -> x0, other arithmetic: 18.3 us -> none  [per_device(): jnp.sum(expo, axis=-1, keepdims=True)]
    all_to_all x0 -> x1, waiting for transfers between devices: none -> 15.2 us  [per_device(): lax.all_to_all(kv_buffer, 'req', split_axis=0, concat_axis=0, tiled=True)]
    all_to_all x0 -> x1, starting transfers between devices: none -> 10.6 us  [per_device(): lax.all_to_all(kv_buffer, 'req', split_axis=0, concat_axis=0, tiled=True)]
    reduce_scatter x1, waiting for transfers between devices: 26 us -> 17.6 us  [per_device(): summed = lax.psum_scatter(partial, 'tp', scatter_dimension=0, tiled=True)[0]]
    all_to_all x1, starting transfers between devices: 6.2 us -> 13.2 us  [per_device(): lax.all_to_all(pos_buffer, 'req', split_axis=0, concat_axis=0, tiled=True)]
  transfers between devices with their start and end apart: 2 -> 3, of which waited for: 2 -> 2; matrix products, arithmetic and copies ran while one was open for 3% -> 10% of each run, Pallas kernels for 0% -> 0%
where the time goes in v1:
time: 118 us; the launch traced here: 117 us
  waiting for transfers between devices  32.8 us (28%)
  starting transfers between devices  23.8 us (20%)
  Pallas kernels  21 us (18%)
  local copies, waits for them, and re-layouts  16.8 us (14%)
  between operations  14.2 us (12%)
  matrix products  5.08 us (4%)
  other arithmetic  3.73 us (3%)
    pallas_call x1, Pallas kernels, attend(): pl.pallas_call(functools.partial(attention_kernel, block, head_dim), grid...  21 us
    reduce_scatter x1, waiting for transfers between devices, per_device(): summed = lax.psum_scatter(partial, 'tp', scatter_dimension=0, tiled=True)[0]  17.6 us
    all_to_all x1, waiting for transfers between devices, per_device(): lax.all_to_all(kv_buffer, 'req', split_axis=0, concat_axis=0, tiled=True)  15.2 us
    all_to_all x1, starting transfers between devices, per_device(): lax.all_to_all(pos_buffer, 'req', split_axis=0, concat_axis=0, tiled=True)  13.2 us
    all_to_all x1, starting transfers between devices, per_device(): lax.all_to_all(kv_buffer, 'req', split_axis=0, concat_axis=0, tiled=True)  10.6 us
    scatter x1, local copies, waits for them, and re-layouts, per_device(): prompt_kv = text_kv[0, :, 0, :].at[places].set(flat_kv, mode='drop')  5.44 us
    dot_general x1, matrix products, per_device(): jnp.einsum('rd,dhc->hrc', image_rows, kv_weight, preferred_element_type=j...  5.08 us
    scatter x1, local copies, waits for them, and re-layouts, per_device(): kv_buffer = jnp.zeros((groups * capacity, image_kv.shape[1]), jnp.bfloat1...  3.14 us
  transfers between devices with their start and end apart: 3, of which 2 were waited for; matrix products, arithmetic and copies ran while one was open for 10% of the time, Pallas kernels for 0%

profile of v1, /device:TPU:1, one launch (start us, length us, event | category | flops | bytes accessed | tf_op | source)
XLA Modules:
  0.0 117.3 jit_solution(6873571908841710017)
XLA Ops:
  6.5 1.2 %copy.25 = bf16[1,1280,1,256]{3,1,2,0:T(8,128)(2,1)S(1)} copy(bf16[1,1280,1,256]{3,1,2,0:T(8,128)(2,1)} %param.8) | data formatting | bytes 1310720
  7.7 0.4 copy-done
  8.1 5.1 %fusion.2 = f32[4,512,256]{1,2,0:T(8,128)} fusion(bf16[1536,4,256]{2,1,0:T(4,128)(2,1)} %param.13, bf16[512,1536]{1,0:T(8,128)(2,1)S(1)} %copy-done), kind=kOutput, calls=%fused_computation.5 | convolution fusion | flops 1610612736 | bytes 6815744 | tf_op jit(solution)/shard_map/rd,dhc->hrc/dot_general | solution.py:78
  13.2 0.0 reduce-scatter.2.cloned.1.call-update
  13.2 0.7 copy-done.2
  13.9 1.2 %reduce-window.6 = s32[64,4,128]{2,0,1:T(8,128)S(1)} reduce-window(s32[64,4,128]{2,0,1:T(8,128)S(1)} %fusion.19, s32[]{:T(128)} %constant.8.clone.1), window={size=1x1x128 pad=0_0x0_0x127_0}, to_apply=%region_0.0 | reduce-window | flops 4161536 | bytes 262148 | tf_op jit(solution)/shard_map/reduce-window
  15.1 0.2 slice_reduce_fusion
  15.4 0.1 fusion.18
  15.5 2.4 %scatter_custom_fusion = s32[1024]{0:T(1024)S(1)} fusion(s32[512]{0:T(512)S(1)} %compare_select_fusion.1, s32[512]{0:T(512)S(1)} %copy-done.3, s32[]{:T(128)} %constant.6.clone.1), kind=kCustom, calls=%fused_computation.32 | custom fusion | bytes 4100 | tf_op jit(solution)/shard_map/scatter | solution.py:90
  18.0 0.7 all_to_all.9
  18.7 13.2 %all-to-all-start = ((s32[64,1,16]{2,1,0:T(1,128)}), s32[64,1,16]{2,1,0:T(1,128)S(1)}, u32[]{:S(2)}, u32[]{:S(2)}) async-start(s32[64,1,16]{2,1,0:T(1,128)} %bitcast.5), calls=%async_computation | async-start | bytes 65536 | tf_op jit(solution)/shard_map/all_to_all | solution.py:100
  31.9 17.6 %reduce-scatter.2.cloned.1.call-done = f32[1,512,256]{1,2,0:T(8,128)} async-done(((f32[4,512,256]{1,2,0:T(8,128)}), f32[1,512,256]{1,2,0:T(8,128)}) %reduce-scatter.2.cloned.1.call-update) | async-done | bytes 524304 | tf_op jit(solution)/shard_map/reduce_scatter | solution.py:79
  49.4 1.0 slice.31
  50.4 1.5 %fusion.13 = (bf16[512,64]{0,1:T(8,128)(2,1)S(1)}, bf16[512,64]{0,1:T(8,128)(2,1)S(1)}) fusion(f32[512,256]{0,1:T(8,128)} %bitcast.41, f32[64]{0:T(128)S(1)} %multiply_exponential_fusion, f32[512]{0:T(512)S(1)} %convert_element_type.13), kind=kLoop, calls=%fused_computation.18 | loop fusion | flops 294912 | bytes 395520 | tf_op jit(solution)/shard_map/convert
  52.0 0.1 copy.15
  52.1 3.1 %scatter_custom_fusion.1 = bf16[1024,256]{1,0:T(8,128)(2,1)} fusion(s32[512]{0:T(512)S(1)} %compare_select_fusion.1, bf16[512,256]{1,0:T(8,128)(2,1)S(1)} %copy.15, bf16[]{:T(256)} %constant.4.clone.1), kind=kCustom, calls=%fused_computation.9 | custom fusion | bytes 524290 | tf_op jit(solution)/shard_map/scatter | solution.py:96
  55.3 10.6 %all-to-all-start.1 = ((bf16[64,16,256]{2,1,0:T(8,128)(2,1)}), bf16[64,16,256]{2,1,0:T(8,128)(2,1)S(1)}, u32[]{:S(2)}, u32[]{:S(2)}) async-start(bf16[64,16,256]{2,1,0:T(8,128)(2,1)} %bitcast.10), calls=%async_computation.2 | async-start | bytes 1048576 | tf_op jit(solution)/shard_map/all_to_all | solution.py:99
  66.6 0.6 broadcast.62
  67.1 0.8 reduce.5
  67.9 0.1 reshape.65
  68.0 15.2 %all-to-all-done.1 = bf16[64,16,256]{2,1,0:T(8,128)(2,1)S(1)} async-done(((bf16[64,16,256]{2,1,0:T(8,128)(2,1)}), bf16[64,16,256]{2,1,0:T(8,128)(2,1)S(1)}, u32[]{:S(2)}, u32[]{:S(2)}) %all-to-all-start.1) | async-done | bytes 524320 | tf_op jit(solution)/shard_map/all_to_all | solution.py:99
  83.2 5.4 %scatter_fusion = bf16[1280,256]{1,0:T(8,128)(2,1)S(1)} fusion(bf16[1280,256]{1,0:T(8,128)(2,1)S(1)} %bitcast.37, s32[1024]{0:T(1024)S(1)} %bitcast.43, bf16[1024,256]{1,0:T(8,128)(2,1)S(1)} %bitcast.38), kind=kCustom, calls=%fused_computation.2 | custom fusion | bytes 1576960 | tf_op jit(solution)/shard_map/scatter | solution.py:103
  88.7 0.8 copy-done.1
  89.5 21.0 %shard_map.73 = bf16[6,1280,128]{2,1,0:T(8,128)(2,1)} custom-call(s32[1]{0:T(128)S(6)} %copy.24.len_ref, bf16[6,1280,128]{2,1,0:T(8,128)(2,1)} %bitcast.39, bf16[1280,256]{1,0:T(8,128)(2,1)} %copy-done.1), custom_call_target="tpu_custom_call" | custom-call | tf_op jit(solution)/shard_map/pallas_call | solution.py:64
  (15 shorter events, 0.1 us)
Async XLA Ops:
  6.5 1.6 %copy-start = (bf16[512,1536]{1,0:T(8,128)(2,1)S(1)}, bf16[512,1536]{1,0:T(8,128)(2,1)}, u32[]{:S(2)}) copy-start(bf16[512,1536]{1,0:T(8,128)(2,1)} %param.9) | copy-start | bytes 4718596
  6.5 42.9 %reduce-scatter.2.cloned.1.call-start = ((), (), s32[]{:S(2)}) async-start(), calls=%async_computation.3 | async-start | bytes 2621440 | tf_op jit(solution)/shard_map/reduce_scatter | solution.py:79
  13.2 0.7 copy-start.2
  13.2 2.3 %copy-start.3 = (s32[512]{0:T(512)S(1)}, s32[512]{0:T(512)}, u32[]{:S(2)}) copy-start(s32[512]{0:T(512)} %param.11) | copy-start | bytes 6148
  18.7 36.6 %all-to-all-start = ((s32[64,1,16]{2,1,0:T(1,128)}), s32[64,1,16]{2,1,0:T(1,128)S(1)}, u32[]{:S(2)}, u32[]{:S(2)}) async-start(s32[64,1,16]{2,1,0:T(1,128)} %bitcast.5), calls=%async_computation | async-start | bytes 65536 | tf_op jit(solution)/shard_map/all_to_all | solution.py:100
  55.3 28.0 %all-to-all-start.1 = ((bf16[64,16,256]{2,1,0:T(8,128)(2,1)}), bf16[64,16,256]{2,1,0:T(8,128)(2,1)S(1)}, u32[]{:S(2)}, u32[]{:S(2)}) async-start(bf16[64,16,256]{2,1,0:T(8,128)(2,1)} %bitcast.10), calls=%async_computation.2 | async-start | bytes 1048576 | tf_op jit(solution)/shard_map/all_to_all | solution.py:99
  88.7 0.8 copy-start.1
Sparse Core Ops, SparseCore 0:
  13.4 36.0 reduce-scatter.1

commit v2 on v1

--- a/solution.py
+++ b/solution.py
@@ -75,8 +75,11 @@
     capacity = 2 * own_rows // groups
     prompt = queries.shape[1]
     head_dim = queries.shape[3]
+    width = 2 * head_dim
     partial = jnp.einsum("rd,dhc->hrc", image_rows, kv_weight, preferred_element_type=jnp.float32)
-    summed = lax.psum_scatter(partial, "tp", scatter_dimension=0, tiled=True)[0]
+    summed = lax.psum_scatter(
+        partial.astype(jnp.bfloat16), "tp", scatter_dimension=0, tiled=True
+    )[0].astype(jnp.float32)
     image_kv = rotate_keys(summed, row_position, head_dim)
     one_hot = (row_request[:, None] == jnp.arange(groups, dtype=jnp.int32)[None, :]).astype(
         jnp.int32
@@ -84,23 +87,26 @@
     before = jnp.cumsum(one_hot, axis=0) - one_hot
     slot_index = jnp.sum(before * one_hot, axis=1)
     target = row_request * capacity + slot_index
-    pos_buffer = (
-        jnp.full((groups * capacity,), prompt, jnp.int32)
-        .at[target]
-        .set(row_position)
-        .reshape(groups, capacity)
-    )
-    kv_buffer = (
-        jnp.zeros((groups * capacity, image_kv.shape[1]), jnp.bfloat16)
-        .at[target]
-        .set(image_kv)
-        .reshape(groups, capacity, image_kv.shape[1])
-    )
-    got_kv = lax.all_to_all(kv_buffer, "req", split_axis=0, concat_axis=0, tiled=True)
-    got_pos = lax.all_to_all(pos_buffer, "req", split_axis=0, concat_axis=0, tiled=True)
-    places = got_pos.reshape(groups * capacity)
-    flat_kv = got_kv.reshape(groups * capacity, image_kv.shape[1])
-    prompt_kv = text_kv[0, :, 0, :].at[places].set(flat_kv, mode="drop")
+    slots = groups * capacity
+    pick = (target[None, :] == jnp.arange(slots, dtype=jnp.int32)[:, None]).astype(jnp.bfloat16)
+    send_kv = jnp.dot(pick, image_kv, preferred_element_type=jnp.float32).astype(jnp.bfloat16)
+    pos_f = row_position.astype(jnp.float32)
+    digits = jnp.stack([jnp.floor(pos_f / 16.0), pos_f - 16.0 * jnp.floor(pos_f / 16.0)], axis=1)
+    send_pos = jnp.dot(pick.astype(jnp.float32), digits, precision=lax.Precision.HIGHEST)
+    filled = jnp.sum(pick.astype(jnp.float32), axis=1, keepdims=True)
+    send_pos = jnp.where(filled > 0, send_pos, jnp.float32(prompt / 16.0) * jnp.array([1.0, 0.0]))
+    tail = send_pos.reshape(groups, 2 * capacity).astype(jnp.bfloat16)
+    tail = jnp.pad(tail, ((0, 0), (0, 128 - 2 * capacity)))
+    packet = jnp.concatenate([send_kv.reshape(groups, capacity * width), tail], axis=1)
+    got = lax.all_to_all(packet, "req", split_axis=0, concat_axis=0, tiled=True)
+    got_kv = got[:, : capacity * width].reshape(slots, width)
+    got_digits = got[:, capacity * width : capacity * width + 2 * capacity].astype(jnp.int32)
+    got_digits = got_digits.reshape(slots, 2)
+    places = got_digits[:, 0] * 16 + got_digits[:, 1]
+    place = (places[None, :] == jnp.arange(prompt, dtype=jnp.int32)[:, None]).astype(jnp.bfloat16)
+    placed = jnp.dot(place, got_kv, preferred_element_type=jnp.float32).astype(jnp.bfloat16)
+    hit = jnp.any(places[None, :] == jnp.arange(prompt, dtype=jnp.int32)[:, None], axis=1)
+    prompt_kv = jnp.where(hit[:, None], placed, text_kv[0, :, 0, :])
     heads_first = jnp.transpose(queries[0], (1, 0, 2))
     out = attend(heads_first, prompt_kv, prompt_lengths, head_dim)
     return jnp.transpose(out, (1, 0, 2))[None]

time: 118 us -> 110 us (0.932)
  starting transfers between devices: 23.8 us -> 12.1 us
  local copies, waits for them, and re-layouts: 16.8 us -> 6.2 us
  waiting for transfers between devices: 32.8 us -> 42.5 us
  matrix products: 5.08 us -> 8.14 us
  other arithmetic: 3.73 us -> 5.32 us
    all_to_all x2 -> x1, starting transfers between devices: 23.8 us -> 12.1 us  [per_device(): got = lax.all_to_all(packet, 'req', split_axis=0, concat_axis=0, tiled=True)]
    scatter x3 -> x0, local copies, waits for them, and re-layouts: 11 us -> none  [the longest x1 5.44 us: per_device(): prompt_kv = text_kv[0, :, 0, :].at[places].set(flat_kv, mode='drop')]
    reduce_scatter x1, waiting for transfers between devices: 17.6 us -> 25.1 us  [per_device(): lax.psum_scatter(partial.astype(jnp.bfloat16), 'tp', scatter_dimension=0,...]
    dot_general x0 -> x3, matrix products: none -> 3.45 us  [the longest x1 1.93 us: per_device(): jnp.dot(place, got_kv, preferred_element_type=jnp.float32)]
    all_to_all x2 -> x1, waiting for transfers between devices: 15.2 us -> 17.4 us  [per_device(): got = lax.all_to_all(packet, 'req', split_axis=0, concat_axis=0, tiled=True)]
    unnamed x9 -> x13, local copies, waits for them, and re-layouts: 3.09 us -> 3.26 us
  transfers between devices with their start and end apart: 3 -> 2, of which waited for: 2 -> 2; matrix products, arithmetic and copies ran while one was open for 10% -> 3% of each run, Pallas kernels for 0% -> 0%
where the time goes in v2:
time: 110 us
  waiting for transfers between devices  42.5 us (39%)
  Pallas kernels  21 us (19%)
  between operations  14.2 us (13%)
  starting transfers between devices  12.1 us (11%)
  matrix products  8.14 us (7%)
  local copies, waits for them, and re-layouts  6.2 us (6%)
  other arithmetic  5.32 us (5%)
    reduce_scatter x1, waiting for transfers between devices, per_device(): lax.psum_scatter(partial.astype(jnp.bfloat16), 'tp', scatter_dimension=0,...  25.1 us
    pallas_call x1, Pallas kernels, attend(): pl.pallas_call(functools.partial(attention_kernel, block, head_dim), grid...  21 us
    all_to_all x1, waiting for transfers between devices, per_device(): got = lax.all_to_all(packet, 'req', split_axis=0, concat_axis=0, tiled=True)  17.4 us
    all_to_all x1, starting transfers between devices, per_device(): got = lax.all_to_all(packet, 'req', split_axis=0, concat_axis=0, tiled=True)  12.1 us
    dot_general x1, matrix products, per_device(): jnp.einsum('rd,dhc->hrc', image_rows, kv_weight, preferred_element_type=j...  4.7 us
    unnamed x13, local copies, waits for them, and re-layouts  3.26 us
  transfers between devices with their start and end apart: 2, of which 2 were waited for; matrix products, arithmetic and copies ran while one was open for 3% of the time, Pallas kernels for 0%

profile of v2, /device:TPU:1, one launch (start us, length us, event | category | flops | bytes accessed | tf_op | source)
XLA Modules:
  0.0 109.5 jit_solution(17574523389595079396)
XLA Ops:
  6.6 1.4 %copy-done = bf16[512,1536]{1,0:T(8,128)(2,1)S(1)} copy-done((bf16[512,1536]{1,0:T(8,128)(2,1)S(1)}, bf16[512,1536]{1,0:T(8,128)(2,1)}, u32[]{:S(2)}) %copy-start) | copy-done | bytes 1572888
  8.0 4.7 %fusion.16 = bf16[4,512,256]{1,2,0:T(8,128)(2,1)} fusion(bf16[512,1536]{1,0:T(8,128)(2,1)S(1)} %copy-done, bf16[1536,4,256]{2,1,0:T(4,128)(2,1)} %param.14), kind=kOutput, calls=%fused_computation.15 | convolution fusion | flops 1611137024 | bytes 5767168 | tf_op jit(solution)/shard_map/rd,dhc->hrc/dot_general | solution.py:79
  12.7 1.2 %reduce-window.6 = s32[64,4,128]{2,0,1:T(8,128)S(1)} reduce-window(s32[64,4,128]{2,0,1:T(8,128)S(1)} %fusion.46, s32[]{:T(128)} %constant.6.clone.1), window={size=1x1x128 pad=0_0x0_0x127_0}, to_apply=%region_0.0 | reduce-window | flops 4161536 | bytes 262148 | tf_op jit(solution)/shard_map/reduce-window
  14.4 0.3 convert_reduce_fusion
  14.7 1.0 fusion.23
  15.9 0.2 convert_element_type.58
  16.2 25.1 %reduce-scatter.2.cloned.1.call-done = bf16[1,512,256]{1,2,0:T(8,128)(2,1)} async-done(((bf16[4,512,256]{1,2,0:T(8,128)(2,1)}), bf16[1,512,256]{1,2,0:T(8,128)(2,1)}) %reduce-scatter.2.cloned.1.call-update) | async-done | bytes 262160 | tf_op jit(solution)/shard_map/reduce_scatter | solution.py:80
  41.3 0.9 slice.40
  42.2 1.0 bitcast_convert_fusion
  43.2 0.6 fusion.40
  43.8 0.5 fusion.21
  44.3 0.2 reshape.60
  44.6 0.5 broadcast.62
  45.1 1.0 reduce.4
  46.1 1.2 %reshape.70 = bf16[64,2,2112]{2,1,0:T(2,128)(2,1)} reshape(bf16[64,4224]{1,0:T(8,128)(2,1)S(1)} %reduce.4) | data formatting | bytes 1081344
  47.3 12.1 %all-to-all-start = ((bf16[64,2,2112]{2,1,0:T(2,128)(2,1)}), bf16[64,2,2112]{2,1,0:T(2,128)(2,1)S(1)}, u32[]{:S(2)}, u32[]{:S(2)}) async-start(bf16[64,2,2112]{2,1,0:T(2,128)(2,1)} %reshape.70), calls=%async_computation.1 | async-start | bytes 1114112 | tf_op jit(solution)/shard_map/all_to_all | solution.py:101
  60.0 17.4 %all-to-all-done = bf16[64,2,2112]{2,1,0:T(2,128)(2,1)S(1)} async-done(((bf16[64,2,2112]{2,1,0:T(2,128)(2,1)}), bf16[64,2,2112]{2,1,0:T(2,128)(2,1)S(1)}, u32[]{:S(2)}, u32[]{:S(2)}) %all-to-all-start) | async-done | bytes 540704 | tf_op jit(solution)/shard_map/all_to_all | solution.py:101
  77.4 0.6 reshape.71
  78.2 0.2 reshape.63
  78.4 0.3 reshape.65
  78.7 0.4 fusion.29
  79.1 0.7 fusion.1
  79.8 1.9 %fusion.6.kv_ref = bf16[1280,256]{1,0:T(8,128)(2,1)} fusion(bf16[1024,256]{1,0:T(8,128)(2,1)S(1)} %reshape.63, s32[1024]{0:T(1024)S(1)} %fusion.29, bf16[1,1280,1,256]{3,1,2,0:T(8,128)(2,1)S(1)} %copy-done.3, pred[1280]{0:T(1024)(128)(4,1)S(1)} %fusion.1), kind=kOutput, calls=%fused_computation.7 | convolution fusion | flops 673054720 | bytes 1840384 | tf_op jit(solution)/shard_map/dot_general | solution.py:107
  81.7 21.0 %shard_map.82 = bf16[6,1280,128]{2,1,0:T(8,128)(2,1)} custom-call(s32[1]{0:T(128)S(6)} %copy.36.len_ref, bf16[6,1280,128]{2,1,0:T(8,128)(2,1)} %bitcast.49, bf16[1280,256]{1,0:T(8,128)(2,1)} %fusion.6.kv_ref), custom_call_target="tpu_custom_call" | custom-call | tf_op jit(solution)/shard_map/pallas_call | solution.py:64
  (26 shorter events, 0.9 us)
Async XLA Ops:
  6.5 1.4 %copy-start = (bf16[512,1536]{1,0:T(8,128)(2,1)S(1)}, bf16[512,1536]{1,0:T(8,128)(2,1)}, u32[]{:S(2)}) copy-start(bf16[512,1536]{1,0:T(8,128)(2,1)} %param.10) | copy-start | bytes 4718596
  6.5 8.2 %copy-start.4 = (bf16[2]{0:T(256)(128)(2,1)S(1)}, bf16[2]{0:T(256)(128)(2,1)}, u32[]{:S(2)}) copy-start(bf16[2]{0:T(256)(128)(2,1)} %constant.91) | copy-start | bytes 16
  6.5 6.2 %copy-start.2 = (s32[512]{0:T(512)S(1)}, s32[512]{0:T(512)}, u32[]{:S(2)}) copy-start(s32[512]{0:T(512)} %param.12) | copy-start | bytes 6148
  6.5 6.2 %copy-start.1 = (s32[512]{0:T(512)S(1)}, s32[512]{0:T(512)}, u32[]{:S(2)}) copy-start(s32[512]{0:T(512)} %param.11) | copy-start | bytes 6148
  6.5 34.8 %reduce-scatter.2.cloned.1.call-start = ((), (), s32[]{:S(2)}) async-start(), calls=%async_computation.2 | async-start | bytes 1310720 | tf_op jit(solution)/shard_map/reduce_scatter | solution.py:80
  47.3 30.1 %all-to-all-start = ((bf16[64,2,2112]{2,1,0:T(2,128)(2,1)}), bf16[64,2,2112]{2,1,0:T(2,128)(2,1)S(1)}, u32[]{:S(2)}, u32[]{:S(2)}) async-start(bf16[64,2,2112]{2,1,0:T(2,128)(2,1)} %reshape.70), calls=%async_computation.1 | async-start | bytes 1114112 | tf_op jit(solution)/shard_map/all_to_all | solution.py:101
  78.1 1.7 %copy-start.3 = (bf16[1,1280,1,256]{3,1,2,0:T(8,128)(2,1)S(1)}, bf16[1,1280,1,256]{3,1,2,0:T(8,128)(2,1)}, u32[]{:S(2)}) copy-start(bf16[1,1280,1,256]{3,1,2,0:T(8,128)(2,1)} %param.9) | copy-start | bytes 1966084
Sparse Core Ops, SparseCore 0:
  12.8 28.4 reduce-scatter.1

commit v3 on v2

--- a/solution.py
+++ b/solution.py
@@ -77,9 +77,7 @@
     head_dim = queries.shape[3]
     width = 2 * head_dim
     partial = jnp.einsum("rd,dhc->hrc", image_rows, kv_weight, preferred_element_type=jnp.float32)
-    summed = lax.psum_scatter(
-        partial.astype(jnp.bfloat16), "tp", scatter_dimension=0, tiled=True
-    )[0].astype(jnp.float32)
+    summed = jnp.sum(lax.all_to_all(partial, "tp", split_axis=0, concat_axis=0, tiled=True), axis=0)
     image_kv = rotate_keys(summed, row_position, head_dim)
     one_hot = (row_request[:, None] == jnp.arange(groups, dtype=jnp.int32)[None, :]).astype(
         jnp.int32

time: 110 us -> 100 us (0.909)
  between operations: 14.2 us -> 0.83 us
  starting transfers between devices: 12.1 us -> 20.3 us
  waiting for transfers between devices: 42.5 us -> 38 us
    reduce_scatter x1 -> x0, waiting for transfers between devices: 25.1 us -> none  [per_device(): lax.psum_scatter(partial.astype(jnp.bfloat16), 'tp', scatter_dimension=0,...]
    all_to_all x0 -> x1, waiting for transfers between devices: none -> 20.6 us  [per_device(): lax.all_to_all(partial, 'tp', split_axis=0, concat_axis=0, tiled=True)]
    all_to_all x0 -> x1, starting transfers between devices: none -> 4.97 us  [per_device(): lax.all_to_all(partial, 'tp', split_axis=0, concat_axis=0, tiled=True)]
    all_to_all x1, starting transfers between devices: 12.1 us -> 15.4 us  [per_device(): got = lax.all_to_all(packet, 'req', split_axis=0, concat_axis=0, tiled=True)]
    reduce_sum x0 -> x1, other arithmetic: none -> 1.87 us  [per_device(): jnp.sum(lax.all_to_all(partial, 'tp', split_axis=0, concat_axis=0, tiled=...]
where the time goes in v3:
time: 100 us
  waiting for transfers between devices  38 us (38%)
  Pallas kernels  20.9 us (21%)
  starting transfers between devices  20.3 us (20%)
  matrix products  8.46 us (8%)
  other arithmetic  6.18 us (6%)
  local copies, waits for them, and re-layouts  5.32 us (5%)
    pallas_call x1, Pallas kernels, attend(): pl.pallas_call(functools.partial(attention_kernel, block, head_dim), grid...  20.9 us
    all_to_all x1, waiting for transfers between devices, per_device(): lax.all_to_all(partial, 'tp', split_axis=0, concat_axis=0, tiled=True)  20.6 us
    all_to_all x1, waiting for transfers between devices, per_device(): got = lax.all_to_all(packet, 'req', split_axis=0, concat_axis=0, tiled=True)  17.4 us
    all_to_all x1, starting transfers between devices, per_device(): got = lax.all_to_all(packet, 'req', split_axis=0, concat_axis=0, tiled=True)  15.4 us
    dot_general x1, matrix products, per_device(): jnp.einsum('rd,dhc->hrc', image_rows, kv_weight, preferred_element_type=j...  5.02 us
    all_to_all x1, starting transfers between devices, per_device(): lax.all_to_all(partial, 'tp', split_axis=0, concat_axis=0, tiled=True)  4.97 us
    unnamed x13, local copies, waits for them, and re-layouts  3.27 us
  transfers between devices with their start and end apart: 2, of which 2 were waited for; matrix products, arithmetic and copies ran while one was open for 3% of the time, Pallas kernels for 0%

profile of v3, /device:TPU:1, one launch (start us, length us, event | category | flops | bytes accessed | tf_op | source)
XLA Modules:
  0.0 100.0 jit_solution(7170505929582652487)
XLA Ops:
  0.0 1.4 %copy-done = bf16[512,1536]{1,0:T(8,128)(2,1)S(1)} copy-done((bf16[512,1536]{1,0:T(8,128)(2,1)S(1)}, bf16[512,1536]{1,0:T(8,128)(2,1)}, u32[]{:S(2)}) %copy-start) | copy-done | bytes 1572888
  1.4 5.0 %fusion.10 = f32[4,512,256]{1,2,0:T(8,128)} fusion(bf16[1536,4,256]{2,1,0:T(4,128)(2,1)} %param.14, bf16[512,1536]{1,0:T(8,128)(2,1)S(1)} %copy-done), kind=kOutput, calls=%fused_computation.13 | convolution fusion | flops 1610612736 | bytes 6815744 | tf_op jit(solution)/shard_map/rd,dhc->hrc/dot_general | solution.py:79
  6.4 5.0 %all-to-all-start = ((f32[4,512,256]{1,2,0:T(8,128)}), f32[4,512,256]{1,2,0:T(8,128)}, u32[]{:S(2)}, u32[]{:S(2)}) async-start(f32[4,512,256]{1,2,0:T(8,128)} %fusion.10), calls=%async_computation | async-start | bytes 4194304 | tf_op jit(solution)/shard_map/all_to_all | solution.py:80
  11.4 1.2 %reduce-window.6 = s32[64,4,128]{2,0,1:T(8,128)S(1)} reduce-window(s32[64,4,128]{2,0,1:T(8,128)S(1)} %fusion.39, s32[]{:T(128)} %constant.6.clone.1), window={size=1x1x128 pad=0_0x0_0x127_0}, to_apply=%region_0.0 | reduce-window | flops 4161536 | bytes 262148 | tf_op jit(solution)/shard_map/reduce-window
  13.1 0.3 convert_reduce_fusion
  13.4 1.0 %fusion.16 = bf16[1024,2]{0,1:T(2,128)(2,1)S(1)} fusion(s32[512]{0:T(512)S(1)} %multiply_add_fusion, pred[1024]{0:T(1024)(128)(4,1)S(1)} %broadcast_compare_fusion, bf16[2]{0:T(256)(128)(2,1)S(1)} %copy-done.4, f32[512,1]{0,1:T(1,128)S(1)} %bitcast.46, f32[512,1]{0,1:T(1,128)S(1)} %bitcast.45), kind=kOutput, calls=%fused_computation.17 | convolution fusion | flops 13110272 | bytes 11268 | tf_op jit(solution)/shard_map/dot_general | solution.py:93
  14.6 0.2 convert_element_type.42
  14.9 20.6 %all-to-all-done = f32[4,512,256]{1,2,0:T(8,128)} async-done(((f32[4,512,256]{1,2,0:T(8,128)}), f32[4,512,256]{1,2,0:T(8,128)}, u32[]{:S(2)}, u32[]{:S(2)}) %all-to-all-start) | async-done | bytes 2097184 | tf_op jit(solution)/shard_map/all_to_all | solution.py:80
  35.5 1.9 %reduce_sum.28 = f32[512,256]{0,1:T(8,128)S(1)} reduce(f32[4,512,256]{1,2,0:T(8,128)} %all-to-all-done, f32[]{:T(128)} %constant.7.clone.1), dimensions={0}, to_apply=%region_3.4 | reduce | flops 393216 | bytes 2621444 | tf_op jit(solution)/shard_map/reduce_sum | solution.py:80
  37.4 0.6 fusion.33
  37.9 0.5 fusion.14
  38.5 0.2 reshape.58
  38.8 0.5 broadcast.62
  39.3 1.0 reduce.4
  40.2 1.2 %reshape.68 = bf16[64,2,2112]{2,1,0:T(2,128)(2,1)} reshape(bf16[64,4224]{1,0:T(8,128)(2,1)S(1)} %reduce.4) | data formatting | bytes 1081344
  41.4 15.4 %all-to-all-start.1 = ((bf16[64,2,2112]{2,1,0:T(2,128)(2,1)}), bf16[64,2,2112]{2,1,0:T(2,128)(2,1)S(1)}, u32[]{:S(2)}, u32[]{:S(2)}) async-start(bf16[64,2,2112]{2,1,0:T(2,128)(2,1)} %reshape.68), calls=%async_computation.1 | async-start | bytes 1114112 | tf_op jit(solution)/shard_map/all_to_all | solution.py:99
  57.4 17.4 %all-to-all-done.1 = bf16[64,2,2112]{2,1,0:T(2,128)(2,1)S(1)} async-done(((bf16[64,2,2112]{2,1,0:T(2,128)(2,1)}), bf16[64,2,2112]{2,1,0:T(2,128)(2,1)S(1)}, u32[]{:S(2)}, u32[]{:S(2)}) %all-to-all-start.1) | async-done | bytes 540704 | tf_op jit(solution)/shard_map/all_to_all | solution.py:99
  74.8 0.6 reshape.69
  75.6 0.3 reshape.63
  75.9 0.4 fusion.22
  76.3 0.7 fusion.1
  76.9 0.2 reshape.61
  77.2 1.9 %fusion.6.kv_ref = bf16[1280,256]{1,0:T(8,128)(2,1)} fusion(bf16[1024,256]{1,0:T(8,128)(2,1)S(1)} %reshape.61, s32[1024]{0:T(1024)S(1)} %fusion.22, bf16[1,1280,1,256]{3,1,2,0:T(8,128)(2,1)S(1)} %copy-done.3, pred[1280]{0:T(1024)(128)(4,1)S(1)} %fusion.1), kind=kOutput, calls=%fused_computation.7 | convolution fusion | flops 673054720 | bytes 1840384 | tf_op jit(solution)/shard_map/dot_general | solution.py:105
  79.1 20.9 %shard_map.82 = bf16[6,1280,128]{2,1,0:T(8,128)(2,1)} custom-call(s32[1]{0:T(128)S(6)} %copy.34.len_ref, bf16[6,1280,128]{2,1,0:T(8,128)(2,1)} %bitcast.43, bf16[1280,256]{1,0:T(8,128)(2,1)} %fusion.6.kv_ref), custom_call_target="tpu_custom_call" | custom-call | tf_op jit(solution)/shard_map/pallas_call | solution.py:64
  (25 shorter events, 0.8 us)
Async XLA Ops:
  0.0 1.4 %copy-start = (bf16[512,1536]{1,0:T(8,128)(2,1)S(1)}, bf16[512,1536]{1,0:T(8,128)(2,1)}, u32[]{:S(2)}) copy-start(bf16[512,1536]{1,0:T(8,128)(2,1)} %param.10) | copy-start | bytes 4718596
  6.4 5.0 %copy-start.1 = (s32[512]{0:T(512)S(1)}, s32[512]{0:T(512)}, u32[]{:S(2)}) copy-start(s32[512]{0:T(512)} %param.11) | copy-start | bytes 6148
  6.4 6.5 %copy-start.2 = (s32[512]{0:T(512)S(1)}, s32[512]{0:T(512)}, u32[]{:S(2)}) copy-start(s32[512]{0:T(512)} %param.12) | copy-start | bytes 6148
  6.4 6.9 %copy-start.4 = (bf16[2]{0:T(256)(128)(2,1)S(1)}, bf16[2]{0:T(256)(128)(2,1)}, u32[]{:S(2)}) copy-start(bf16[2]{0:T(256)(128)(2,1)} %constant.90) | copy-start | bytes 16
  6.4 29.0 %all-to-all-start = ((f32[4,512,256]{1,2,0:T(8,128)}), f32[4,512,256]{1,2,0:T(8,128)}, u32[]{:S(2)}, u32[]{:S(2)}) async-start(f32[4,512,256]{1,2,0:T(8,128)} %fusion.10), calls=%async_computation | async-start | bytes 4194304 | tf_op jit(solution)/shard_map/all_to_all | solution.py:80
  41.4 33.4 %all-to-all-start.1 = ((bf16[64,2,2112]{2,1,0:T(2,128)(2,1)}), bf16[64,2,2112]{2,1,0:T(2,128)(2,1)S(1)}, u32[]{:S(2)}, u32[]{:S(2)}) async-start(bf16[64,2,2112]{2,1,0:T(2,128)(2,1)} %reshape.68), calls=%async_computation.1 | async-start | bytes 1114112 | tf_op jit(solution)/shard_map/all_to_all | solution.py:99
  75.5 1.7 %copy-start.3 = (bf16[1,1280,1,256]{3,1,2,0:T(8,128)(2,1)S(1)}, bf16[1,1280,1,256]{3,1,2,0:T(8,128)(2,1)}, u32[]{:S(2)}) copy-start(bf16[1,1280,1,256]{3,1,2,0:T(8,128)(2,1)} %param.9) | copy-start | bytes 1966084

commit v4 on v3

--- a/solution.py
+++ b/solution.py
@@ -77,7 +77,11 @@
     head_dim = queries.shape[3]
     width = 2 * head_dim
     partial = jnp.einsum("rd,dhc->hrc", image_rows, kv_weight, preferred_element_type=jnp.float32)
-    summed = jnp.sum(lax.all_to_all(partial, "tp", split_axis=0, concat_axis=0, tiled=True), axis=0)
+    me = lax.axis_index("tp")
+    got = lax.all_to_all(partial.astype(jnp.bfloat16), "tp", split_axis=0, concat_axis=0, tiled=True)
+    others = jnp.arange(partial.shape[0], dtype=jnp.int32)[:, None, None] != me
+    own = lax.dynamic_index_in_dim(partial, me, axis=0, keepdims=False)
+    summed = jnp.sum(jnp.where(others, got.astype(jnp.float32), 0.0), axis=0) + own
     image_kv = rotate_keys(summed, row_position, head_dim)
     one_hot = (row_request[:, None] == jnp.arange(groups, dtype=jnp.int32)[None, :]).astype(
         jnp.int32

time: 100 us -> 89.4 us (0.89)
  waiting for transfers between devices: 38 us -> 27.1 us
  local copies, waits for them, and re-layouts: 5.32 us -> 6.67 us
  matrix products: 8.46 us -> 7.17 us
    all_to_all x1, waiting for transfers between devices: 20.6 us -> 9.74 us  [per_device(): lax.all_to_all(partial.astype(jnp.bfloat16), 'tp', split_axis=0, concat_a...]
    reduce_sum x1, other arithmetic: 1.87 us -> 0.29 us  [per_device(): jnp.sum(jnp.where(others, got.astype(jnp.float32), 0.0), axis=0) + own]
    unnamed x13 -> x15, local copies, waits for them, and re-layouts: 3.27 us -> 4.62 us
    dot_general x1, matrix products: 5.02 us -> 3.72 us  [per_device(): jnp.einsum('rd,dhc->hrc', image_rows, kv_weight, preferred_element_type=j...]
    add x0 -> x1, other arithmetic: none -> 1.13 us  [per_device(): jnp.sum(jnp.where(others, got.astype(jnp.float32), 0.0), axis=0) + own]
    convert_element_type x0 -> x1, other arithmetic: none -> 1.1 us  [per_device(): partial.astype(jnp.bfloat16)]
  transfers between devices with their start and end apart: 2 -> 2, of which waited for: 2 -> 2; matrix products, arithmetic and copies ran while one was open for 3% -> 4% of each run, Pallas kernels for 0% -> 0%
where the time goes in v4:
time: 89.4 us; the launch traced here: 89.1 us
  waiting for transfers between devices  27.1 us (30%)
  Pallas kernels  21 us (23%)
  starting transfers between devices  19.4 us (22%)
  matrix products  7.17 us (8%)
  other arithmetic  6.85 us (8%)
  local copies, waits for them, and re-layouts  6.67 us (7%)
    pallas_call x1, Pallas kernels, attend(): pl.pallas_call(functools.partial(attention_kernel, block, head_dim), grid...  21 us
    all_to_all x1, waiting for transfers between devices, per_device(): got = lax.all_to_all(packet, 'req', split_axis=0, concat_axis=0, tiled=True)  17.4 us
    all_to_all x1, starting transfers between devices, per_device(): got = lax.all_to_all(packet, 'req', split_axis=0, concat_axis=0, tiled=True)  14.5 us
    all_to_all x1, waiting for transfers between devices, per_device(): lax.all_to_all(partial.astype(jnp.bfloat16), 'tp', split_axis=0, concat_a...  9.74 us
    all_to_all x1, starting transfers between devices, per_device(): lax.all_to_all(partial.astype(jnp.bfloat16), 'tp', split_axis=0, concat_a...  4.97 us
    unnamed x15, local copies, waits for them, and re-layouts  4.62 us
    dot_general x1, matrix products, per_device(): jnp.einsum('rd,dhc->hrc', image_rows, kv_weight, preferred_element_type=j...  3.72 us
    dot_general x1, matrix products, per_device(): jnp.dot(place, got_kv, preferred_element_type=jnp.float32)  1.93 us
  transfers between devices with their start and end apart: 2, of which 2 were waited for; matrix products, arithmetic and copies ran while one was open for 4% of the time, Pallas kernels for 0%

profile of v4, /device:TPU:1, one launch (start us, length us, event | category | flops | bytes accessed | tf_op | source)
XLA Modules:
  0.0 89.1 jit_solution(15271427297714412553)
XLA Ops:
  0.0 1.4 %copy-done = bf16[512,1536]{1,0:T(8,128)(2,1)S(1)} copy-done((bf16[512,1536]{1,0:T(8,128)(2,1)S(1)}, bf16[512,1536]{1,0:T(8,128)(2,1)}, u32[]{:S(2)}) %copy-start) | copy-done | bytes 1572888
  1.4 3.7 %fusion.2 = f32[4,256,512]{2,1,0:T(8,128)S(1)} fusion(bf16[1536,4,256]{2,1,0:T(4,128)(2,1)} %param.14, bf16[512,1536]{1,0:T(8,128)(2,1)S(1)} %copy-done), kind=kOutput, calls=%fused_computation.3 | convolution fusion | flops 1610612736 | bytes 6815744 | tf_op jit(solution)/shard_map/rd,dhc->hrc/dot_general | solution.py:79
  5.1 1.3 %copy-done.1 = f32[4,256,512]{2,1,0:T(8,128)} copy-done((f32[4,256,512]{2,1,0:T(8,128)}, f32[4,256,512]{2,1,0:T(8,128)S(1)}, u32[]{:S(2)}) %copy-start.1) | copy-done | bytes 2097176
  6.5 1.1 %convert_bitcast_fusion = bf16[4,512,256]{1,2,0:T(8,128)(2,1)} fusion(f32[4,256,512]{2,1,0:T(8,128)S(1)} %fusion.2), kind=kLoop, calls=%fused_computation.20 | loop fusion | flops 524288 | bytes 3145728 | tf_op jit(solution)/shard_map/convert_element_type | solution.py:81
  7.6 5.0 %all-to-all-start = ((bf16[4,512,256]{1,2,0:T(8,128)(2,1)}), bf16[4,512,256]{1,2,0:T(8,128)(2,1)S(1)}, u32[]{:S(2)}, u32[]{:S(2)}) async-start(bf16[4,512,256]{1,2,0:T(8,128)(2,1)} %convert_bitcast_fusion), calls=%async_computation | async-start | bytes 2097152 | tf_op jit(solution)/shard_map/all_to_all | solution.py:81
  12.6 1.2 %reduce-window.6 = s32[64,4,128]{2,0,1:T(8,128)S(1)} reduce-window(s32[64,4,128]{2,0,1:T(8,128)S(1)} %fusion.36, s32[]{:T(128)} %constant.13.clone.1), window={size=1x1x128 pad=0_0x0_0x127_0}, to_apply=%region_0.1 | reduce-window | flops 4161536 | bytes 262148 | tf_op jit(solution)/shard_map/reduce-window
  14.2 0.3 convert_reduce_fusion
  14.6 1.0 %fusion.13 = bf16[1024,2]{0,1:T(2,128)(2,1)S(1)} fusion(s32[512]{0:T(512)S(1)} %multiply_add_fusion, pred[1024]{0:T(1024)(128)(4,1)S(1)} %broadcast_compare_fusion, bf16[2]{0:T(256)(128)(2,1)S(1)} %copy-done.5, f32[512,1]{0,1:T(1,128)S(1)} %bitcast.50, f32[512,1]{0,1:T(1,128)S(1)} %bitcast.49), kind=kOutput, calls=%fused_computation.17 | convolution fusion | flops 13110272 | bytes 11268 | tf_op jit(solution)/shard_map/dot_general | solution.py:97
  16.1 9.7 %all-to-all-done = bf16[4,512,256]{1,2,0:T(8,128)(2,1)S(1)} async-done(((bf16[4,512,256]{1,2,0:T(8,128)(2,1)}), bf16[4,512,256]{1,2,0:T(8,128)(2,1)S(1)}, u32[]{:S(2)}, u32[]{:S(2)}) %all-to-all-start) | async-done | bytes 1048608 | tf_op jit(solution)/shard_map/all_to_all | solution.py:81
  25.8 0.3 select_reduce_fusion
  26.1 1.1 %bitcast_add_fusion = f32[512,256]{0,1:T(8,128)S(1)} fusion(f32[512,256]{0,1:T(8,128)S(1)} %select_reduce_fusion, f32[4,256,512]{2,1,0:T(8,128)} %copy-done.1, s32[]{:T(128)S(6)} %select_n.17), kind=kLoop, calls=%fused_computation.29 | loop fusion | flops 131072 | bytes 1572868 | tf_op jit(solution)/shard_map/add | solution.py:84
  27.3 0.6 fusion.30
  27.8 0.5 fusion.11
  28.6 0.5 broadcast.67
  29.2 1.0 %reduce.4 = bf16[64,4224]{1,0:T(8,128)(2,1)S(1)} reduce(bf16[64,1,4224]{2,0,1:T(8,128)(2,1)S(1)} %fusion.18, bf16[]{:T(256)} %broadcast.67), dimensions={1}, to_apply=%copy.23.reduce_sub_computation | reduce | bytes 1081346 | tf_op jit(solution)/shard_map/all_to_all | solution.py:103
  30.1 1.2 %reshape.73 = bf16[64,2,2112]{2,1,0:T(2,128)(2,1)} reshape(bf16[64,4224]{1,0:T(8,128)(2,1)S(1)} %reduce.4) | data formatting | bytes 1081344
  31.3 14.5 %all-to-all-start.1 = ((bf16[64,2,2112]{2,1,0:T(2,128)(2,1)}), bf16[64,2,2112]{2,1,0:T(2,128)(2,1)S(1)}, u32[]{:S(2)}, u32[]{:S(2)}) async-start(bf16[64,2,2112]{2,1,0:T(2,128)(2,1)} %reshape.73), calls=%async_computation.1 | async-start | bytes 1114112 | tf_op jit(solution)/shard_map/all_to_all | solution.py:103
  46.4 17.4 %all-to-all-done.1 = bf16[64,2,2112]{2,1,0:T(2,128)(2,1)S(1)} async-done(((bf16[64,2,2112]{2,1,0:T(2,128)(2,1)}), bf16[64,2,2112]{2,1,0:T(2,128)(2,1)S(1)}, u32[]{:S(2)}, u32[]{:S(2)}) %all-to-all-start.1) | async-done | bytes 540704 | tf_op jit(solution)/shard_map/all_to_all | solution.py:103
  63.8 0.6 reshape.74
  64.6 0.3 reshape.68
  64.9 0.4 fusion.19
  65.3 0.7 fusion.1
  66.2 1.9 %fusion.6.kv_ref = bf16[1280,256]{1,0:T(8,128)(2,1)} fusion(bf16[1024,256]{1,0:T(8,128)(2,1)S(1)} %reshape.66, s32[1024]{0:T(1024)S(1)} %fusion.19, bf16[1,1280,1,256]{3,1,2,0:T(8,128)(2,1)S(1)} %copy-done.4, pred[1280]{0:T(1024)(128)(4,1)S(1)} %fusion.1), kind=kOutput, calls=%fused_computation.7 | convolution fusion | flops 673054720 | bytes 1840384 | tf_op jit(solution)/shard_map/dot_general | solution.py:109
  68.1 21.0 %shard_map.82 = bf16[6,1280,128]{2,1,0:T(8,128)(2,1)} custom-call(s32[1]{0:T(128)S(6)} %copy.32.len_ref, bf16[6,1280,128]{2,1,0:T(8,128)(2,1)} %bitcast.47, bf16[1280,256]{1,0:T(8,128)(2,1)} %fusion.6.kv_ref), custom_call_target="tpu_custom_call" | custom-call | tf_op jit(solution)/shard_map/pallas_call | solution.py:64
  (30 shorter events, 1.6 us)
Async XLA Ops:
  0.0 1.4 %copy-start = (bf16[512,1536]{1,0:T(8,128)(2,1)S(1)}, bf16[512,1536]{1,0:T(8,128)(2,1)}, u32[]{:S(2)}) copy-start(bf16[512,1536]{1,0:T(8,128)(2,1)} %param.10) | copy-start | bytes 4718596
  5.1 1.4 %copy-start.1 = (f32[4,256,512]{2,1,0:T(8,128)}, f32[4,256,512]{2,1,0:T(8,128)S(1)}, u32[]{:S(2)}) copy-start(f32[4,256,512]{2,1,0:T(8,128)S(1)} %fusion.2) | copy-start | bytes 6291460
  6.5 6.1 %copy-start.3 = (s32[512]{0:T(512)S(1)}, s32[512]{0:T(512)}, u32[]{:S(2)}) copy-start(s32[512]{0:T(512)} %param.12) | copy-start | bytes 6148
  6.5 6.1 %copy-start.2 = (s32[512]{0:T(512)S(1)}, s32[512]{0:T(512)}, u32[]{:S(2)}) copy-start(s32[512]{0:T(512)} %param.11) | copy-start | bytes 6148
  7.6 7.0 %copy-start.5 = (bf16[2]{0:T(256)(128)(2,1)S(1)}, bf16[2]{0:T(256)(128)(2,1)}, u32[]{:S(2)}) copy-start(bf16[2]{0:T(256)(128)(2,1)} %constant.98) | copy-start | bytes 16
  7.6 18.2 %all-to-all-start = ((bf16[4,512,256]{1,2,0:T(8,128)(2,1)}), bf16[4,512,256]{1,2,0:T(8,128)(2,1)S(1)}, u32[]{:S(2)}, u32[]{:S(2)}) async-start(bf16[4,512,256]{1,2,0:T(8,128)(2,1)} %convert_bitcast_fusion), calls=%async_computation | async-start | bytes 2097152 | tf_op jit(solution)/shard_map/all_to_all | solution.py:81
  31.3 32.5 %all-to-all-start.1 = ((bf16[64,2,2112]{2,1,0:T(2,128)(2,1)}), bf16[64,2,2112]{2,1,0:T(2,128)(2,1)S(1)}, u32[]{:S(2)}, u32[]{:S(2)}) async-start(bf16[64,2,2112]{2,1,0:T(2,128)(2,1)} %reshape.73), calls=%async_computation.1 | async-start | bytes 1114112 | tf_op jit(solution)/shard_map/all_to_all | solution.py:103
  64.5 1.7 %copy-start.4 = (bf16[1,1280,1,256]{3,1,2,0:T(8,128)(2,1)S(1)}, bf16[1,1280,1,256]{3,1,2,0:T(8,128)(2,1)}, u32[]{:S(2)}) copy-start(bf16[1,1280,1,256]{3,1,2,0:T(8,128)(2,1)} %param.9) | copy-start | bytes 1966084

commit v5 on v4

--- a/solution.py
+++ b/solution.py
@@ -24,7 +24,7 @@
     return rotated.astype(jnp.bfloat16)
 
 
-def attention_kernel(block, head_dim, len_ref, q_ref, kv_ref, o_ref):
+def attention_kernel(block, head_dim, len_ref, q_ref, kt_ref, vx_ref, o_ref):
     prompt = q_ref.shape[1]
     length = len_ref[0]
     scale = head_dim ** (-0.5)
@@ -32,31 +32,31 @@
         row_start = index * block
         keys_used = row_start + block
         query = q_ref[0, row_start:keys_used, :]
-        keys = kv_ref[0:keys_used, 0:head_dim]
-        scores = lax.dot_general(
-            query, keys, (((1,), (1,)), ((), ())), preferred_element_type=jnp.float32
-        ) * scale
+        scores = jnp.dot(query, kt_ref[:, 0:keys_used], preferred_element_type=jnp.float32)
         query_index = row_start + lax.broadcasted_iota(jnp.int32, (block, 1), 0)
         limit = jnp.minimum(query_index, length - 1)
         key_index = lax.broadcasted_iota(jnp.int32, (1, keys_used), 1)
         scores = jnp.where(key_index <= limit, scores, jnp.float32(-1e30))
         highest = jnp.max(scores, axis=-1, keepdims=True)
-        expo = jnp.exp(scores - highest)
-        total = jnp.sum(expo, axis=-1, keepdims=True)
-        weights = (expo * (1.0 / total)).astype(jnp.bfloat16)
-        values = kv_ref[0:keys_used, head_dim:]
-        result = jnp.dot(weights, values, preferred_element_type=jnp.float32)
+        weights = jnp.exp((scores - highest) * scale).astype(jnp.bfloat16)
+        both = jnp.dot(weights, vx_ref[0:keys_used, :], preferred_element_type=jnp.float32)
+        result = both[:, :head_dim] / both[:, head_dim : head_dim + 1]
         result = jnp.where(query_index < length, result, jnp.float32(0.0))
         o_ref[0, row_start:keys_used, :] = result.astype(o_ref.dtype)
 
 
 def attend(heads_first, prompt_kv, length, head_dim, block=256):
     heads, prompt, _ = heads_first.shape
+    keys_t = jnp.transpose(prompt_kv[:, :head_dim])
+    values_ext = jnp.concatenate(
+        [prompt_kv[:, head_dim:], jnp.ones((prompt, head_dim), prompt_kv.dtype)], axis=1
+    )
     grid_spec = pltpu.PrefetchScalarGridSpec(
         num_scalar_prefetch=1,
         grid=(heads,),
         in_specs=[
             pl.BlockSpec((1, prompt, head_dim), lambda h, lens: (h, 0, 0)),
+            pl.BlockSpec((head_dim, prompt), lambda h, lens: (0, 0)),
             pl.BlockSpec((prompt, 2 * head_dim), lambda h, lens: (0, 0)),
         ],
         out_specs=pl.BlockSpec((1, prompt, head_dim), lambda h, lens: (h, 0, 0)),
@@ -66,7 +66,7 @@
         grid_spec=grid_spec,
         out_shape=jax.ShapeDtypeStruct((heads, prompt, head_dim), jnp.bfloat16),
         compiler_params=pltpu.CompilerParams(dimension_semantics=("arbitrary",)),
-    )(length, heads_first, prompt_kv)
+    )(length, heads_first, keys_t, values_ext)
 
 
 def per_device(queries, text_kv, image_rows, row_request, row_position, prompt_lengths, kv_weight):

time: 89.4 us -> 86.7 us (0.970)
  Pallas kernels: 21 us -> 17.2 us
  local copies, waits for them, and re-layouts: 6.67 us -> 8.52 us
    pallas_call x1, Pallas kernels: 21 us -> 17.2 us  [attend(): pl.pallas_call(functools.partial(attention_kernel, block, head_dim), grid...]
    transpose x0 -> x1, local copies, waits for them, and re-layouts: none -> 0.91 us  [attend(): keys_t = jnp.transpose(prompt_kv[:, :head_dim])]
    concatenate x0 -> x1, local copies, waits for them, and re-layouts: none -> 0.89 us  [attend(): jnp.concatenate([prompt_kv[:, head_dim:], jnp.ones((prompt, head_dim), pr...]
where the time goes in v5:
time: 86.7 us; the launch traced here: 86.3 us
  waiting for transfers between devices  27.1 us (31%)
  starting transfers between devices  19.4 us (22%)
  Pallas kernels  17.2 us (20%)
  local copies, waits for them, and re-layouts  8.52 us (10%)
  other arithmetic  6.85 us (8%)
  matrix products  6.33 us (7%)
  between operations  0.87 us (1%)
    all_to_all x1, waiting for transfers between devices, per_device(): got = lax.all_to_all(packet, 'req', split_axis=0, concat_axis=0, tiled=True)  17.4 us
    pallas_call x1, Pallas kernels, attend(): pl.pallas_call(functools.partial(attention_kernel, block, head_dim), grid...  17.2 us
    all_to_all x1, starting transfers between devices, per_device(): got = lax.all_to_all(packet, 'req', split_axis=0, concat_axis=0, tiled=True)  14.5 us
    all_to_all x1, waiting for transfers between devices, per_device(): lax.all_to_all(partial.astype(jnp.bfloat16), 'tp', split_axis=0, concat_a...  9.74 us
    all_to_all x1, starting transfers between devices, per_device(): lax.all_to_all(partial.astype(jnp.bfloat16), 'tp', split_axis=0, concat_a...  4.97 us
    unnamed x15, local copies, waits for them, and re-layouts  4.62 us
    dot_general x1, matrix products, per_device(): jnp.einsum('rd,dhc->hrc', image_rows, kv_weight, preferred_element_type=j...  3.72 us
    another operation x3, other arithmetic  1.8 us
  transfers between devices with their start and end apart: 2, of which 2 were waited for; matrix products, arithmetic and copies ran while one was open for 4% of the time, Pallas kernels for 0%

profile of v5, /device:TPU:1, one launch (start us, length us, event | category | flops | bytes accessed | tf_op | source)
XLA Modules:
  0.0 86.3 jit_solution(18004337296841377397)
XLA Ops:
  0.0 1.4 %copy-done = bf16[512,1536]{1,0:T(8,128)(2,1)S(1)} copy-done((bf16[512,1536]{1,0:T(8,128)(2,1)S(1)}, bf16[512,1536]{1,0:T(8,128)(2,1)}, u32[]{:S(2)}) %copy-start) | copy-done | bytes 1572888
  1.4 3.7 %fusion.2 = f32[4,256,512]{2,1,0:T(8,128)S(1)} fusion(bf16[1536,4,256]{2,1,0:T(4,128)(2,1)} %param.14, bf16[512,1536]{1,0:T(8,128)(2,1)S(1)} %copy-done), kind=kOutput, calls=%fused_computation.3 | convolution fusion | flops 1610612736 | bytes 6815744 | tf_op jit(solution)/shard_map/rd,dhc->hrc/dot_general | solution.py:79
  5.1 1.3 %copy-done.1 = f32[4,256,512]{2,1,0:T(8,128)} copy-done((f32[4,256,512]{2,1,0:T(8,128)}, f32[4,256,512]{2,1,0:T(8,128)S(1)}, u32[]{:S(2)}) %copy-start.1) | copy-done | bytes 2097176
  6.5 1.1 %convert_bitcast_fusion = bf16[4,512,256]{1,2,0:T(8,128)(2,1)} fusion(f32[4,256,512]{2,1,0:T(8,128)S(1)} %fusion.2), kind=kLoop, calls=%fused_computation.20 | loop fusion | flops 524288 | bytes 3145728 | tf_op jit(solution)/shard_map/convert_element_type | solution.py:81
  7.6 5.0 %all-to-all-start = ((bf16[4,512,256]{1,2,0:T(8,128)(2,1)}), bf16[4,512,256]{1,2,0:T(8,128)(2,1)S(1)}, u32[]{:S(2)}, u32[]{:S(2)}) async-start(bf16[4,512,256]{1,2,0:T(8,128)(2,1)} %convert_bitcast_fusion), calls=%async_computation | async-start | bytes 2097152 | tf_op jit(solution)/shard_map/all_to_all | solution.py:81
  12.6 1.2 %reduce-window.6 = s32[64,4,128]{2,0,1:T(8,128)S(1)} reduce-window(s32[64,4,128]{2,0,1:T(8,128)S(1)} %fusion.36, s32[]{:T(128)} %constant.14.clone.1), window={size=1x1x128 pad=0_0x0_0x127_0}, to_apply=%region_0.1 | reduce-window | flops 4161536 | bytes 262148 | tf_op jit(solution)/shard_map/reduce-window
  14.6 1.0 %fusion.13 = bf16[1024,2]{0,1:T(2,128)(2,1)S(1)} fusion(s32[512]{0:T(512)S(1)} %multiply_add_fusion, pred[1024]{0:T(1024)(128)(4,1)S(1)} %broadcast_compare_fusion, bf16[2]{0:T(256)(128)(2,1)S(1)} %copy-done.5, f32[512,1]{0,1:T(1,128)S(1)} %bitcast.52, f32[512,1]{0,1:T(1,128)S(1)} %bitcast.51), kind=kOutput, calls=%fused_computation.17 | convolution fusion | flops 13110272 | bytes 11268 | tf_op jit(solution)/shard_map/dot_general | solution.py:97
  16.1 9.7 %all-to-all-done = bf16[4,512,256]{1,2,0:T(8,128)(2,1)S(1)} async-done(((bf16[4,512,256]{1,2,0:T(8,128)(2,1)}), bf16[4,512,256]{1,2,0:T(8,128)(2,1)S(1)}, u32[]{:S(2)}, u32[]{:S(2)}) %all-to-all-start) | async-done | bytes 1048608 | tf_op jit(solution)/shard_map/all_to_all | solution.py:81
  26.1 1.1 %bitcast_add_fusion = f32[512,256]{0,1:T(8,128)S(1)} fusion(f32[512,256]{0,1:T(8,128)S(1)} %select_reduce_fusion, f32[4,256,512]{2,1,0:T(8,128)} %copy-done.1, s32[]{:T(128)S(6)} %select_n.17), kind=kLoop, calls=%fused_computation.29 | loop fusion | flops 131072 | bytes 1572868 | tf_op jit(solution)/shard_map/add | solution.py:84
  27.3 0.6 fusion.30
  27.8 0.5 fusion.11
  28.6 0.5 broadcast.69
  29.2 1.0 %reduce.4 = bf16[64,4224]{1,0:T(8,128)(2,1)S(1)} reduce(bf16[64,1,4224]{2,0,1:T(8,128)(2,1)S(1)} %fusion.18, bf16[]{:T(256)} %broadcast.69), dimensions={1}, to_apply=%copy.27.reduce_sub_computation | reduce | bytes 1081346 | tf_op jit(solution)/shard_map/all_to_all | solution.py:103
  30.1 1.2 %reshape.73 = bf16[64,2,2112]{2,1,0:T(2,128)(2,1)} reshape(bf16[64,4224]{1,0:T(8,128)(2,1)S(1)} %reduce.4) | data formatting | bytes 1081344
  31.3 14.5 %all-to-all-start.1 = ((bf16[64,2,2112]{2,1,0:T(2,128)(2,1)}), bf16[64,2,2112]{2,1,0:T(2,128)(2,1)S(1)}, u32[]{:S(2)}, u32[]{:S(2)}) async-start(bf16[64,2,2112]{2,1,0:T(2,128)(2,1)} %reshape.73), calls=%async_computation.1 | async-start | bytes 1114112 | tf_op jit(solution)/shard_map/all_to_all | solution.py:103
  46.4 17.4 %all-to-all-done.1 = bf16[64,2,2112]{2,1,0:T(2,128)(2,1)S(1)} async-done(((bf16[64,2,2112]{2,1,0:T(2,128)(2,1)}), bf16[64,2,2112]{2,1,0:T(2,128)(2,1)S(1)}, u32[]{:S(2)}, u32[]{:S(2)}) %all-to-all-start.1) | async-done | bytes 540704 | tf_op jit(solution)/shard_map/all_to_all | solution.py:103
  63.8 0.6 reshape.74
  64.6 0.3 reshape.68
  64.9 0.4 fusion.19
  65.3 0.7 fusion.1
  66.2 1.1 %fusion.6 = bf16[1280,256]{1,0:T(8,128)(2,1)S(1)} fusion(bf16[1024,256]{1,0:T(8,128)(2,1)S(1)} %reshape.66, s32[1024]{0:T(1024)S(1)} %fusion.19, bf16[1,1280,1,256]{3,1,2,0:T(8,128)(2,1)S(1)} %copy-done.4, pred[1280]{0:T(1024)(128)(4,1)S(1)} %fusion.1), kind=kOutput, calls=%fused_computation.7 | convolution fusion | flops 673054720 | bytes 1840384 | tf_op jit(solution)/shard_map/dot_general | solution.py:109
  67.3 0.9 %copy.28.kt_ref = bf16[128,1280]{1,0:T(8,128)(2,1)} copy(bf16[128,1280]{0,1:T(8,128)(2,1)S(1)} %get-tuple-element.6) | data formatting | bytes 655360 | tf_op jit(solution)/shard_map/transpose | solution.py:50
  68.2 0.9 %concatenate.12.vx_ref = bf16[1280,256]{1,0:T(8,128)(2,1)} pad(bf16[1280,128]{1,0:T(8,128)(2,1)S(1)} %get-tuple-element.5, bf16[]{:T(256)} %constant.36.clone.1), padding=0_0x0_128 | pad | bytes 983042 | tf_op jit(solution)/shard_map/concatenate | solution.py:51
  69.1 17.2 %shard_map.82 = bf16[6,1280,128]{2,1,0:T(8,128)(2,1)} custom-call(s32[1]{0:T(128)S(6)} %copy.37.len_ref, bf16[6,1280,128]{2,1,0:T(8,128)(2,1)} %bitcast.49, bf16[128,1280]{1,0:T(8,128)(2,1)} %copy.28.kt_ref, bf16[1280,256]{1,0:T(8,128)(2,1)} %concatenate.12.vx_ref), custom_call_target="tpu_custom_call" | custom-call | tf_op jit(solution)/shard_map/pallas_call | solution.py:64
  (33 shorter events, 2.2 us)
Async XLA Ops:
  0.0 1.4 %copy-start = (bf16[512,1536]{1,0:T(8,128)(2,1)S(1)}, bf16[512,1536]{1,0:T(8,128)(2,1)}, u32[]{:S(2)}) copy-start(bf16[512,1536]{1,0:T(8,128)(2,1)} %param.10) | copy-start | bytes 4718596
  5.1 1.4 %copy-start.1 = (f32[4,256,512]{2,1,0:T(8,128)}, f32[4,256,512]{2,1,0:T(8,128)S(1)}, u32[]{:S(2)}) copy-start(f32[4,256,512]{2,1,0:T(8,128)S(1)} %fusion.2) | copy-start | bytes 6291460
  6.5 6.1 %copy-start.3 = (s32[512]{0:T(512)S(1)}, s32[512]{0:T(512)}, u32[]{:S(2)}) copy-start(s32[512]{0:T(512)} %param.12) | copy-start | bytes 6148
  6.5 6.1 %copy-start.2 = (s32[512]{0:T(512)S(1)}, s32[512]{0:T(512)}, u32[]{:S(2)}) copy-start(s32[512]{0:T(512)} %param.11) | copy-start | bytes 6148
  7.6 7.0 %copy-start.5 = (bf16[2]{0:T(256)(128)(2,1)S(1)}, bf16[2]{0:T(256)(128)(2,1)}, u32[]{:S(2)}) copy-start(bf16[2]{0:T(256)(128)(2,1)} %constant.102) | copy-start | bytes 16
  7.6 18.2 %all-to-all-start = ((bf16[4,512,256]{1,2,0:T(8,128)(2,1)}), bf16[4,512,256]{1,2,0:T(8,128)(2,1)S(1)}, u32[]{:S(2)}, u32[]{:S(2)}) async-start(bf16[4,512,256]{1,2,0:T(8,128)(2,1)} %convert_bitcast_fusion), calls=%async_computation | async-start | bytes 2097152 | tf_op jit(solution)/shard_map/all_to_all | solution.py:81
  31.3 32.5 %all-to-all-start.1 = ((bf16[64,2,2112]{2,1,0:T(2,128)(2,1)}), bf16[64,2,2112]{2,1,0:T(2,128)(2,1)S(1)}, u32[]{:S(2)}, u32[]{:S(2)}) async-start(bf16[64,2,2112]{2,1,0:T(2,128)(2,1)} %reshape.73), calls=%async_computation.1 | async-start | bytes 1114112 | tf_op jit(solution)/shard_map/all_to_all | solution.py:103
  64.5 1.7 %copy-start.4 = (bf16[1,1280,1,256]{3,1,2,0:T(8,128)(2,1)S(1)}, bf16[1,1280,1,256]{3,1,2,0:T(8,128)(2,1)}, u32[]{:S(2)}) copy-start(bf16[1,1280,1,256]{3,1,2,0:T(8,128)(2,1)} %param.9) | copy-start | bytes 1966084

commit v6 on v5

--- a/solution.py
+++ b/solution.py
@@ -45,12 +45,8 @@
         o_ref[0, row_start:keys_used, :] = result.astype(o_ref.dtype)
 
 
-def attend(heads_first, prompt_kv, length, head_dim, block=256):
+def attend(heads_first, keys_t, values_ext, length, head_dim, block=256):
     heads, prompt, _ = heads_first.shape
-    keys_t = jnp.transpose(prompt_kv[:, :head_dim])
-    values_ext = jnp.concatenate(
-        [prompt_kv[:, head_dim:], jnp.ones((prompt, head_dim), prompt_kv.dtype)], axis=1
-    )
     grid_spec = pltpu.PrefetchScalarGridSpec(
         num_scalar_prefetch=1,
         grid=(heads,),
@@ -76,11 +72,12 @@
     prompt = queries.shape[1]
     head_dim = queries.shape[3]
     width = 2 * head_dim
-    partial = jnp.einsum("rd,dhc->hrc", image_rows, kv_weight, preferred_element_type=jnp.float32)
     me = lax.axis_index("tp")
-    got = lax.all_to_all(partial.astype(jnp.bfloat16), "tp", split_axis=0, concat_axis=0, tiled=True)
+    partial = jnp.einsum("rd,dhc->hrc", image_rows, kv_weight, preferred_element_type=jnp.bfloat16)
+    got = lax.all_to_all(partial, "tp", split_axis=0, concat_axis=0, tiled=True)
+    own_weight = lax.dynamic_index_in_dim(kv_weight, me, axis=1, keepdims=False)
+    own = jnp.dot(image_rows, own_weight, preferred_element_type=jnp.float32)
     others = jnp.arange(partial.shape[0], dtype=jnp.int32)[:, None, None] != me
-    own = lax.dynamic_index_in_dim(partial, me, axis=0, keepdims=False)
     summed = jnp.sum(jnp.where(others, got.astype(jnp.float32), 0.0), axis=0) + own
     image_kv = rotate_keys(summed, row_position, head_dim)
     one_hot = (row_request[:, None] == jnp.arange(groups, dtype=jnp.int32)[None, :]).astype(
@@ -92,25 +89,35 @@
     slots = groups * capacity
     pick = (target[None, :] == jnp.arange(slots, dtype=jnp.int32)[:, None]).astype(jnp.bfloat16)
     send_kv = jnp.dot(pick, image_kv, preferred_element_type=jnp.float32).astype(jnp.bfloat16)
-    pos_f = row_position.astype(jnp.float32)
+    pos_f = row_position.astype(jnp.float32) + 1.0
     digits = jnp.stack([jnp.floor(pos_f / 16.0), pos_f - 16.0 * jnp.floor(pos_f / 16.0)], axis=1)
     send_pos = jnp.dot(pick.astype(jnp.float32), digits, precision=lax.Precision.HIGHEST)
-    filled = jnp.sum(pick.astype(jnp.float32), axis=1, keepdims=True)
-    send_pos = jnp.where(filled > 0, send_pos, jnp.float32(prompt / 16.0) * jnp.array([1.0, 0.0]))
     tail = send_pos.reshape(groups, 2 * capacity).astype(jnp.bfloat16)
     tail = jnp.pad(tail, ((0, 0), (0, 128 - 2 * capacity)))
     packet = jnp.concatenate([send_kv.reshape(groups, capacity * width), tail], axis=1)
+    text = text_kv[0, :, 0, :]
+    text_keys_t = jnp.transpose(text[:, :head_dim])
+    ones = jnp.ones((prompt, head_dim), text.dtype)
+    text_values_ext = jnp.concatenate([text[:, head_dim:], ones], axis=1)
     got = lax.all_to_all(packet, "req", split_axis=0, concat_axis=0, tiled=True)
     got_kv = got[:, : capacity * width].reshape(slots, width)
     got_digits = got[:, capacity * width : capacity * width + 2 * capacity].astype(jnp.int32)
     got_digits = got_digits.reshape(slots, 2)
-    places = got_digits[:, 0] * 16 + got_digits[:, 1]
-    place = (places[None, :] == jnp.arange(prompt, dtype=jnp.int32)[:, None]).astype(jnp.bfloat16)
-    placed = jnp.dot(place, got_kv, preferred_element_type=jnp.float32).astype(jnp.bfloat16)
-    hit = jnp.any(places[None, :] == jnp.arange(prompt, dtype=jnp.int32)[:, None], axis=1)
-    prompt_kv = jnp.where(hit[:, None], placed, text_kv[0, :, 0, :])
+    places = got_digits[:, 0] * 16 + got_digits[:, 1] - 1
+    match = places[None, :] == jnp.arange(prompt, dtype=jnp.int32)[:, None]
+    place = match.astype(jnp.bfloat16)
+    hit = jnp.any(match, axis=1)
+    image_keys_t = jnp.einsum(
+        "sd,ps->dp", got_kv[:, :head_dim], place, preferred_element_type=jnp.float32
+    ).astype(jnp.bfloat16)
+    image_values = jnp.dot(place, got_kv[:, head_dim:], preferred_element_type=jnp.float32)
+    keys_t = jnp.where(hit[None, :], image_keys_t, text_keys_t)
+    values_ext = jnp.where(
+        hit[:, None], jnp.concatenate([image_values.astype(jnp.bfloat16), ones], axis=1),
+        text_values_ext,
+    )
     heads_first = jnp.transpose(queries[0], (1, 0, 2))
-    out = attend(heads_first, prompt_kv, prompt_lengths, head_dim)
+    out = attend(heads_first, keys_t, values_ext, prompt_lengths, head_dim)
     return jnp.transpose(out, (1, 0, 2))[None]
 
 

time: 86.7 us -> 87.1 us (level)
  waiting for transfers between devices: 27.1 us -> 22.9 us
  local copies, waits for them, and re-layouts: 8.52 us -> 11.9 us
  matrix products: 6.33 us -> 8.88 us
  other arithmetic: 6.85 us -> 5.46 us
    dynamic_slice x0 -> x1, local copies, waits for them, and re-layouts: none -> 4.54 us  [per_device(): own_weight = lax.dynamic_index_in_dim(kv_weight, me, axis=1, keepdims=False)]
    all_to_all x1, waiting for transfers between devices: 9.74 us -> 5.52 us  [per_device(): got = lax.all_to_all(partial, 'tp', split_axis=0, concat_axis=0, tiled=True)]
    dot_general x1 -> x3, matrix products: 1.09 us -> 2.64 us  [the longest x1 1.02 us: per_device(): jnp.einsum('sd,ps->dp', got_kv[:, :head_dim], place, preferred_element_ty...]
    add x2 -> x0, other arithmetic: 1.49 us -> none  [the longest x1 1.13 us: per_device(): jnp.sum(jnp.where(others, got.astype(jnp.float32), 0.0), axis=0) + own]
    convert_element_type x1 -> x0, other arithmetic: 1.1 us -> none  [per_device(): partial.astype(jnp.bfloat16)]
    select_n x0 -> x1, other arithmetic: none -> 1.07 us  [per_device(): jnp.where(hit[:, None], jnp.concatenate([image_values.astype(jnp.bfloat16...]
    dot_general x1, matrix products: 3.72 us -> 4.72 us  [per_device(): jnp.einsum('rd,dhc->hrc', image_rows, kv_weight, preferred_element_type=j...]
    select_n x0 -> x1, local copies, waits for them, and re-layouts: none -> 0.91 us  [per_device(): keys_t = jnp.where(hit[None, :], image_keys_t, text_keys_t)]
  transfers between devices with their start and end apart: 2 -> 2, of which waited for: 2 -> 2; matrix products, arithmetic and copies ran while one was open for 4% -> 9% of each run, Pallas kernels for 0% -> 0%
where the time goes in v6:
time: 87.1 us; the launch traced here: 86.6 us
  waiting for transfers between devices  22.9 us (26%)
  starting transfers between devices  19.4 us (22%)
  Pallas kernels  17.2 us (20%)
  local copies, waits for them, and re-layouts  11.9 us (14%)
  matrix products  8.88 us (10%)
  other arithmetic  5.46 us (6%)
    all_to_all x1, waiting for transfers between devices, per_device(): got = lax.all_to_all(packet, 'req', split_axis=0, concat_axis=0, tiled=True)  17.4 us
    pallas_call x1, Pallas kernels, attend(): pl.pallas_call(functools.partial(attention_kernel, block, head_dim), grid...  17.2 us
    all_to_all x1, starting transfers between devices, per_device(): got = lax.all_to_all(packet, 'req', split_axis=0, concat_axis=0, tiled=True)  14.5 us
    all_to_all x1, waiting for transfers between devices, per_device(): got = lax.all_to_all(partial, 'tp', split_axis=0, concat_axis=0, tiled=True)  5.52 us
    all_to_all x1, starting transfers between devices, per_device(): got = lax.all_to_all(partial, 'tp', split_axis=0, concat_axis=0, tiled=True)  4.97 us
    dot_general x1, matrix products, per_device(): jnp.einsum('rd,dhc->hrc', image_rows, kv_weight, preferred_element_type=j...  4.72 us
    dynamic_slice x1, local copies, waits for them, and re-layouts, per_device(): own_weight = lax.dynamic_index_in_dim(kv_weight, me, axis=1, keepdims=False)  4.54 us
    unnamed x15, local copies, waits for them, and re-layouts  4.39 us
  transfers between devices with their start and end apart: 2, of which 2 were waited for; matrix products, arithmetic and copies ran while one was open for 9% of the time, Pallas kernels for 0%

profile of v6, /device:TPU:1, one launch (start us, length us, event | category | flops | bytes accessed | tf_op | source)
XLA Modules:
  0.0 86.6 jit_solution(2319008792305820078)
XLA Ops:
  0.0 1.4 %copy-done = bf16[512,1536]{1,0:T(8,128)(2,1)S(1)} copy-done((bf16[512,1536]{1,0:T(8,128)(2,1)S(1)}, bf16[512,1536]{1,0:T(8,128)(2,1)}, u32[]{:S(2)}) %copy-start) | copy-done | bytes 1572888
  1.4 4.7 %fusion.13 = bf16[4,512,256]{1,2,0:T(8,128)(2,1)} fusion(bf16[512,1536]{1,0:T(8,128)(2,1)S(1)} %copy-done, bf16[1536,4,256]{2,1,0:T(4,128)(2,1)} %param.13), kind=kOutput, calls=%fused_computation.16 | convolution fusion | flops 1610612736 | bytes 5767168 | tf_op jit(solution)/shard_map/rd,dhc->hrc/dot_general | solution.py:76
  6.1 5.0 %all-to-all-start = ((bf16[4,512,256]{1,2,0:T(8,128)(2,1)}), bf16[4,512,256]{1,2,0:T(8,128)(2,1)S(1)}, u32[]{:S(2)}, u32[]{:S(2)}) async-start(bf16[4,512,256]{1,2,0:T(8,128)(2,1)} %fusion.13), calls=%async_computation | async-start | bytes 2097152 | tf_op jit(solution)/shard_map/all_to_all | solution.py:77
  11.2 1.2 %reduce-window.6 = s32[64,4,128]{2,0,1:T(8,128)S(1)} reduce-window(s32[64,4,128]{2,0,1:T(8,128)S(1)} %fusion.46, s32[]{:T(128)} %constant.9.clone.1), window={size=1x1x128 pad=0_0x0_0x127_0}, to_apply=%region_0.1 | reduce-window | flops 4161536 | bytes 262148 | tf_op jit(solution)/shard_map/reduce-window
  12.8 1.0 %fusion.20 = bf16[1024,2]{0,1:T(2,128)(2,1)S(1)} fusion(s32[512]{0:T(512)S(1)} %multiply_add_fusion, f32[512,1]{0,1:T(1,128)S(1)} %bitcast.60, f32[512,1]{0,1:T(1,128)S(1)} %bitcast.59), kind=kOutput, calls=%fused_computation.20 | convolution fusion | flops 13110272 | bytes 10240 | tf_op jit(solution)/shard_map/dot_general | solution.py:94
  14.3 4.5 %constant_dynamic-slice_fusion = bf16[1536,1,256]{2,1,0:T(2,128)(2,1)} fusion(bf16[1536,4,256]{2,1,0:T(4,128)(2,1)} %param.13, s32[]{:T(128)S(6)} %select_n.17), kind=kLoop, calls=%fused_computation.71 | loop fusion | bytes 1572868 | tf_op jit(solution)/shard_map/jit(dynamic_index_in_dim)/dynamic_slice | solution.py:78
  18.8 5.5 %all-to-all-done = bf16[4,512,256]{1,2,0:T(8,128)(2,1)S(1)} async-done(((bf16[4,512,256]{1,2,0:T(8,128)(2,1)}), bf16[4,512,256]{1,2,0:T(8,128)(2,1)S(1)}, u32[]{:S(2)}, u32[]{:S(2)}) %all-to-all-start) | async-done | bytes 1048608 | tf_op jit(solution)/shard_map/all_to_all | solution.py:77
  24.6 1.1 %copy-done.1 = bf16[1536,1,256]{2,1,0:T(2,128)(2,1)S(1)} copy-done((bf16[1536,1,256]{2,1,0:T(2,128)(2,1)S(1)}, bf16[1536,1,256]{2,1,0:T(2,128)(2,1)}, u32[]{:S(2)}) %copy-start.1) | copy-done | bytes 786456
  25.8 0.6 fusion.19
  26.4 0.6 fusion.40
  27.0 0.5 fusion.18
  27.8 0.5 broadcast.74
  28.3 1.0 %reduce.4 = bf16[64,4224]{1,0:T(8,128)(2,1)S(1)} reduce(bf16[64,1,4224]{2,0,1:T(8,128)(2,1)S(1)} %fusion.25, bf16[]{:T(256)} %broadcast.74), dimensions={1}, to_apply=%copy.34.reduce_sub_computation | reduce | bytes 1081346 | tf_op jit(solution)/shard_map/all_to_all | solution.py:102
  29.3 1.2 %reshape.73 = bf16[64,2,2112]{2,1,0:T(2,128)(2,1)} reshape(bf16[64,4224]{1,0:T(8,128)(2,1)S(1)} %reduce.4) | data formatting | bytes 1081344
  30.5 14.5 %all-to-all-start.1 = ((bf16[64,2,2112]{2,1,0:T(2,128)(2,1)}), bf16[64,2,2112]{2,1,0:T(2,128)(2,1)S(1)}, u32[]{:S(2)}, u32[]{:S(2)}) async-start(bf16[64,2,2112]{2,1,0:T(2,128)(2,1)} %reshape.73), calls=%async_computation.1 | async-start | bytes 1114112 | tf_op jit(solution)/shard_map/all_to_all | solution.py:102
  45.7 17.4 %all-to-all-done.1 = bf16[64,2,2112]{2,1,0:T(2,128)(2,1)S(1)} async-done(((bf16[64,2,2112]{2,1,0:T(2,128)(2,1)}), bf16[64,2,2112]{2,1,0:T(2,128)(2,1)S(1)}, u32[]{:S(2)}, u32[]{:S(2)}) %all-to-all-start.1) | async-done | bytes 540704 | tf_op jit(solution)/shard_map/all_to_all | solution.py:102
  63.0 0.6 reshape.74
  64.3 0.4 fusion.27
  64.7 0.7 fusion.2
  65.4 1.0 %fusion.8 = bf16[1280,128]{1,0:T(8,128)(2,1)S(1)} fusion(s32[1024]{0:T(1024)S(1)} %fusion.27, bf16[1024,256]{1,0:T(8,128)(2,1)S(1)} %reshape.66), kind=kOutput, calls=%fused_computation.9 | convolution fusion | flops 337018880 | bytes 593920 | tf_op jit(solution)/shard_map/dot_general | solution.py:113
  66.4 1.0 %fusion.9 = bf16[128,1280]{0,1:T(8,128)(2,1)S(1)} fusion(s32[1024]{0:T(1024)S(1)} %fusion.27, bf16[1280,256]{1,0:T(8,128)(2,1)S(1)} %bitcast.57, pred[1280]{0:T(1024)(128)(4,1)S(1)} %fusion.2, bf16[1024,256]{1,0:T(8,128)(2,1)S(1)} %reshape.66), kind=kOutput, calls=%fused_computation.10 | convolution fusion | flops 337182720 | bytes 923648 | tf_op jit(solution)/shard_map/sd,ps->dp/dot_general | solution.py:110
  67.4 0.9 %copy.36.kt_ref = bf16[128,1280]{1,0:T(8,128)(2,1)} copy(bf16[128,1280]{0,1:T(8,128)(2,1)S(1)} %fusion.9) | data formatting | bytes 655360 | tf_op jit(solution)/shard_map/jit(_where)/select_n | solution.py:114
  68.3 1.1 %pad_select_fusion.vx_ref = bf16[1280,256]{1,0:T(8,128)(2,1)} fusion(bf16[1280,128]{1,0:T(8,128)(2,1)S(1)} %slice.64, bf16[1280,128]{1,0:T(8,128)(2,1)S(1)} %fusion.8, pred[1280]{0:T(1024)(128)(4,1)S(1)} %fusion.2), kind=kLoop, calls=%fused_computation.26 | loop fusion | flops 327680 | bytes 1312000 | tf_op jit(solution)/shard_map/jit(_where)/select_n | solution.py:115
  69.4 17.2 %shard_map.73 = bf16[6,1280,128]{2,1,0:T(8,128)(2,1)} custom-call(s32[1]{0:T(128)S(6)} %copy.51.len_ref, bf16[6,1280,128]{2,1,0:T(8,128)(2,1)} %bitcast.55, bf16[128,1280]{1,0:T(8,128)(2,1)} %copy.36.kt_ref, bf16[1280,256]{1,0:T(8,128)(2,1)} %pad_select_fusion.vx_ref), custom_call_target="tpu_custom_call" | custom-call | tf_op jit(solution)/shard_map/pallas_call | solution.py:60
  (32 shorter events, 2.2 us)
Async XLA Ops:
  0.0 1.4 %copy-start = (bf16[512,1536]{1,0:T(8,128)(2,1)S(1)}, bf16[512,1536]{1,0:T(8,128)(2,1)}, u32[]{:S(2)}) copy-start(bf16[512,1536]{1,0:T(8,128)(2,1)} %param.9) | copy-start | bytes 4718596
  6.1 5.0 %copy-start.5 = (s32[512]{0:T(512)S(1)}, s32[512]{0:T(512)}, u32[]{:S(2)}) copy-start(s32[512]{0:T(512)} %param.11) | copy-start | bytes 6148
  6.1 5.0 %copy-start.4 = (s32[512]{0:T(512)S(1)}, s32[512]{0:T(512)}, u32[]{:S(2)}) copy-start(s32[512]{0:T(512)} %param.10) | copy-start | bytes 6148
  6.1 18.2 %all-to-all-start = ((bf16[4,512,256]{1,2,0:T(8,128)(2,1)}), bf16[4,512,256]{1,2,0:T(8,128)(2,1)S(1)}, u32[]{:S(2)}, u32[]{:S(2)}) async-start(bf16[4,512,256]{1,2,0:T(8,128)(2,1)} %fusion.13), calls=%async_computation | async-start | bytes 2097152 | tf_op jit(solution)/shard_map/all_to_all | solution.py:77
  24.3 1.4 %copy-start.1 = (bf16[1536,1,256]{2,1,0:T(2,128)(2,1)S(1)}, bf16[1536,1,256]{2,1,0:T(2,128)(2,1)}, u32[]{:S(2)}) copy-start(bf16[1536,1,256]{2,1,0:T(2,128)(2,1)} %constant_dynamic-slice_fusion) | copy-start | bytes 2359300
  28.3 17.4 %copy-start.2 = (bf16[1,1280,1,256]{3,1,2,0:T(8,128)(2,1)S(1)}, bf16[1,1280,1,256]{3,1,2,0:T(8,128)(2,1)}, u32[]{:S(2)}) copy-start(bf16[1,1280,1,256]{3,1,2,0:T(8,128)(2,1)} %param.8) | copy-start | bytes 1966084
  30.5 32.5 %all-to-all-start.1 = ((bf16[64,2,2112]{2,1,0:T(2,128)(2,1)}), bf16[64,2,2112]{2,1,0:T(2,128)(2,1)S(1)}, u32[]{:S(2)}, u32[]{:S(2)}) async-start(bf16[64,2,2112]{2,1,0:T(2,128)(2,1)} %reshape.73), calls=%async_computation.1 | async-start | bytes 1114112 | tf_op jit(solution)/shard_map/all_to_all | solution.py:102
  64.7 1.7 %copy-start.3 = (bf16[1,1280,1,256]{3,1,2,0:T(8,128)(2,1)S(1)}, bf16[1,1280,1,256]{3,1,2,0:T(8,128)(2,1)}, u32[]{:S(2)}) copy-start(bf16[1,1280,1,256]{3,1,2,0:T(8,128)(2,1)} %param.8) | copy-start | bytes 1966084

commit v7 on v6

--- a/solution.py
+++ b/solution.py
@@ -35,8 +35,9 @@
         scores = jnp.dot(query, kt_ref[:, 0:keys_used], preferred_element_type=jnp.float32)
         query_index = row_start + lax.broadcasted_iota(jnp.int32, (block, 1), 0)
         limit = jnp.minimum(query_index, length - 1)
-        key_index = lax.broadcasted_iota(jnp.int32, (1, keys_used), 1)
-        scores = jnp.where(key_index <= limit, scores, jnp.float32(-1e30))
+        key_index = row_start + lax.broadcasted_iota(jnp.int32, (1, block), 1)
+        diag = jnp.where(key_index <= limit, scores[:, row_start:], jnp.float32(-1e30))
+        scores = jnp.concatenate([scores[:, :row_start], diag], axis=1) if row_start else diag
         highest = jnp.max(scores, axis=-1, keepdims=True)
         weights = jnp.exp((scores - highest) * scale).astype(jnp.bfloat16)
         both = jnp.dot(weights, vx_ref[0:keys_used, :], preferred_element_type=jnp.float32)

time: 87.1 us -> 86.6 us (level)
  no operation moved by 1% of the time
where the time goes in v7:
time: 86.6 us; the launch traced here: 86.1 us
  waiting for transfers between devices  22.9 us (26%)
  starting transfers between devices  19.4 us (22%)
  Pallas kernels  16.7 us (19%)
  local copies, waits for them, and re-layouts  11.9 us (14%)
  matrix products  8.88 us (10%)
  other arithmetic  5.46 us (6%)
    all_to_all x1, waiting for transfers between devices, per_device(): got = lax.all_to_all(packet, 'req', split_axis=0, concat_axis=0, tiled=True)  17.4 us
    pallas_call x1, Pallas kernels, attend(): pl.pallas_call(functools.partial(attention_kernel, block, head_dim), grid...  16.7 us
    all_to_all x1, starting transfers between devices, per_device(): got = lax.all_to_all(packet, 'req', split_axis=0, concat_axis=0, tiled=True)  14.5 us
    all_to_all x1, waiting for transfers between devices, per_device(): got = lax.all_to_all(partial, 'tp', split_axis=0, concat_axis=0, tiled=True)  5.52 us
    all_to_all x1, starting transfers between devices, per_device(): got = lax.all_to_all(partial, 'tp', split_axis=0, concat_axis=0, tiled=True)  4.97 us
    dot_general x1, matrix products, per_device(): jnp.einsum('rd,dhc->hrc', image_rows, kv_weight, preferred_element_type=j...  4.72 us
    dynamic_slice x1, local copies, waits for them, and re-layouts, per_device(): own_weight = lax.dynamic_index_in_dim(kv_weight, me, axis=1, keepdims=False)  4.54 us
    unnamed x15, local copies, waits for them, and re-layouts  4.39 us
  transfers between devices with their start and end apart: 2, of which 2 were waited for; matrix products, arithmetic and copies ran while one was open for 9% of the time, Pallas kernels for 0%

profile of v7, /device:TPU:1, one launch (start us, length us, event | category | flops | bytes accessed | tf_op | source)
XLA Modules:
  0.0 86.1 jit_solution(17481027976486613263)
XLA Ops:
  0.0 1.4 %copy-done = bf16[512,1536]{1,0:T(8,128)(2,1)S(1)} copy-done((bf16[512,1536]{1,0:T(8,128)(2,1)S(1)}, bf16[512,1536]{1,0:T(8,128)(2,1)}, u32[]{:S(2)}) %copy-start) | copy-done | bytes 1572888
  1.4 4.7 %fusion.13 = bf16[4,512,256]{1,2,0:T(8,128)(2,1)} fusion(bf16[512,1536]{1,0:T(8,128)(2,1)S(1)} %copy-done, bf16[1536,4,256]{2,1,0:T(4,128)(2,1)} %param.13), kind=kOutput, calls=%fused_computation.16 | convolution fusion | flops 1610612736 | bytes 5767168 | tf_op jit(solution)/shard_map/rd,dhc->hrc/dot_general | solution.py:77
  6.1 5.0 %all-to-all-start = ((bf16[4,512,256]{1,2,0:T(8,128)(2,1)}), bf16[4,512,256]{1,2,0:T(8,128)(2,1)S(1)}, u32[]{:S(2)}, u32[]{:S(2)}) async-start(bf16[4,512,256]{1,2,0:T(8,128)(2,1)} %fusion.13), calls=%async_computation | async-start | bytes 2097152 | tf_op jit(solution)/shard_map/all_to_all | solution.py:78
  11.2 1.2 %reduce-window.6 = s32[64,4,128]{2,0,1:T(8,128)S(1)} reduce-window(s32[64,4,128]{2,0,1:T(8,128)S(1)} %fusion.46, s32[]{:T(128)} %constant.9.clone.1), window={size=1x1x128 pad=0_0x0_0x127_0}, to_apply=%region_0.1 | reduce-window | flops 4161536 | bytes 262148 | tf_op jit(solution)/shard_map/reduce-window
  12.8 1.0 %fusion.20 = bf16[1024,2]{0,1:T(2,128)(2,1)S(1)} fusion(s32[512]{0:T(512)S(1)} %multiply_add_fusion, f32[512,1]{0,1:T(1,128)S(1)} %bitcast.60, f32[512,1]{0,1:T(1,128)S(1)} %bitcast.59), kind=kOutput, calls=%fused_computation.20 | convolution fusion | flops 13110272 | bytes 10240 | tf_op jit(solution)/shard_map/dot_general | solution.py:95
  14.3 4.5 %constant_dynamic-slice_fusion = bf16[1536,1,256]{2,1,0:T(2,128)(2,1)} fusion(bf16[1536,4,256]{2,1,0:T(4,128)(2,1)} %param.13, s32[]{:T(128)S(6)} %select_n.17), kind=kLoop, calls=%fused_computation.71 | loop fusion | bytes 1572868 | tf_op jit(solution)/shard_map/jit(dynamic_index_in_dim)/dynamic_slice | solution.py:79
  18.8 5.5 %all-to-all-done = bf16[4,512,256]{1,2,0:T(8,128)(2,1)S(1)} async-done(((bf16[4,512,256]{1,2,0:T(8,128)(2,1)}), bf16[4,512,256]{1,2,0:T(8,128)(2,1)S(1)}, u32[]{:S(2)}, u32[]{:S(2)}) %all-to-all-start) | async-done | bytes 1048608 | tf_op jit(solution)/shard_map/all_to_all | solution.py:78
  24.6 1.1 %copy-done.1 = bf16[1536,1,256]{2,1,0:T(2,128)(2,1)S(1)} copy-done((bf16[1536,1,256]{2,1,0:T(2,128)(2,1)S(1)}, bf16[1536,1,256]{2,1,0:T(2,128)(2,1)}, u32[]{:S(2)}) %copy-start.1) | copy-done | bytes 786456
  25.8 0.6 fusion.19
  26.4 0.6 fusion.40
  27.0 0.5 fusion.18
  27.8 0.5 broadcast.74
  28.3 1.0 %reduce.4 = bf16[64,4224]{1,0:T(8,128)(2,1)S(1)} reduce(bf16[64,1,4224]{2,0,1:T(8,128)(2,1)S(1)} %fusion.25, bf16[]{:T(256)} %broadcast.74), dimensions={1}, to_apply=%copy.34.reduce_sub_computation | reduce | bytes 1081346 | tf_op jit(solution)/shard_map/all_to_all | solution.py:103
  29.3 1.2 %reshape.73 = bf16[64,2,2112]{2,1,0:T(2,128)(2,1)} reshape(bf16[64,4224]{1,0:T(8,128)(2,1)S(1)} %reduce.4) | data formatting | bytes 1081344
  30.5 14.5 %all-to-all-start.1 = ((bf16[64,2,2112]{2,1,0:T(2,128)(2,1)}), bf16[64,2,2112]{2,1,0:T(2,128)(2,1)S(1)}, u32[]{:S(2)}, u32[]{:S(2)}) async-start(bf16[64,2,2112]{2,1,0:T(2,128)(2,1)} %reshape.73), calls=%async_computation.1 | async-start | bytes 1114112 | tf_op jit(solution)/shard_map/all_to_all | solution.py:103
  45.7 17.4 %all-to-all-done.1 = bf16[64,2,2112]{2,1,0:T(2,128)(2,1)S(1)} async-done(((bf16[64,2,2112]{2,1,0:T(2,128)(2,1)}), bf16[64,2,2112]{2,1,0:T(2,128)(2,1)S(1)}, u32[]{:S(2)}, u32[]{:S(2)}) %all-to-all-start.1) | async-done | bytes 540704 | tf_op jit(solution)/shard_map/all_to_all | solution.py:103
  63.0 0.6 reshape.74
  64.3 0.4 fusion.27
  64.7 0.7 fusion.2
  65.4 1.0 %fusion.8 = bf16[1280,128]{1,0:T(8,128)(2,1)S(1)} fusion(s32[1024]{0:T(1024)S(1)} %fusion.27, bf16[1024,256]{1,0:T(8,128)(2,1)S(1)} %reshape.66), kind=kOutput, calls=%fused_computation.9 | convolution fusion | flops 337018880 | bytes 593920 | tf_op jit(solution)/shard_map/dot_general | solution.py:114
  66.4 1.0 %fusion.9 = bf16[128,1280]{0,1:T(8,128)(2,1)S(1)} fusion(s32[1024]{0:T(1024)S(1)} %fusion.27, bf16[1280,256]{1,0:T(8,128)(2,1)S(1)} %bitcast.57, pred[1280]{0:T(1024)(128)(4,1)S(1)} %fusion.2, bf16[1024,256]{1,0:T(8,128)(2,1)S(1)} %reshape.66), kind=kOutput, calls=%fused_computation.10 | convolution fusion | flops 337182720 | bytes 923648 | tf_op jit(solution)/shard_map/sd,ps->dp/dot_general | solution.py:111
  67.4 0.9 %copy.36.kt_ref = bf16[128,1280]{1,0:T(8,128)(2,1)} copy(bf16[128,1280]{0,1:T(8,128)(2,1)S(1)} %fusion.9) | data formatting | bytes 655360 | tf_op jit(solution)/shard_map/jit(_where)/select_n | solution.py:115
  68.3 1.1 %pad_select_fusion.vx_ref = bf16[1280,256]{1,0:T(8,128)(2,1)} fusion(bf16[1280,128]{1,0:T(8,128)(2,1)S(1)} %slice.64, bf16[1280,128]{1,0:T(8,128)(2,1)S(1)} %fusion.8, pred[1280]{0:T(1024)(128)(4,1)S(1)} %fusion.2), kind=kLoop, calls=%fused_computation.26 | loop fusion | flops 327680 | bytes 1312000 | tf_op jit(solution)/shard_map/jit(_where)/select_n | solution.py:116
  69.4 16.7 %shard_map.73 = bf16[6,1280,128]{2,1,0:T(8,128)(2,1)} custom-call(s32[1]{0:T(128)S(6)} %copy.51.len_ref, bf16[6,1280,128]{2,1,0:T(8,128)(2,1)} %bitcast.55, bf16[128,1280]{1,0:T(8,128)(2,1)} %copy.36.kt_ref, bf16[1280,256]{1,0:T(8,128)(2,1)} %pad_select_fusion.vx_ref), custom_call_target="tpu_custom_call" | custom-call | tf_op jit(solution)/shard_map/pallas_call | solution.py:61
  (32 shorter events, 2.2 us)
Async XLA Ops:
  0.0 1.4 %copy-start = (bf16[512,1536]{1,0:T(8,128)(2,1)S(1)}, bf16[512,1536]{1,0:T(8,128)(2,1)}, u32[]{:S(2)}) copy-start(bf16[512,1536]{1,0:T(8,128)(2,1)} %param.9) | copy-start | bytes 4718596
  6.1 5.0 %copy-start.5 = (s32[512]{0:T(512)S(1)}, s32[512]{0:T(512)}, u32[]{:S(2)}) copy-start(s32[512]{0:T(512)} %param.11) | copy-start | bytes 6148
  6.1 5.0 %copy-start.4 = (s32[512]{0:T(512)S(1)}, s32[512]{0:T(512)}, u32[]{:S(2)}) copy-start(s32[512]{0:T(512)} %param.10) | copy-start | bytes 6148
  6.1 18.2 %all-to-all-start = ((bf16[4,512,256]{1,2,0:T(8,128)(2,1)}), bf16[4,512,256]{1,2,0:T(8,128)(2,1)S(1)}, u32[]{:S(2)}, u32[]{:S(2)}) async-start(bf16[4,512,256]{1,2,0:T(8,128)(2,1)} %fusion.13), calls=%async_computation | async-start | bytes 2097152 | tf_op jit(solution)/shard_map/all_to_all | solution.py:78
  24.3 1.4 %copy-start.1 = (bf16[1536,1,256]{2,1,0:T(2,128)(2,1)S(1)}, bf16[1536,1,256]{2,1,0:T(2,128)(2,1)}, u32[]{:S(2)}) copy-start(bf16[1536,1,256]{2,1,0:T(2,128)(2,1)} %constant_dynamic-slice_fusion) | copy-start | bytes 2359300
  28.3 17.4 %copy-start.2 = (bf16[1,1280,1,256]{3,1,2,0:T(8,128)(2,1)S(1)}, bf16[1,1280,1,256]{3,1,2,0:T(8,128)(2,1)}, u32[]{:S(2)}) copy-start(bf16[1,1280,1,256]{3,1,2,0:T(8,128)(2,1)} %param.8) | copy-start | bytes 1966084
  30.5 32.5 %all-to-all-start.1 = ((bf16[64,2,2112]{2,1,0:T(2,128)(2,1)}), bf16[64,2,2112]{2,1,0:T(2,128)(2,1)S(1)}, u32[]{:S(2)}, u32[]{:S(2)}) async-start(bf16[64,2,2112]{2,1,0:T(2,128)(2,1)} %reshape.73), calls=%async_computation.1 | async-start | bytes 1114112 | tf_op jit(solution)/shard_map/all_to_all | solution.py:103
  64.7 1.7 %copy-start.3 = (bf16[1,1280,1,256]{3,1,2,0:T(8,128)(2,1)S(1)}, bf16[1,1280,1,256]{3,1,2,0:T(8,128)(2,1)}, u32[]{:S(2)}) copy-start(bf16[1,1280,1,256]{3,1,2,0:T(8,128)(2,1)} %param.8) | copy-start | bytes 1966084

commit v8 on v7

--- a/solution.py
+++ b/solution.py
@@ -75,11 +75,15 @@
     width = 2 * head_dim
     me = lax.axis_index("tp")
     partial = jnp.einsum("rd,dhc->hrc", image_rows, kv_weight, preferred_element_type=jnp.bfloat16)
-    got = lax.all_to_all(partial, "tp", split_axis=0, concat_axis=0, tiled=True)
+    heads = partial.shape[0]
     own_weight = lax.dynamic_index_in_dim(kv_weight, me, axis=1, keepdims=False)
-    own = jnp.dot(image_rows, own_weight, preferred_element_type=jnp.float32)
-    others = jnp.arange(partial.shape[0], dtype=jnp.int32)[:, None, None] != me
-    summed = jnp.sum(jnp.where(others, got.astype(jnp.float32), 0.0), axis=0) + own
+    summed = jnp.dot(image_rows, own_weight, preferred_element_type=jnp.float32)
+    for shift in range(1, heads):
+        outgoing = lax.dynamic_index_in_dim(partial, (me + shift) % heads, axis=0, keepdims=False)
+        incoming = lax.ppermute(
+            outgoing, "tp", perm=[(i, (i + shift) % heads) for i in range(heads)]
+        )
+        summed = summed + incoming.astype(jnp.float32)
     image_kv = rotate_keys(summed, row_position, head_dim)
     one_hot = (row_request[:, None] == jnp.arange(groups, dtype=jnp.int32)[None, :]).astype(
         jnp.int32

time: 86.6 us -> 80.6 us (0.931)
  waiting for transfers between devices: 22.9 us -> 20.8 us
  local copies, waits for them, and re-layouts: 11.9 us -> 9.9 us
  matrix products: 8.88 us -> 7.93 us
    ppermute x0 -> x3, starting transfers between devices: none -> 5.72 us  [per_device(): lax.ppermute(outgoing, 'tp', perm=[(i, (i + shift) % heads) for i in rang...]
    all_to_all x1 -> x0, waiting for transfers between devices: 5.52 us -> none  [per_device(): got = lax.all_to_all(partial, 'tp', split_axis=0, concat_axis=0, tiled=True)]
    all_to_all x1 -> x0, starting transfers between devices: 4.97 us -> none  [per_device(): got = lax.all_to_all(partial, 'tp', split_axis=0, concat_axis=0, tiled=True)]
    ppermute x0 -> x3, waiting for transfers between devices: none -> 3.43 us  [per_device(): lax.ppermute(outgoing, 'tp', perm=[(i, (i + shift) % heads) for i in rang...]
    all_to_all x1, starting transfers between devices: 14.5 us -> 13.2 us  [per_device(): got = lax.all_to_all(packet, 'req', split_axis=0, concat_axis=0, tiled=True)]
    unnamed x15 -> x13, local copies, waits for them, and re-layouts: 4.39 us -> 3.28 us
    dot_general x1, matrix products: 4.72 us -> 3.72 us  [per_device(): jnp.einsum('rd,dhc->hrc', image_rows, kv_weight, preferred_element_type=j...]
    dynamic_slice x1, local copies, waits for them, and re-layouts: 4.54 us -> 3.57 us  [per_device(): own_weight = lax.dynamic_index_in_dim(kv_weight, me, axis=1, keepdims=False)]
  transfers between devices with their start and end apart: 2 -> 4, of which waited for: 2 -> 2; matrix products, arithmetic and copies ran while one was open for 9% -> 8% of each run, Pallas kernels for 0% -> 0%
where the time goes in v8:
time: 80.6 us; the launch traced here: 80.3 us
  waiting for transfers between devices  20.8 us (26%)
  starting transfers between devices  18.9 us (23%)
  Pallas kernels  16.7 us (21%)
  local copies, waits for them, and re-layouts  9.9 us (12%)
  matrix products  7.93 us (10%)
  other arithmetic  5.16 us (6%)
  between operations  0.89 us (1%)
    all_to_all x1, waiting for transfers between devices, per_device(): got = lax.all_to_all(packet, 'req', split_axis=0, concat_axis=0, tiled=True)  17.4 us
    pallas_call x1, Pallas kernels, attend(): pl.pallas_call(functools.partial(attention_kernel, block, head_dim), grid...  16.7 us
    all_to_all x1, starting transfers between devices, per_device(): got = lax.all_to_all(packet, 'req', split_axis=0, concat_axis=0, tiled=True)  13.2 us
    ppermute x3, starting transfers between devices, per_device(): lax.ppermute(outgoing, 'tp', perm=[(i, (i + shift) % heads) for i in rang...  5.72 us
    dot_general x1, matrix products, per_device(): jnp.einsum('rd,dhc->hrc', image_rows, kv_weight, preferred_element_type=j...  3.72 us
    dynamic_slice x1, local copies, waits for them, and re-layouts, per_device(): own_weight = lax.dynamic_index_in_dim(kv_weight, me, axis=1, keepdims=False)  3.57 us
    ppermute x3, waiting for transfers between devices, per_device(): lax.ppermute(outgoing, 'tp', perm=[(i, (i + shift) % heads) for i in rang...  3.43 us
    unnamed x13, local copies, waits for them, and re-layouts  3.28 us
  transfers between devices with their start and end apart: 4, of which 2 were waited for; matrix products, arithmetic and copies ran while one was open for 8% of the time, Pallas kernels for 0%

profile of v8, /device:TPU:1, one launch (start us, length us, event | category | flops | bytes accessed | tf_op | source)
XLA Modules:
  0.0 80.3 jit_solution(9236273888772226841)
XLA Ops:
  0.0 1.4 %copy-done = bf16[512,1536]{1,0:T(8,128)(2,1)S(1)} copy-done((bf16[512,1536]{1,0:T(8,128)(2,1)S(1)}, bf16[512,1536]{1,0:T(8,128)(2,1)}, u32[]{:S(2)}) %copy-start) | copy-done | bytes 1572888
  1.4 3.7 %fusion.3 = bf16[4,256,512]{2,1,0:T(8,128)(2,1)S(1)} fusion(bf16[1536,4,256]{2,1,0:T(4,128)(2,1)} %param.13, bf16[512,1536]{1,0:T(8,128)(2,1)S(1)} %copy-done), kind=kOutput, calls=%fused_computation.4 | convolution fusion | flops 1610612736 | bytes 5767168 | tf_op jit(solution)/shard_map/rd,dhc->hrc/dot_general | solution.py:77
  5.2 2.1 %collective-permute-start = (bf16[512,256]{0,1:T(8,128)(2,1)S(1)}, bf16[512,256]{0,1:T(8,128)(2,1)S(1)}, u32[]{:S(2)}, u32[]{:S(2)}) collective-permute-start(bf16[512,256]{0,1:T(8,128)(2,1)S(1)} %get-tuple-element.5), channel_id=1, source_target_pairs={{0,1},{1,2},{2,3},{3,0},{4,5},{5,6},{6,7},{7,4},{8,9},{9,10},{10,1... | collective-permute-start | bytes 786440 | tf_op jit(solution)/shard_map/ppermute | solution.py:83
  7.4 2.5 %collective-permute-start.1 = (bf16[512,256]{0,1:T(8,128)(2,1)S(1)}, bf16[512,256]{0,1:T(8,128)(2,1)S(1)}, u32[]{:S(2)}, u32[]{:S(2)}) collective-permute-start(bf16[512,256]{0,1:T(8,128)(2,1)S(1)} %get-tuple-element.7), channel_id=1, source_target_pairs={{0,2},{1,3},{2,0},{3,1},{4,6},{5,7},{6,4},{7,5},{8,10},{9,11},{10,... | collective-permute-start | bytes 786440 | tf_op jit(solution)/shard_map/ppermute | solution.py:83
  9.8 1.2 %collective-permute-start.2 = (bf16[512,256]{0,1:T(8,128)(2,1)S(1)}, bf16[512,256]{0,1:T(8,128)(2,1)S(1)}, u32[]{:S(2)}, u32[]{:S(2)}) collective-permute-start(bf16[512,256]{0,1:T(8,128)(2,1)S(1)} %get-tuple-element.6), channel_id=1, source_target_pairs={{0,3},{1,0},{2,1},{3,2},{4,7},{5,4},{6,5},{7,6},{8,11},{9,8},{10,9... | collective-permute-start | bytes 786440 | tf_op jit(solution)/shard_map/ppermute | solution.py:83
  11.0 1.2 %reduce-window.6 = s32[64,4,128]{2,0,1:T(8,128)S(1)} reduce-window(s32[64,4,128]{2,0,1:T(8,128)S(1)} %fusion.40, s32[]{:T(128)} %constant.53.clone.1), window={size=1x1x128 pad=0_0x0_0x127_0}, to_apply=%region_0.1 | reduce-window | flops 4161536 | bytes 262148 | tf_op jit(solution)/shard_map/reduce-window
  12.6 1.0 %fusion.14 = bf16[1024,2]{0,1:T(2,128)(2,1)S(1)} fusion(s32[512]{0:T(512)S(1)} %multiply_add_fusion, f32[512,1]{0,1:T(1,128)S(1)} %bitcast.68, f32[512,1]{0,1:T(1,128)S(1)} %bitcast.67), kind=kOutput, calls=%fused_computation.17 | convolution fusion | flops 13110272 | bytes 10240 | tf_op jit(solution)/shard_map/dot_general | solution.py:99
  14.1 3.6 %constant_dynamic-slice_fusion = bf16[1536,1,256]{2,1,0:T(2,128)(2,1)S(1)} fusion(bf16[1536,4,256]{2,1,0:T(4,128)(2,1)} %param.13, s32[]{:T(128)S(6)} %select_n.37), kind=kLoop, calls=%fused_computation.70 | loop fusion | bytes 1572868 | tf_op jit(solution)/shard_map/jit(dynamic_index_in_dim)/dynamic_slice | solution.py:79
  17.7 3.4 %collective-permute-done.1 = bf16[512,256]{0,1:T(8,128)(2,1)S(1)} collective-permute-done((bf16[512,256]{0,1:T(8,128)(2,1)S(1)}, bf16[512,256]{0,1:T(8,128)(2,1)S(1)}, u32[]{:S(2)}, u32[]{:S(2)}) %collective-permute-start.1) | collective-permute-done | bytes 262176 | tf_op jit(solution)/shard_map/ppermute | solution.py:83
  21.1 0.7 convert_add_fusion
  21.8 0.6 fusion.34
  22.4 0.5 fusion.13
  23.2 0.5 broadcast.72
  23.7 1.0 %reduce.4 = bf16[64,4224]{1,0:T(8,128)(2,1)S(1)} reduce(bf16[64,1,4224]{2,0,1:T(8,128)(2,1)S(1)} %fusion.19, bf16[]{:T(256)} %broadcast.72), dimensions={1}, to_apply=%copy.34.reduce_sub_computation | reduce | bytes 1081346 | tf_op jit(solution)/shard_map/all_to_all | solution.py:107
  24.8 1.2 %reshape.68 = bf16[64,2,2112]{2,1,0:T(2,128)(2,1)} reshape(bf16[64,4224]{1,0:T(8,128)(2,1)S(1)} %reduce.4) | data formatting | bytes 1081344
  26.0 13.2 %all-to-all-start = ((bf16[64,2,2112]{2,1,0:T(2,128)(2,1)}), bf16[64,2,2112]{2,1,0:T(2,128)(2,1)S(1)}, u32[]{:S(2)}, u32[]{:S(2)}) async-start(bf16[64,2,2112]{2,1,0:T(2,128)(2,1)} %reshape.68), calls=%async_computation | async-start | bytes 1114112 | tf_op jit(solution)/shard_map/all_to_all | solution.py:107
  39.9 17.4 %all-to-all-done = bf16[64,2,2112]{2,1,0:T(2,128)(2,1)S(1)} async-done(((bf16[64,2,2112]{2,1,0:T(2,128)(2,1)}), bf16[64,2,2112]{2,1,0:T(2,128)(2,1)S(1)}, u32[]{:S(2)}, u32[]{:S(2)}) %all-to-all-start) | async-done | bytes 540704 | tf_op jit(solution)/shard_map/all_to_all | solution.py:107
  57.2 0.6 reshape.69
  58.9 0.7 fusion.2
  59.6 1.0 %fusion.8 = bf16[1280,128]{1,0:T(8,128)(2,1)S(1)} fusion(s32[1024]{0:T(1024)S(1)} %fusion.21, bf16[1024,256]{1,0:T(8,128)(2,1)S(1)} %reshape.61), kind=kOutput, calls=%fused_computation.9 | convolution fusion | flops 337018880 | bytes 593920 | tf_op jit(solution)/shard_map/dot_general | solution.py:118
  60.6 1.0 %fusion.9 = bf16[128,1280]{0,1:T(8,128)(2,1)S(1)} fusion(s32[1024]{0:T(1024)S(1)} %fusion.21, bf16[1280,256]{1,0:T(8,128)(2,1)S(1)} %bitcast.65, pred[1280]{0:T(1024)(128)(4,1)S(1)} %fusion.2, bf16[1024,256]{1,0:T(8,128)(2,1)S(1)} %reshape.61), kind=kOutput, calls=%fused_computation.10 | convolution fusion | flops 337182720 | bytes 923648 | tf_op jit(solution)/shard_map/sd,ps->dp/dot_general | solution.py:115
  61.6 0.9 %copy.36.kt_ref = bf16[128,1280]{1,0:T(8,128)(2,1)} copy(bf16[128,1280]{0,1:T(8,128)(2,1)S(1)} %fusion.9) | data formatting | bytes 655360 | tf_op jit(solution)/shard_map/jit(_where)/select_n | solution.py:119
  62.5 1.1 %pad_select_fusion.vx_ref = bf16[1280,256]{1,0:T(8,128)(2,1)} fusion(bf16[1280,128]{1,0:T(8,128)(2,1)S(1)} %slice.64, bf16[1280,128]{1,0:T(8,128)(2,1)S(1)} %fusion.8, pred[1280]{0:T(1024)(128)(4,1)S(1)} %fusion.2), kind=kLoop, calls=%fused_computation.23 | loop fusion | flops 327680 | bytes 1312000 | tf_op jit(solution)/shard_map/jit(_where)/select_n | solution.py:120
  63.6 16.7 %shard_map.73 = bf16[6,1280,128]{2,1,0:T(8,128)(2,1)} custom-call(s32[1]{0:T(128)S(6)} %copy.51.len_ref, bf16[6,1280,128]{2,1,0:T(8,128)(2,1)} %bitcast.63, bf16[128,1280]{1,0:T(8,128)(2,1)} %copy.36.kt_ref, bf16[1280,256]{1,0:T(8,128)(2,1)} %pad_select_fusion.vx_ref), custom_call_target="tpu_custom_call" | custom-call | tf_op jit(solution)/shard_map/pallas_call | solution.py:61
  (33 shorter events, 2.3 us)
Async XLA Ops:
  0.0 1.4 %copy-start = (bf16[512,1536]{1,0:T(8,128)(2,1)S(1)}, bf16[512,1536]{1,0:T(8,128)(2,1)}, u32[]{:S(2)}) copy-start(bf16[512,1536]{1,0:T(8,128)(2,1)} %param.9) | copy-start | bytes 4718596
  5.1 5.8 %copy-start.4 = (s32[512]{0:T(512)S(1)}, s32[512]{0:T(512)}, u32[]{:S(2)}) copy-start(s32[512]{0:T(512)} %param.11) | copy-start | bytes 6148
  5.2 5.8 %copy-start.3 = (s32[512]{0:T(512)S(1)}, s32[512]{0:T(512)}, u32[]{:S(2)}) copy-start(s32[512]{0:T(512)} %param.10) | copy-start | bytes 6148
  5.2 12.5 %collective-permute-start = (bf16[512,256]{0,1:T(8,128)(2,1)S(1)}, bf16[512,256]{0,1:T(8,128)(2,1)S(1)}, u32[]{:S(2)}, u32[]{:S(2)}) collective-permute-start(bf16[512,256]{0,1:T(8,128)(2,1)S(1)} %get-tuple-element.5), channel_id=1, source_target_pairs={{0,1},{1,2},{2,3},{3,0},{4,5},{5,6},{6,7},{7,4},{8,9},{9,10},{10,1... | collective-permute-start | bytes 786440 | tf_op jit(solution)/shard_map/ppermute | solution.py:83
  7.4 13.8 %collective-permute-start.1 = (bf16[512,256]{0,1:T(8,128)(2,1)S(1)}, bf16[512,256]{0,1:T(8,128)(2,1)S(1)}, u32[]{:S(2)}, u32[]{:S(2)}) collective-permute-start(bf16[512,256]{0,1:T(8,128)(2,1)S(1)} %get-tuple-element.7), channel_id=1, source_target_pairs={{0,2},{1,3},{2,0},{3,1},{4,6},{5,7},{6,4},{7,5},{8,10},{9,11},{10,... | collective-permute-start | bytes 786440 | tf_op jit(solution)/shard_map/ppermute | solution.py:83
  9.8 11.3 %collective-permute-start.2 = (bf16[512,256]{0,1:T(8,128)(2,1)S(1)}, bf16[512,256]{0,1:T(8,128)(2,1)S(1)}, u32[]{:S(2)}, u32[]{:S(2)}) collective-permute-start(bf16[512,256]{0,1:T(8,128)(2,1)S(1)} %get-tuple-element.6), channel_id=1, source_target_pairs={{0,3},{1,0},{2,1},{3,2},{4,7},{5,4},{6,5},{7,6},{8,11},{9,8},{10,9... | collective-permute-start | bytes 786440 | tf_op jit(solution)/shard_map/ppermute | solution.py:83
  23.7 15.4 %copy-start.1 = (bf16[1,1280,1,256]{3,1,2,0:T(8,128)(2,1)S(1)}, bf16[1,1280,1,256]{3,1,2,0:T(8,128)(2,1)}, u32[]{:S(2)}) copy-start(bf16[1,1280,1,256]{3,1,2,0:T(8,128)(2,1)} %param.8) | copy-start | bytes 1966084
  26.0 31.3 %all-to-all-start = ((bf16[64,2,2112]{2,1,0:T(2,128)(2,1)}), bf16[64,2,2112]{2,1,0:T(2,128)(2,1)S(1)}, u32[]{:S(2)}, u32[]{:S(2)}) async-start(bf16[64,2,2112]{2,1,0:T(2,128)(2,1)} %reshape.68), calls=%async_computation | async-start | bytes 1114112 | tf_op jit(solution)/shard_map/all_to_all | solution.py:107
  58.9 1.7 %copy-start.2 = (bf16[1,1280,1,256]{3,1,2,0:T(8,128)(2,1)S(1)}, bf16[1,1280,1,256]{3,1,2,0:T(8,128)(2,1)}, u32[]{:S(2)}) copy-start(bf16[1,1280,1,256]{3,1,2,0:T(8,128)(2,1)} %param.8) | copy-start | bytes 1966084

commit v9 on v8

--- a/solution.py
+++ b/solution.py
@@ -66,6 +66,40 @@
     )(length, heads_first, keys_t, values_ext)
 
 
+def torus_factors(groups):
+    cores = 2 if groups % 2 == 0 else 1
+    rows = 4 if (groups // cores) % 4 == 0 else 1
+    return rows, groups // (rows * cores), cores
+
+
+def staged_exchange(packet, factors):
+    ny, nz, nc = factors
+    groups = ny * nz * nc
+    width = packet.shape[1]
+
+    def shifted(axis, step):
+        pairs = []
+        for i in range(groups):
+            coord = [i // (nz * nc), (i // nc) % nz, i % nc]
+            coord[axis] = (coord[axis] + step) % factors[axis]
+            pairs.append((i, (coord[0] * nz + coord[1]) * nc + coord[2]))
+        return pairs
+
+    buf = packet.reshape(ny, nz, nc, width)
+    pieces = [buf[:, :, 0]]
+    for step in range(1, nc):
+        pieces.append(lax.ppermute(buf[:, :, step], "req", perm=shifted(2, step)))
+    buf = jnp.stack(pieces, axis=2)
+    pieces = [buf[:, 0]]
+    for step in range(1, nz):
+        pieces.append(lax.ppermute(buf[:, step], "req", perm=shifted(1, step)))
+    buf = jnp.stack(pieces, axis=1)
+    pieces = [buf[0]]
+    for step in range(1, ny):
+        pieces.append(lax.ppermute(buf[step], "req", perm=shifted(0, step)))
+    return jnp.stack(pieces, axis=0).reshape(groups, width)
+
+
 def per_device(queries, text_kv, image_rows, row_request, row_position, prompt_lengths, kv_weight):
     groups = lax.axis_size("req")
     own_rows = image_rows.shape[0]
@@ -90,7 +124,14 @@
     )
     before = jnp.cumsum(one_hot, axis=0) - one_hot
     slot_index = jnp.sum(before * one_hot, axis=1)
-    target = row_request * capacity + slot_index
+    ny, nz, nc = factors = torus_factors(groups)
+    here = lax.axis_index("req")
+    relative = (
+        ((row_request // (nz * nc) - here // (nz * nc)) % ny * nz
+         + (row_request // nc - here // nc) % nz) * nc
+        + (row_request - here) % nc
+    )
+    target = relative * capacity + slot_index
     slots = groups * capacity
     pick = (target[None, :] == jnp.arange(slots, dtype=jnp.int32)[:, None]).astype(jnp.bfloat16)
     send_kv = jnp.dot(pick, image_kv, preferred_element_type=jnp.float32).astype(jnp.bfloat16)
@@ -104,7 +145,7 @@
     text_keys_t = jnp.transpose(text[:, :head_dim])
     ones = jnp.ones((prompt, head_dim), text.dtype)
     text_values_ext = jnp.concatenate([text[:, head_dim:], ones], axis=1)
-    got = lax.all_to_all(packet, "req", split_axis=0, concat_axis=0, tiled=True)
+    got = staged_exchange(packet, factors)
     got_kv = got[:, : capacity * width].reshape(slots, width)
     got_digits = got[:, capacity * width : capacity * width + 2 * capacity].astype(jnp.int32)
     got_digits = got_digits.reshape(slots, 2)

time: 80.6 us -> 87.9 us (1.091)
  the two profiles are of different devices: /device:TPU:1 before, /device:TPU:32 now
where the time goes in v9:
time: 87.9 us; the launch traced here: 87.7 us
  starting transfers between devices  29.9 us (34%)
  Pallas kernels  16.7 us (19%)
  waiting for transfers between devices  14.5 us (16%)
  local copies, waits for them, and re-layouts  12.4 us (14%)
  matrix products  7.96 us (9%)
  other arithmetic  5.19 us (6%)
  between operations  1.04 us (1%)
    ppermute x7, starting transfers between devices, staged_exchange(): pieces.append(lax.ppermute(buf[:, step], 'req', perm=shifted(1, step)))  18.1 us
    pallas_call x1, Pallas kernels, attend(): pl.pallas_call(functools.partial(attention_kernel, block, head_dim), grid...  16.7 us
    ppermute x7, waiting for transfers between devices, staged_exchange(): pieces.append(lax.ppermute(buf[:, step], 'req', perm=shifted(1, step)))  6.24 us
    ppermute x3, starting transfers between devices, staged_exchange(): pieces.append(lax.ppermute(buf[step], 'req', perm=shifted(0, step)))  5.9 us
    ppermute x3, starting transfers between devices, per_device(): lax.ppermute(outgoing, 'tp', perm=[(i, (i + shift) % heads) for i in rang...  5.74 us
    dot_general x1, matrix products, per_device(): jnp.einsum('rd,dhc->hrc', image_rows, kv_weight, preferred_element_type=j...  3.75 us
    dynamic_slice x1, local copies, waits for them, and re-layouts, per_device(): own_weight = lax.dynamic_index_in_dim(kv_weight, me, axis=1, keepdims=False)  3.57 us
    ppermute x3, waiting for transfers between devices, per_device(): lax.ppermute(outgoing, 'tp', perm=[(i, (i + shift) % heads) for i in rang...  3.39 us
  transfers between devices with their start and end apart: 14, of which 6 were waited for; matrix products, arithmetic and copies ran while one was open for 10% of the time, Pallas kernels for 0%

profile of v9, /device:TPU:32, one launch (start us, length us, event | category | flops | bytes accessed | tf_op | source)
XLA Modules:
  0.0 87.7 jit_solution(8235667771981308840)
XLA Ops:
  0.0 1.4 %copy-done = bf16[512,1536]{1,0:T(8,128)(2,1)S(1)} copy-done((bf16[512,1536]{1,0:T(8,128)(2,1)S(1)}, bf16[512,1536]{1,0:T(8,128)(2,1)}, u32[]{:S(2)}) %copy-start) | copy-done | bytes 1572888
  1.4 3.7 %fusion.3 = bf16[4,256,512]{2,1,0:T(8,128)(2,1)S(1)} fusion(bf16[1536,4,256]{2,1,0:T(4,128)(2,1)} %param.13, bf16[512,1536]{1,0:T(8,128)(2,1)S(1)} %copy-done), kind=kOutput, calls=%fused_computation.4 | convolution fusion | flops 1610612736 | bytes 5767168 | tf_op jit(solution)/shard_map/rd,dhc->hrc/dot_general | solution.py:111
  5.2 1.6 %collective-permute-start = (bf16[512,256]{0,1:T(8,128)(2,1)S(1)}, bf16[512,256]{0,1:T(8,128)(2,1)S(1)}, u32[]{:S(2)}, u32[]{:S(2)}) collective-permute-start(bf16[512,256]{0,1:T(8,128)(2,1)S(1)} %get-tuple-element.5), channel_id=1, source_target_pairs={{0,1},{1,2},{2,3},{3,0},{4,5},{5,6},{6,7},{7,4},{8,9},{9,10},{10,1... | collective-permute-start | bytes 786440 | tf_op jit(solution)/shard_map/ppermute | solution.py:117
  6.8 2.7 %collective-permute-start.1 = (bf16[512,256]{0,1:T(8,128)(2,1)S(1)}, bf16[512,256]{0,1:T(8,128)(2,1)S(1)}, u32[]{:S(2)}, u32[]{:S(2)}) collective-permute-start(bf16[512,256]{0,1:T(8,128)(2,1)S(1)} %get-tuple-element.7), channel_id=1, source_target_pairs={{0,2},{1,3},{2,0},{3,1},{4,6},{5,7},{6,4},{7,5},{8,10},{9,11},{10,... | collective-permute-start | bytes 786440 | tf_op jit(solution)/shard_map/ppermute | solution.py:117
  9.5 1.4 %collective-permute-start.2 = (bf16[512,256]{0,1:T(8,128)(2,1)S(1)}, bf16[512,256]{0,1:T(8,128)(2,1)S(1)}, u32[]{:S(2)}, u32[]{:S(2)}) collective-permute-start(bf16[512,256]{0,1:T(8,128)(2,1)S(1)} %get-tuple-element.6), channel_id=1, source_target_pairs={{0,3},{1,0},{2,1},{3,2},{4,7},{5,4},{6,5},{7,6},{8,11},{9,8},{10,9... | collective-permute-start | bytes 786440 | tf_op jit(solution)/shard_map/ppermute | solution.py:117
  11.0 1.2 %reduce-window.6 = s32[64,4,128]{2,0,1:T(8,128)S(1)} reduce-window(s32[64,4,128]{2,0,1:T(8,128)S(1)} %fusion.44, s32[]{:T(128)} %constant.118.clone.1), window={size=1x1x128 pad=0_0x0_0x127_0}, to_apply=%region_0.1 | reduce-window | flops 4161536 | bytes 262148 | tf_op jit(solution)/shard_map/reduce-window
  14.2 3.6 %constant_dynamic-slice_fusion = bf16[1536,1,256]{2,1,0:T(2,128)(2,1)S(1)} fusion(bf16[1536,4,256]{2,1,0:T(4,128)(2,1)} %param.13, s32[]{:T(128)S(6)} %select_n.73), kind=kLoop, calls=%fused_computation.130 | loop fusion | bytes 1572868 | tf_op jit(solution)/shard_map/jit(dynamic_index_in_dim)/dynamic_slice | solution.py:113
  17.8 3.4 %collective-permute-done.1 = bf16[512,256]{0,1:T(8,128)(2,1)S(1)} collective-permute-done((bf16[512,256]{0,1:T(8,128)(2,1)S(1)}, bf16[512,256]{0,1:T(8,128)(2,1)S(1)}, u32[]{:S(2)}, u32[]{:S(2)}) %collective-permute-start.1) | collective-permute-done | bytes 262176 | tf_op jit(solution)/shard_map/ppermute | solution.py:117
  23.6 1.5 %collective-permute-done.3 = bf16[4,8,4224]{2,1,0:T(8,128)(2,1)S(1)} collective-permute-done((bf16[4,8,4224]{2,1,0:T(8,128)(2,1)S(1)}, bf16[4,8,4224]{2,1,0:T(8,128)(2,1)S(1)}, u32[]{:S(2)}, u32[]{:S(2)}) %collective-permute-start.3) | collective-permute-done | bytes 270368 | tf_op jit(solution)/shard_map/ppermute | solution.py:91
  26.2 2.0 %collective-permute-start.4 = (bf16[4,2,4224]{2,1,0:T(2,128)(2,1)S(1)}, bf16[4,2,4224]{2,1,0:T(2,128)(2,1)S(1)}, u32[]{:S(2)}, u32[]{:S(2)}) collective-permute-start(bf16[4,2,4224]{2,1,0:T(2,128)(2,1)S(1)} %bitcast.122), channel_id=1, source_target_pairs={{0,8},{4,12},{8,16},{12,20},{16,24},{20,28},{24,32},{28,36},{32,40... | collective-permute-start | bytes 202760 | tf_op jit(solution)/shard_map/ppermute | solution.py:95
  28.2 4.6 %collective-permute-start.5 = (bf16[4,2,4224]{2,1,0:T(2,128)(2,1)S(1)}, bf16[4,2,4224]{2,1,0:T(2,128)(2,1)S(1)}, u32[]{:S(2)}, u32[]{:S(2)}) collective-permute-start(bf16[4,2,4224]{2,1,0:T(2,128)(2,1)S(1)} %bitcast.120), channel_id=1, source_target_pairs={{0,16},{4,20},{8,24},{12,28},{16,32},{20,36},{24,40},{28,44},{32,4... | collective-permute-start | bytes 202760 | tf_op jit(solution)/shard_map/ppermute | solution.py:95
  32.9 2.0 %collective-permute-start.6 = (bf16[4,2,4224]{2,1,0:T(2,128)(2,1)S(1)}, bf16[4,2,4224]{2,1,0:T(2,128)(2,1)S(1)}, u32[]{:S(2)}, u32[]{:S(2)}) collective-permute-start(bf16[4,2,4224]{2,1,0:T(2,128)(2,1)S(1)} %bitcast.113), channel_id=1, source_target_pairs={{0,24},{4,28},{8,32},{12,36},{16,40},{20,44},{24,48},{28,52},{32,5... | collective-permute-start | bytes 202760 | tf_op jit(solution)/shard_map/ppermute | solution.py:95
  35.0 1.7 %collective-permute-start.7 = (bf16[4,2,4224]{2,1,0:T(2,128)(2,1)S(1)}, bf16[4,2,4224]{2,1,0:T(2,128)(2,1)S(1)}, u32[]{:S(2)}, u32[]{:S(2)}) collective-permute-start(bf16[4,2,4224]{2,1,0:T(2,128)(2,1)S(1)} %bitcast.115), channel_id=1, source_target_pairs={{0,32},{4,36},{8,40},{12,44},{16,48},{20,52},{24,56},{28,60},{32,0... | collective-permute-start | bytes 202760 | tf_op jit(solution)/shard_map/ppermute | solution.py:95
  36.7 3.1 %collective-permute-start.8 = (bf16[4,2,4224]{2,1,0:T(2,128)(2,1)S(1)}, bf16[4,2,4224]{2,1,0:T(2,128)(2,1)S(1)}, u32[]{:S(2)}, u32[]{:S(2)}) collective-permute-start(bf16[4,2,4224]{2,1,0:T(2,128)(2,1)S(1)} %bitcast.117), channel_id=1, source_target_pairs={{0,40},{4,44},{8,48},{12,52},{16,56},{20,60},{24,0},{28,4},{32,8},... | collective-permute-start | bytes 202760 | tf_op jit(solution)/shard_map/ppermute | solution.py:95
  40.0 2.5 %collective-permute-start.9 = (bf16[4,2,4224]{2,1,0:T(2,128)(2,1)S(1)}, bf16[4,2,4224]{2,1,0:T(2,128)(2,1)S(1)}, u32[]{:S(2)}, u32[]{:S(2)}) collective-permute-start(bf16[4,2,4224]{2,1,0:T(2,128)(2,1)S(1)} %bitcast.119), channel_id=1, source_target_pairs={{0,48},{4,52},{8,56},{12,60},{16,0},{20,4},{24,8},{28,12},{32,16},... | collective-permute-start | bytes 202760 | tf_op jit(solution)/shard_map/ppermute | solution.py:95
  42.6 2.2 %collective-permute-start.10 = (bf16[4,2,4224]{2,1,0:T(2,128)(2,1)S(1)}, bf16[4,2,4224]{2,1,0:T(2,128)(2,1)S(1)}, u32[]{:S(2)}, u32[]{:S(2)}) collective-permute-start(bf16[4,2,4224]{2,1,0:T(2,128)(2,1)S(1)} %bitcast.111), channel_id=1, source_target_pairs={{0,56},{4,60},{8,0},{12,4},{16,8},{20,12},{24,16},{28,20},{32,24},... | collective-permute-start | bytes 202760 | tf_op jit(solution)/shard_map/ppermute | solution.py:95
  45.3 2.6 %collective-permute-done.8 = bf16[4,2,4224]{2,1,0:T(2,128)(2,1)S(1)} collective-permute-done((bf16[4,2,4224]{2,1,0:T(2,128)(2,1)S(1)}, bf16[4,2,4224]{2,1,0:T(2,128)(2,1)S(1)}, u32[]{:S(2)}, u32[]{:S(2)}) %collective-permute-start.8) | collective-permute-done | bytes 67616 | tf_op jit(solution)/shard_map/ppermute | solution.py:95
  48.0 2.8 %collective-permute-done.9 = bf16[4,2,4224]{2,1,0:T(2,128)(2,1)S(1)} collective-permute-done((bf16[4,2,4224]{2,1,0:T(2,128)(2,1)S(1)}, bf16[4,2,4224]{2,1,0:T(2,128)(2,1)S(1)}, u32[]{:S(2)}, u32[]{:S(2)}) %collective-permute-start.9) | collective-permute-done | bytes 67616 | tf_op jit(solution)/shard_map/ppermute | solution.py:95
  51.8 1.8 %stack.63 = bf16[4,8,2,4224]{3,1,0,2:T(8,128)(2,1)S(1)} concatenate(bf16[4,1,2,4224]{3,1,0,2:T(2,128)(2,1)S(1)} %get-tuple-element.13, bf16[4,1,2,4224]{3,1,0,2:T(2,128)(2,1)S(1)} %copy.234, bf16[4,1,2,4224]{3,1,0,2:T(2,128)(2,1)S(1)} %copy.235, bf16[4,1,2,4224]{3,1,0,2:T(2,128)(2,1)S(1)} %copy.236, bf16[4,1,2,4224]{3,1,0,2:T(2,128)(2,1)S(1)} %copy.237, ...), dimensions={1} | concatenate | bytes 1081344 | tf_op jit(solution)/shard_map/stack | solution.py:96
  53.6 1.7 %collective-permute-start.11 = (bf16[8,2,4224]{2,0,1:T(8,128)(2,1)S(1)}, bf16[8,2,4224]{2,0,1:T(8,128)(2,1)S(1)}, u32[]{:S(2)}, u32[]{:S(2)}) collective-permute-start(bf16[8,2,4224]{2,0,1:T(8,128)(2,1)S(1)} %get-tuple-element.11), channel_id=1, source_target_pairs={{0,64},{4,68},{8,72},{12,76},{16,80},{20,84},{24,88},{28,92},{32,9... | collective-permute-start | bytes 405512 | tf_op jit(solution)/shard_map/ppermute | solution.py:99
  55.3 2.9 %collective-permute-start.12 = (bf16[8,2,4224]{2,0,1:T(8,128)(2,1)S(1)}, bf16[8,2,4224]{2,0,1:T(8,128)(2,1)S(1)}, u32[]{:S(2)}, u32[]{:S(2)}) collective-permute-start(bf16[8,2,4224]{2,0,1:T(8,128)(2,1)S(1)} %get-tuple-element.10), channel_id=1, source_target_pairs={{0,128},{4,132},{8,136},{12,140},{16,144},{20,148},{24,152},{28,15... | collective-permute-start | bytes 405512 | tf_op jit(solution)/shard_map/ppermute | solution.py:99
  58.2 1.3 %collective-permute-start.13 = (bf16[8,2,4224]{2,0,1:T(8,128)(2,1)S(1)}, bf16[8,2,4224]{2,0,1:T(8,128)(2,1)S(1)}, u32[]{:S(2)}, u32[]{:S(2)}) collective-permute-start(bf16[8,2,4224]{2,0,1:T(8,128)(2,1)S(1)} %get-tuple-element.9), channel_id=1, source_target_pairs={{0,192},{4,196},{8,200},{12,204},{16,208},{20,212},{24,216},{28,22... | collective-permute-start | bytes 405512 | tf_op jit(solution)/shard_map/ppermute | solution.py:99
  61.2 3.4 %collective-permute-done.12 = bf16[8,2,4224]{2,0,1:T(8,128)(2,1)S(1)} collective-permute-done((bf16[8,2,4224]{2,0,1:T(8,128)(2,1)S(1)}, bf16[8,2,4224]{2,0,1:T(8,128)(2,1)S(1)}, u32[]{:S(2)}, u32[]{:S(2)}) %collective-permute-start.12) | collective-permute-done | bytes 135200 | tf_op jit(solution)/shard_map/ppermute | solution.py:99
  71.0 16.7 %shard_map.73 = bf16[6,1280,128]{2,1,0:T(8,128)(2,1)} custom-call(s32[1]{0:T(128)S(6)} %copy.274.len_ref, bf16[6,1280,128]{2,1,0:T(8,128)(2,1)} %bitcast.103, bf16[128,1280]{1,0:T(8,128)(2,1)} %copy.246.kt_ref, bf16[1280,256]{1,0:T(8,128)(2,1)} %pad_select_fusion.vx_ref), custom_call_target="tpu_custom_call" | custom-call | tf_op jit(solution)/shard_map/pallas_call | solution.py:61
  (69 shorter events, 14.8 us)
Async XLA Ops:
  0.0 1.4 %copy-start = (bf16[512,1536]{1,0:T(8,128)(2,1)S(1)}, bf16[512,1536]{1,0:T(8,128)(2,1)}, u32[]{:S(2)}) copy-start(bf16[512,1536]{1,0:T(8,128)(2,1)} %param.9) | copy-start | bytes 4718596
  1.4 9.6 %copy-start.3 = (s32[512]{0:T(512)S(1)}, s32[512]{0:T(512)}, u32[]{:S(2)}) copy-start(s32[512]{0:T(512)} %param.11) | copy-start | bytes 6148
  1.4 9.6 %copy-start.2 = (s32[512]{0:T(512)S(1)}, s32[512]{0:T(512)}, u32[]{:S(2)}) copy-start(s32[512]{0:T(512)} %param.10) | copy-start | bytes 6148
  5.2 12.5 %collective-permute-start = (bf16[512,256]{0,1:T(8,128)(2,1)S(1)}, bf16[512,256]{0,1:T(8,128)(2,1)S(1)}, u32[]{:S(2)}, u32[]{:S(2)}) collective-permute-start(bf16[512,256]{0,1:T(8,128)(2,1)S(1)} %get-tuple-element.5), channel_id=1, source_target_pairs={{0,1},{1,2},{2,3},{3,0},{4,5},{5,6},{6,7},{7,4},{8,9},{9,10},{10,1... | collective-permute-start | bytes 786440 | tf_op jit(solution)/shard_map/ppermute | solution.py:117
  6.8 14.4 %collective-permute-start.1 = (bf16[512,256]{0,1:T(8,128)(2,1)S(1)}, bf16[512,256]{0,1:T(8,128)(2,1)S(1)}, u32[]{:S(2)}, u32[]{:S(2)}) collective-permute-start(bf16[512,256]{0,1:T(8,128)(2,1)S(1)} %get-tuple-element.7), channel_id=1, source_target_pairs={{0,2},{1,3},{2,0},{3,1},{4,6},{5,7},{6,4},{7,5},{8,10},{9,11},{10,... | collective-permute-start | bytes 786440 | tf_op jit(solution)/shard_map/ppermute | solution.py:117
  9.5 11.6 %collective-permute-start.2 = (bf16[512,256]{0,1:T(8,128)(2,1)S(1)}, bf16[512,256]{0,1:T(8,128)(2,1)S(1)}, u32[]{:S(2)}, u32[]{:S(2)}) collective-permute-start(bf16[512,256]{0,1:T(8,128)(2,1)S(1)} %get-tuple-element.6), channel_id=1, source_target_pairs={{0,3},{1,0},{2,1},{3,2},{4,7},{5,4},{6,5},{7,6},{8,11},{9,8},{10,9... | collective-permute-start | bytes 786440 | tf_op jit(solution)/shard_map/ppermute | solution.py:117
  23.5 1.6 %collective-permute-start.3 = (bf16[4,8,4224]{2,1,0:T(8,128)(2,1)S(1)}, bf16[4,8,4224]{2,1,0:T(8,128)(2,1)S(1)}, u32[]{:S(2)}, u32[]{:S(2)}) collective-permute-start(bf16[4,8,4224]{2,1,0:T(8,128)(2,1)S(1)} %get-tuple-element.20), channel_id=1, source_target_pairs={{0,4},{4,0},{8,12},{12,8},{16,20},{20,16},{24,28},{28,24},{32,36},... | collective-permute-start | bytes 811016 | tf_op jit(solution)/shard_map/ppermute | solution.py:91
  26.2 13.8 %collective-permute-start.4 = (bf16[4,2,4224]{2,1,0:T(2,128)(2,1)S(1)}, bf16[4,2,4224]{2,1,0:T(2,128)(2,1)S(1)}, u32[]{:S(2)}, u32[]{:S(2)}) collective-permute-start(bf16[4,2,4224]{2,1,0:T(2,128)(2,1)S(1)} %bitcast.122), channel_id=1, source_target_pairs={{0,8},{4,12},{8,16},{12,20},{16,24},{20,28},{24,32},{28,36},{32,40... | collective-permute-start | bytes 202760 | tf_op jit(solution)/shard_map/ppermute | solution.py:95
  28.2 14.3 %collective-permute-start.5 = (bf16[4,2,4224]{2,1,0:T(2,128)(2,1)S(1)}, bf16[4,2,4224]{2,1,0:T(2,128)(2,1)S(1)}, u32[]{:S(2)}, u32[]{:S(2)}) collective-permute-start(bf16[4,2,4224]{2,1,0:T(2,128)(2,1)S(1)} %bitcast.120), channel_id=1, source_target_pairs={{0,16},{4,20},{8,24},{12,28},{16,32},{20,36},{24,40},{28,44},{32,4... | collective-permute-start | bytes 202760 | tf_op jit(solution)/shard_map/ppermute | solution.py:95
  32.9 12.1 %collective-permute-start.6 = (bf16[4,2,4224]{2,1,0:T(2,128)(2,1)S(1)}, bf16[4,2,4224]{2,1,0:T(2,128)(2,1)S(1)}, u32[]{:S(2)}, u32[]{:S(2)}) collective-permute-start(bf16[4,2,4224]{2,1,0:T(2,128)(2,1)S(1)} %bitcast.113), channel_id=1, source_target_pairs={{0,24},{4,28},{8,32},{12,36},{16,40},{20,44},{24,48},{28,52},{32,5... | collective-permute-start | bytes 202760 | tf_op jit(solution)/shard_map/ppermute | solution.py:95
  35.0 10.2 %collective-permute-start.7 = (bf16[4,2,4224]{2,1,0:T(2,128)(2,1)S(1)}, bf16[4,2,4224]{2,1,0:T(2,128)(2,1)S(1)}, u32[]{:S(2)}, u32[]{:S(2)}) collective-permute-start(bf16[4,2,4224]{2,1,0:T(2,128)(2,1)S(1)} %bitcast.115), channel_id=1, source_target_pairs={{0,32},{4,36},{8,40},{12,44},{16,48},{20,52},{24,56},{28,60},{32,0... | collective-permute-start | bytes 202760 | tf_op jit(solution)/shard_map/ppermute | solution.py:95
  36.7 11.1 %collective-permute-start.8 = (bf16[4,2,4224]{2,1,0:T(2,128)(2,1)S(1)}, bf16[4,2,4224]{2,1,0:T(2,128)(2,1)S(1)}, u32[]{:S(2)}, u32[]{:S(2)}) collective-permute-start(bf16[4,2,4224]{2,1,0:T(2,128)(2,1)S(1)} %bitcast.117), channel_id=1, source_target_pairs={{0,40},{4,44},{8,48},{12,52},{16,56},{20,60},{24,0},{28,4},{32,8},... | collective-permute-start | bytes 202760 | tf_op jit(solution)/shard_map/ppermute | solution.py:95
  40.0 10.7 %collective-permute-start.9 = (bf16[4,2,4224]{2,1,0:T(2,128)(2,1)S(1)}, bf16[4,2,4224]{2,1,0:T(2,128)(2,1)S(1)}, u32[]{:S(2)}, u32[]{:S(2)}) collective-permute-start(bf16[4,2,4224]{2,1,0:T(2,128)(2,1)S(1)} %bitcast.119), channel_id=1, source_target_pairs={{0,48},{4,52},{8,56},{12,60},{16,0},{20,4},{24,8},{28,12},{32,16},... | collective-permute-start | bytes 202760 | tf_op jit(solution)/shard_map/ppermute | solution.py:95
  42.6 9.1 %collective-permute-start.10 = (bf16[4,2,4224]{2,1,0:T(2,128)(2,1)S(1)}, bf16[4,2,4224]{2,1,0:T(2,128)(2,1)S(1)}, u32[]{:S(2)}, u32[]{:S(2)}) collective-permute-start(bf16[4,2,4224]{2,1,0:T(2,128)(2,1)S(1)} %bitcast.111), channel_id=1, source_target_pairs={{0,56},{4,60},{8,0},{12,4},{16,8},{20,12},{24,16},{28,20},{32,24},... | collective-permute-start | bytes 202760 | tf_op jit(solution)/shard_map/ppermute | solution.py:95
  53.6 7.6 %collective-permute-start.11 = (bf16[8,2,4224]{2,0,1:T(8,128)(2,1)S(1)}, bf16[8,2,4224]{2,0,1:T(8,128)(2,1)S(1)}, u32[]{:S(2)}, u32[]{:S(2)}) collective-permute-start(bf16[8,2,4224]{2,0,1:T(8,128)(2,1)S(1)} %get-tuple-element.11), channel_id=1, source_target_pairs={{0,64},{4,68},{8,72},{12,76},{16,80},{20,84},{24,88},{28,92},{32,9... | collective-permute-start | bytes 405512 | tf_op jit(solution)/shard_map/ppermute | solution.py:99
  55.3 9.3 %collective-permute-start.12 = (bf16[8,2,4224]{2,0,1:T(8,128)(2,1)S(1)}, bf16[8,2,4224]{2,0,1:T(8,128)(2,1)S(1)}, u32[]{:S(2)}, u32[]{:S(2)}) collective-permute-start(bf16[8,2,4224]{2,0,1:T(8,128)(2,1)S(1)} %get-tuple-element.10), channel_id=1, source_target_pairs={{0,128},{4,132},{8,136},{12,140},{16,144},{20,148},{24,152},{28,15... | collective-permute-start | bytes 405512 | tf_op jit(solution)/shard_map/ppermute | solution.py:99
  58.2 6.4 %collective-permute-start.13 = (bf16[8,2,4224]{2,0,1:T(8,128)(2,1)S(1)}, bf16[8,2,4224]{2,0,1:T(8,128)(2,1)S(1)}, u32[]{:S(2)}, u32[]{:S(2)}) collective-permute-start(bf16[8,2,4224]{2,0,1:T(8,128)(2,1)S(1)} %get-tuple-element.9), channel_id=1, source_target_pairs={{0,192},{4,196},{8,200},{12,204},{16,208},{20,212},{24,216},{28,22... | collective-permute-start | bytes 405512 | tf_op jit(solution)/shard_map/ppermute | solution.py:99
  65.9 2.1 %copy-start.1 = (bf16[1,1280,1,256]{3,1,2,0:T(8,128)(2,1)S(1)}, bf16[1,1280,1,256]{3,1,2,0:T(8,128)(2,1)}, u32[]{:S(2)}) copy-start(bf16[1,1280,1,256]{3,1,2,0:T(8,128)(2,1)} %param.8) | copy-start | bytes 1966084

commit v10 on v8

--- a/solution.py
+++ b/solution.py
@@ -24,15 +24,24 @@
     return rotated.astype(jnp.bfloat16)
 
 
-def attention_kernel(block, head_dim, len_ref, q_ref, kt_ref, vx_ref, o_ref):
+def attention_kernel(block, head_dim, len_ref, q_ref, kv_ref, o_ref, vx_ref):
     prompt = q_ref.shape[1]
     length = len_ref[0]
     scale = head_dim ** (-0.5)
+
+    @pl.when(pl.program_id(0) == 0)
+    def _():
+        vx_ref[:, :head_dim] = kv_ref[:, head_dim:]
+        vx_ref[:, head_dim:] = jnp.ones((prompt, head_dim), vx_ref.dtype)
+
     for index in range(prompt // block):
         row_start = index * block
         keys_used = row_start + block
         query = q_ref[0, row_start:keys_used, :]
-        scores = jnp.dot(query, kt_ref[:, 0:keys_used], preferred_element_type=jnp.float32)
+        scores = lax.dot_general(
+            query, kv_ref[0:keys_used, 0:head_dim], (((1,), (1,)), ((), ())),
+            preferred_element_type=jnp.float32,
+        )
         query_index = row_start + lax.broadcasted_iota(jnp.int32, (block, 1), 0)
         limit = jnp.minimum(query_index, length - 1)
         key_index = row_start + lax.broadcasted_iota(jnp.int32, (1, block), 1)
@@ -46,24 +55,24 @@
         o_ref[0, row_start:keys_used, :] = result.astype(o_ref.dtype)
 
 
-def attend(heads_first, keys_t, values_ext, length, head_dim, block=256):
+def attend(heads_first, prompt_kv, length, head_dim, block=256):
     heads, prompt, _ = heads_first.shape
     grid_spec = pltpu.PrefetchScalarGridSpec(
         num_scalar_prefetch=1,
         grid=(heads,),
         in_specs=[
             pl.BlockSpec((1, prompt, head_dim), lambda h, lens: (h, 0, 0)),
-            pl.BlockSpec((head_dim, prompt), lambda h, lens: (0, 0)),
             pl.BlockSpec((prompt, 2 * head_dim), lambda h, lens: (0, 0)),
         ],
         out_specs=pl.BlockSpec((1, prompt, head_dim), lambda h, lens: (h, 0, 0)),
+        scratch_shapes=[pltpu.VMEM((prompt, 2 * head_dim), jnp.bfloat16)],
     )
     return pl.pallas_call(
         functools.partial(attention_kernel, block, head_dim),
         grid_spec=grid_spec,
         out_shape=jax.ShapeDtypeStruct((heads, prompt, head_dim), jnp.bfloat16),
         compiler_params=pltpu.CompilerParams(dimension_semantics=("arbitrary",)),
-    )(length, heads_first, keys_t, values_ext)
+    )(length, heads_first, prompt_kv)
 
 
 def per_device(queries, text_kv, image_rows, row_request, row_position, prompt_lengths, kv_weight):
@@ -100,29 +109,17 @@
     tail = send_pos.reshape(groups, 2 * capacity).astype(jnp.bfloat16)
     tail = jnp.pad(tail, ((0, 0), (0, 128 - 2 * capacity)))
     packet = jnp.concatenate([send_kv.reshape(groups, capacity * width), tail], axis=1)
-    text = text_kv[0, :, 0, :]
-    text_keys_t = jnp.transpose(text[:, :head_dim])
-    ones = jnp.ones((prompt, head_dim), text.dtype)
-    text_values_ext = jnp.concatenate([text[:, head_dim:], ones], axis=1)
     got = lax.all_to_all(packet, "req", split_axis=0, concat_axis=0, tiled=True)
     got_kv = got[:, : capacity * width].reshape(slots, width)
     got_digits = got[:, capacity * width : capacity * width + 2 * capacity].astype(jnp.int32)
     got_digits = got_digits.reshape(slots, 2)
     places = got_digits[:, 0] * 16 + got_digits[:, 1] - 1
     match = places[None, :] == jnp.arange(prompt, dtype=jnp.int32)[:, None]
-    place = match.astype(jnp.bfloat16)
+    placed = jnp.dot(match.astype(jnp.bfloat16), got_kv, preferred_element_type=jnp.float32)
     hit = jnp.any(match, axis=1)
-    image_keys_t = jnp.einsum(
-        "sd,ps->dp", got_kv[:, :head_dim], place, preferred_element_type=jnp.float32
-    ).astype(jnp.bfloat16)
-    image_values = jnp.dot(place, got_kv[:, head_dim:], preferred_element_type=jnp.float32)
-    keys_t = jnp.where(hit[None, :], image_keys_t, text_keys_t)
-    values_ext = jnp.where(
-        hit[:, None], jnp.concatenate([image_values.astype(jnp.bfloat16), ones], axis=1),
-        text_values_ext,
-    )
+    prompt_kv = jnp.where(hit[:, None], placed.astype(jnp.bfloat16), text_kv[0, :, 0, :])
     heads_first = jnp.transpose(queries[0], (1, 0, 2))
-    out = attend(heads_first, keys_t, values_ext, prompt_lengths, head_dim)
+    out = attend(heads_first, prompt_kv, prompt_lengths, head_dim)
     return jnp.transpose(out, (1, 0, 2))[None]
 
 

time: 80.6 us -> 78.6 us (0.975)
  other arithmetic: 5.16 us -> 4.02 us
  local copies, waits for them, and re-layouts: 9.9 us -> 8.96 us
    select_n x1 -> x0, other arithmetic: 1.07 us -> none  [per_device(): jnp.where(hit[:, None], jnp.concatenate([image_values.astype(jnp.bfloat16...]
    select_n x1 -> x0, local copies, waits for them, and re-layouts: 0.91 us -> none  [per_device(): keys_t = jnp.where(hit[None, :], image_keys_t, text_keys_t)]
    dot_general x2 -> x1, matrix products: 2.02 us -> 1.93 us  [per_device(): jnp.dot(match.astype(jnp.bfloat16), got_kv, preferred_element_type=jnp.fl...]
    unnamed x13 -> x11, local copies, waits for them, and re-layouts: 3.28 us -> 3.28 us
  transfers between devices with their start and end apart: 4 -> 4, of which waited for: 2 -> 2; matrix products, arithmetic and copies ran while one was open for 8% -> 9% of each run, Pallas kernels for 0% -> 0%
where the time goes in v10:
time: 78.6 us; the launch traced here: 78.3 us
  waiting for transfers between devices  20.8 us (26%)
  starting transfers between devices  18.9 us (24%)
  Pallas kernels  16.9 us (22%)
  local copies, waits for them, and re-layouts  8.96 us (11%)
  matrix products  7.83 us (10%)
  other arithmetic  4.02 us (5%)
  between operations  0.86 us (1%)
    all_to_all x1, waiting for transfers between devices, per_device(): got = lax.all_to_all(packet, 'req', split_axis=0, concat_axis=0, tiled=True)  17.4 us
    pallas_call x1, Pallas kernels, attend(): pl.pallas_call(functools.partial(attention_kernel, block, head_dim), grid...  16.9 us
    all_to_all x1, starting transfers between devices, per_device(): got = lax.all_to_all(packet, 'req', split_axis=0, concat_axis=0, tiled=True)  13.2 us
    ppermute x3, starting transfers between devices, per_device(): lax.ppermute(outgoing, 'tp', perm=[(i, (i + shift) % heads) for i in rang...  5.72 us
    dot_general x1, matrix products, per_device(): jnp.einsum('rd,dhc->hrc', image_rows, kv_weight, preferred_element_type=j...  3.72 us
    dynamic_slice x1, local copies, waits for them, and re-layouts, per_device(): own_weight = lax.dynamic_index_in_dim(kv_weight, me, axis=1, keepdims=False)  3.57 us
    ppermute x3, waiting for transfers between devices, per_device(): lax.ppermute(outgoing, 'tp', perm=[(i, (i + shift) % heads) for i in rang...  3.43 us
    unnamed x11, local copies, waits for them, and re-layouts  3.28 us
  transfers between devices with their start and end apart: 4, of which 2 were waited for; matrix products, arithmetic and copies ran while one was open for 9% of the time, Pallas kernels for 0%

profile of v10, /device:TPU:1, one launch (start us, length us, event | category | flops | bytes accessed | tf_op | source)
XLA Modules:
  0.0 78.3 jit_solution(9463617456964124167)
XLA Ops:
  0.0 1.4 %copy-done = bf16[512,1536]{1,0:T(8,128)(2,1)S(1)} copy-done((bf16[512,1536]{1,0:T(8,128)(2,1)S(1)}, bf16[512,1536]{1,0:T(8,128)(2,1)}, u32[]{:S(2)}) %copy-start) | copy-done | bytes 1572888
  1.4 3.7 %fusion.2 = bf16[4,256,512]{2,1,0:T(8,128)(2,1)S(1)} fusion(bf16[1536,4,256]{2,1,0:T(4,128)(2,1)} %param.13, bf16[512,1536]{1,0:T(8,128)(2,1)S(1)} %copy-done), kind=kOutput, calls=%fused_computation.3 | convolution fusion | flops 1610612736 | bytes 5767168 | tf_op jit(solution)/shard_map/rd,dhc->hrc/dot_general | solution.py:86
  5.2 2.1 %collective-permute-start = (bf16[512,256]{0,1:T(8,128)(2,1)S(1)}, bf16[512,256]{0,1:T(8,128)(2,1)S(1)}, u32[]{:S(2)}, u32[]{:S(2)}) collective-permute-start(bf16[512,256]{0,1:T(8,128)(2,1)S(1)} %get-tuple-element.5), channel_id=1, source_target_pairs={{0,1},{1,2},{2,3},{3,0},{4,5},{5,6},{6,7},{7,4},{8,9},{9,10},{10,1... | collective-permute-start | bytes 786440 | tf_op jit(solution)/shard_map/ppermute | solution.py:92
  7.4 2.5 %collective-permute-start.1 = (bf16[512,256]{0,1:T(8,128)(2,1)S(1)}, bf16[512,256]{0,1:T(8,128)(2,1)S(1)}, u32[]{:S(2)}, u32[]{:S(2)}) collective-permute-start(bf16[512,256]{0,1:T(8,128)(2,1)S(1)} %get-tuple-element.7), channel_id=1, source_target_pairs={{0,2},{1,3},{2,0},{3,1},{4,6},{5,7},{6,4},{7,5},{8,10},{9,11},{10,... | collective-permute-start | bytes 786440 | tf_op jit(solution)/shard_map/ppermute | solution.py:92
  9.8 1.2 %collective-permute-start.2 = (bf16[512,256]{0,1:T(8,128)(2,1)S(1)}, bf16[512,256]{0,1:T(8,128)(2,1)S(1)}, u32[]{:S(2)}, u32[]{:S(2)}) collective-permute-start(bf16[512,256]{0,1:T(8,128)(2,1)S(1)} %get-tuple-element.6), channel_id=1, source_target_pairs={{0,3},{1,0},{2,1},{3,2},{4,7},{5,4},{6,5},{7,6},{8,11},{9,8},{10,9... | collective-permute-start | bytes 786440 | tf_op jit(solution)/shard_map/ppermute | solution.py:92
  11.0 1.2 %reduce-window.6 = s32[64,4,128]{2,0,1:T(8,128)S(1)} reduce-window(s32[64,4,128]{2,0,1:T(8,128)S(1)} %fusion.35, s32[]{:T(128)} %constant.52.clone.1), window={size=1x1x128 pad=0_0x0_0x127_0}, to_apply=%region_0.1 | reduce-window | flops 4161536 | bytes 262148 | tf_op jit(solution)/shard_map/reduce-window
  12.6 1.0 %fusion.11 = bf16[1024,2]{0,1:T(2,128)(2,1)S(1)} fusion(s32[512]{0:T(512)S(1)} %multiply_add_fusion, f32[512,1]{0,1:T(1,128)S(1)} %bitcast.64, f32[512,1]{0,1:T(1,128)S(1)} %bitcast.63), kind=kOutput, calls=%fused_computation.14 | convolution fusion | flops 13110272 | bytes 10240 | tf_op jit(solution)/shard_map/dot_general | solution.py:108
  13.9 0.2 convert_element_type.47
  14.1 3.6 %constant_dynamic-slice_fusion = bf16[1536,1,256]{2,1,0:T(2,128)(2,1)S(1)} fusion(bf16[1536,4,256]{2,1,0:T(4,128)(2,1)} %param.13, s32[]{:T(128)S(6)} %select_n.33), kind=kLoop, calls=%fused_computation.63 | loop fusion | bytes 1572868 | tf_op jit(solution)/shard_map/jit(dynamic_index_in_dim)/dynamic_slice | solution.py:88
  17.7 3.4 %collective-permute-done.1 = bf16[512,256]{0,1:T(8,128)(2,1)S(1)} collective-permute-done((bf16[512,256]{0,1:T(8,128)(2,1)S(1)}, bf16[512,256]{0,1:T(8,128)(2,1)S(1)}, u32[]{:S(2)}, u32[]{:S(2)}) %collective-permute-start.1) | collective-permute-done | bytes 262176 | tf_op jit(solution)/shard_map/ppermute | solution.py:92
  21.1 0.7 convert_add_fusion
  21.8 0.6 fusion.29
  22.4 0.5 fusion.10
  23.2 0.5 broadcast.67
  23.7 1.0 %reduce.4 = bf16[64,4224]{1,0:T(8,128)(2,1)S(1)} reduce(bf16[64,1,4224]{2,0,1:T(8,128)(2,1)S(1)} %fusion.16, bf16[]{:T(256)} %broadcast.67), dimensions={1}, to_apply=%copy.26.reduce_sub_computation | reduce | bytes 1081346 | tf_op jit(solution)/shard_map/all_to_all | solution.py:112
  24.7 1.2 %reshape.67 = bf16[64,2,2112]{2,1,0:T(2,128)(2,1)} reshape(bf16[64,4224]{1,0:T(8,128)(2,1)S(1)} %reduce.4) | data formatting | bytes 1081344
  25.9 13.2 %all-to-all-start = ((bf16[64,2,2112]{2,1,0:T(2,128)(2,1)}), bf16[64,2,2112]{2,1,0:T(2,128)(2,1)S(1)}, u32[]{:S(2)}, u32[]{:S(2)}) async-start(bf16[64,2,2112]{2,1,0:T(2,128)(2,1)} %reshape.67), calls=%async_computation | async-start | bytes 1114112 | tf_op jit(solution)/shard_map/all_to_all | solution.py:112
  39.7 17.4 %all-to-all-done = bf16[64,2,2112]{2,1,0:T(2,128)(2,1)S(1)} async-done(((bf16[64,2,2112]{2,1,0:T(2,128)(2,1)}), bf16[64,2,2112]{2,1,0:T(2,128)(2,1)S(1)}, u32[]{:S(2)}, u32[]{:S(2)}) %all-to-all-start) | async-done | bytes 540704 | tf_op jit(solution)/shard_map/all_to_all | solution.py:112
  57.1 0.6 reshape.68
  58.1 0.3 reshape.62
  58.4 0.4 fusion.18
  58.8 0.7 fusion.1
  59.5 1.9 %fusion.6.kv_ref = bf16[1280,256]{1,0:T(8,128)(2,1)} fusion(bf16[1024,256]{1,0:T(8,128)(2,1)S(1)} %reshape.60, s32[1024]{0:T(1024)S(1)} %fusion.18, bf16[1,1280,1,256]{3,1,2,0:T(8,128)(2,1)S(1)} %copy-done.3, pred[1280]{0:T(1024)(128)(4,1)S(1)} %fusion.1), kind=kOutput, calls=%fused_computation.7 | convolution fusion | flops 673054720 | bytes 1840384 | tf_op jit(solution)/shard_map/dot_general | solution.py:118
  61.4 16.9 %shard_map.73 = bf16[6,1280,128]{2,1,0:T(8,128)(2,1)} custom-call(s32[1]{0:T(128)S(6)} %copy.40.len_ref, bf16[6,1280,128]{2,1,0:T(8,128)(2,1)} %bitcast.61, bf16[1280,256]{1,0:T(8,128)(2,1)} %fusion.6.kv_ref), custom_call_target="tpu_custom_call" | custom-call | tf_op jit(solution)/shard_map/pallas_call | solution.py:70
  (27 shorter events, 1.4 us)
Async XLA Ops:
  0.0 1.4 %copy-start = (bf16[512,1536]{1,0:T(8,128)(2,1)S(1)}, bf16[512,1536]{1,0:T(8,128)(2,1)}, u32[]{:S(2)}) copy-start(bf16[512,1536]{1,0:T(8,128)(2,1)} %param.9) | copy-start | bytes 4718596
  5.1 5.8 %copy-start.2 = (s32[512]{0:T(512)S(1)}, s32[512]{0:T(512)}, u32[]{:S(2)}) copy-start(s32[512]{0:T(512)} %param.11) | copy-start | bytes 6148
  5.2 5.8 %copy-start.1 = (s32[512]{0:T(512)S(1)}, s32[512]{0:T(512)}, u32[]{:S(2)}) copy-start(s32[512]{0:T(512)} %param.10) | copy-start | bytes 6148
  5.2 12.5 %collective-permute-start = (bf16[512,256]{0,1:T(8,128)(2,1)S(1)}, bf16[512,256]{0,1:T(8,128)(2,1)S(1)}, u32[]{:S(2)}, u32[]{:S(2)}) collective-permute-start(bf16[512,256]{0,1:T(8,128)(2,1)S(1)} %get-tuple-element.5), channel_id=1, source_target_pairs={{0,1},{1,2},{2,3},{3,0},{4,5},{5,6},{6,7},{7,4},{8,9},{9,10},{10,1... | collective-permute-start | bytes 786440 | tf_op jit(solution)/shard_map/ppermute | solution.py:92
  7.4 13.8 %collective-permute-start.1 = (bf16[512,256]{0,1:T(8,128)(2,1)S(1)}, bf16[512,256]{0,1:T(8,128)(2,1)S(1)}, u32[]{:S(2)}, u32[]{:S(2)}) collective-permute-start(bf16[512,256]{0,1:T(8,128)(2,1)S(1)} %get-tuple-element.7), channel_id=1, source_target_pairs={{0,2},{1,3},{2,0},{3,1},{4,6},{5,7},{6,4},{7,5},{8,10},{9,11},{10,... | collective-permute-start | bytes 786440 | tf_op jit(solution)/shard_map/ppermute | solution.py:92
  9.8 11.3 %collective-permute-start.2 = (bf16[512,256]{0,1:T(8,128)(2,1)S(1)}, bf16[512,256]{0,1:T(8,128)(2,1)S(1)}, u32[]{:S(2)}, u32[]{:S(2)}) collective-permute-start(bf16[512,256]{0,1:T(8,128)(2,1)S(1)} %get-tuple-element.6), channel_id=1, source_target_pairs={{0,3},{1,0},{2,1},{3,2},{4,7},{5,4},{6,5},{7,6},{8,11},{9,8},{10,9... | collective-permute-start | bytes 786440 | tf_op jit(solution)/shard_map/ppermute | solution.py:92
  25.9 31.3 %all-to-all-start = ((bf16[64,2,2112]{2,1,0:T(2,128)(2,1)}), bf16[64,2,2112]{2,1,0:T(2,128)(2,1)S(1)}, u32[]{:S(2)}, u32[]{:S(2)}) async-start(bf16[64,2,2112]{2,1,0:T(2,128)(2,1)} %reshape.67), calls=%async_computation | async-start | bytes 1114112 | tf_op jit(solution)/shard_map/all_to_all | solution.py:112
  57.9 1.6 %copy-start.3 = (bf16[1,1280,1,256]{3,1,2,0:T(8,128)(2,1)S(1)}, bf16[1,1280,1,256]{3,1,2,0:T(8,128)(2,1)}, u32[]{:S(2)}) copy-start(bf16[1,1280,1,256]{3,1,2,0:T(8,128)(2,1)} %param.8) | copy-start | bytes 1966084

commit v11 on v10

--- a/solution.py
+++ b/solution.py
@@ -24,7 +24,7 @@
     return rotated.astype(jnp.bfloat16)
 
 
-def attention_kernel(block, head_dim, len_ref, q_ref, kv_ref, o_ref, vx_ref):
+def attention_kernel(block, head_dim, group, len_ref, q_ref, kv_ref, o_ref, vx_ref):
     prompt = q_ref.shape[1]
     length = len_ref[0]
     scale = head_dim ** (-0.5)
@@ -37,12 +37,12 @@
     for index in range(prompt // block):
         row_start = index * block
         keys_used = row_start + block
-        query = q_ref[0, row_start:keys_used, :]
+        query = jnp.concatenate([q_ref[g, row_start:keys_used, :] for g in range(group)], axis=0)
         scores = lax.dot_general(
             query, kv_ref[0:keys_used, 0:head_dim], (((1,), (1,)), ((), ())),
             preferred_element_type=jnp.float32,
         )
-        query_index = row_start + lax.broadcasted_iota(jnp.int32, (block, 1), 0)
+        query_index = row_start + lax.broadcasted_iota(jnp.int32, (group * block, 1), 0) % block
         limit = jnp.minimum(query_index, length - 1)
         key_index = row_start + lax.broadcasted_iota(jnp.int32, (1, block), 1)
         diag = jnp.where(key_index <= limit, scores[:, row_start:], jnp.float32(-1e30))
@@ -51,24 +51,26 @@
         weights = jnp.exp((scores - highest) * scale).astype(jnp.bfloat16)
         both = jnp.dot(weights, vx_ref[0:keys_used, :], preferred_element_type=jnp.float32)
         result = both[:, :head_dim] / both[:, head_dim : head_dim + 1]
-        result = jnp.where(query_index < length, result, jnp.float32(0.0))
-        o_ref[0, row_start:keys_used, :] = result.astype(o_ref.dtype)
+        result = jnp.where(query_index < length, result, jnp.float32(0.0)).astype(o_ref.dtype)
+        for g in range(group):
+            o_ref[g, row_start:keys_used, :] = result[g * block : (g + 1) * block]
 
 
 def attend(heads_first, prompt_kv, length, head_dim, block=256):
     heads, prompt, _ = heads_first.shape
+    group = math.gcd(heads, 3)
     grid_spec = pltpu.PrefetchScalarGridSpec(
         num_scalar_prefetch=1,
-        grid=(heads,),
+        grid=(heads // group,),
         in_specs=[
-            pl.BlockSpec((1, prompt, head_dim), lambda h, lens: (h, 0, 0)),
+            pl.BlockSpec((group, prompt, head_dim), lambda h, lens: (h, 0, 0)),
             pl.BlockSpec((prompt, 2 * head_dim), lambda h, lens: (0, 0)),
         ],
-        out_specs=pl.BlockSpec((1, prompt, head_dim), lambda h, lens: (h, 0, 0)),
+        out_specs=pl.BlockSpec((group, prompt, head_dim), lambda h, lens: (h, 0, 0)),
         scratch_shapes=[pltpu.VMEM((prompt, 2 * head_dim), jnp.bfloat16)],
     )
     return pl.pallas_call(
-        functools.partial(attention_kernel, block, head_dim),
+        functools.partial(attention_kernel, block, head_dim, group),
         grid_spec=grid_spec,
         out_shape=jax.ShapeDtypeStruct((heads, prompt, head_dim), jnp.bfloat16),
         compiler_params=pltpu.CompilerParams(dimension_semantics=("arbitrary",)),

time: 78.6 us -> 74.3 us (0.945)
  Pallas kernels: 16.9 us -> 12.5 us
    pallas_call x1, Pallas kernels: 16.9 us -> 12.5 us  [attend(): pl.pallas_call(functools.partial(attention_kernel, block, head_dim, group...]
where the time goes in v11:
time: 74.3 us; the launch traced here: 74 us
  waiting for transfers between devices  20.8 us (28%)
  starting transfers between devices  18.9 us (25%)
  Pallas kernels  12.5 us (17%)
  local copies, waits for them, and re-layouts  8.96 us (12%)
  matrix products  7.83 us (11%)
  other arithmetic  4.02 us (5%)
  between operations  0.86 us (1%)
    all_to_all x1, waiting for transfers between devices, per_device(): got = lax.all_to_all(packet, 'req', split_axis=0, concat_axis=0, tiled=True)  17.4 us
    all_to_all x1, starting transfers between devices, per_device(): got = lax.all_to_all(packet, 'req', split_axis=0, concat_axis=0, tiled=True)  13.2 us
    pallas_call x1, Pallas kernels, attend(): pl.pallas_call(functools.partial(attention_kernel, block, head_dim, group...  12.5 us
    ppermute x3, starting transfers between devices, per_device(): lax.ppermute(outgoing, 'tp', perm=[(i, (i + shift) % heads) for i in rang...  5.72 us
    dot_general x1, matrix products, per_device(): jnp.einsum('rd,dhc->hrc', image_rows, kv_weight, preferred_element_type=j...  3.72 us
    dynamic_slice x1, local copies, waits for them, and re-layouts, per_device(): own_weight = lax.dynamic_index_in_dim(kv_weight, me, axis=1, keepdims=False)  3.57 us
    ppermute x3, waiting for transfers between devices, per_device(): lax.ppermute(outgoing, 'tp', perm=[(i, (i + shift) % heads) for i in rang...  3.43 us
    unnamed x11, local copies, waits for them, and re-layouts  3.28 us
  transfers between devices with their start and end apart: 4, of which 2 were waited for; matrix products, arithmetic and copies ran while one was open for 9% of the time, Pallas kernels for 0%

profile of v11, /device:TPU:1, one launch (start us, length us, event | category | flops | bytes accessed | tf_op | source)
XLA Modules:
  0.0 74.0 jit_solution(7021069323723012482)
XLA Ops:
  0.0 1.4 %copy-done = bf16[512,1536]{1,0:T(8,128)(2,1)S(1)} copy-done((bf16[512,1536]{1,0:T(8,128)(2,1)S(1)}, bf16[512,1536]{1,0:T(8,128)(2,1)}, u32[]{:S(2)}) %copy-start) | copy-done | bytes 1572888
  1.4 3.7 %fusion.2 = bf16[4,256,512]{2,1,0:T(8,128)(2,1)S(1)} fusion(bf16[1536,4,256]{2,1,0:T(4,128)(2,1)} %param.13, bf16[512,1536]{1,0:T(8,128)(2,1)S(1)} %copy-done), kind=kOutput, calls=%fused_computation.3 | convolution fusion | flops 1610612736 | bytes 5767168 | tf_op jit(solution)/shard_map/rd,dhc->hrc/dot_general | solution.py:88
  5.2 2.1 %collective-permute-start = (bf16[512,256]{0,1:T(8,128)(2,1)S(1)}, bf16[512,256]{0,1:T(8,128)(2,1)S(1)}, u32[]{:S(2)}, u32[]{:S(2)}) collective-permute-start(bf16[512,256]{0,1:T(8,128)(2,1)S(1)} %get-tuple-element.5), channel_id=1, source_target_pairs={{0,1},{1,2},{2,3},{3,0},{4,5},{5,6},{6,7},{7,4},{8,9},{9,10},{10,1... | collective-permute-start | bytes 786440 | tf_op jit(solution)/shard_map/ppermute | solution.py:94
  7.4 2.5 %collective-permute-start.1 = (bf16[512,256]{0,1:T(8,128)(2,1)S(1)}, bf16[512,256]{0,1:T(8,128)(2,1)S(1)}, u32[]{:S(2)}, u32[]{:S(2)}) collective-permute-start(bf16[512,256]{0,1:T(8,128)(2,1)S(1)} %get-tuple-element.7), channel_id=1, source_target_pairs={{0,2},{1,3},{2,0},{3,1},{4,6},{5,7},{6,4},{7,5},{8,10},{9,11},{10,... | collective-permute-start | bytes 786440 | tf_op jit(solution)/shard_map/ppermute | solution.py:94
  9.8 1.2 %collective-permute-start.2 = (bf16[512,256]{0,1:T(8,128)(2,1)S(1)}, bf16[512,256]{0,1:T(8,128)(2,1)S(1)}, u32[]{:S(2)}, u32[]{:S(2)}) collective-permute-start(bf16[512,256]{0,1:T(8,128)(2,1)S(1)} %get-tuple-element.6), channel_id=1, source_target_pairs={{0,3},{1,0},{2,1},{3,2},{4,7},{5,4},{6,5},{7,6},{8,11},{9,8},{10,9... | collective-permute-start | bytes 786440 | tf_op jit(solution)/shard_map/ppermute | solution.py:94
  11.0 1.2 %reduce-window.6 = s32[64,4,128]{2,0,1:T(8,128)S(1)} reduce-window(s32[64,4,128]{2,0,1:T(8,128)S(1)} %fusion.35, s32[]{:T(128)} %constant.52.clone.1), window={size=1x1x128 pad=0_0x0_0x127_0}, to_apply=%region_0.1 | reduce-window | flops 4161536 | bytes 262148 | tf_op jit(solution)/shard_map/reduce-window
  12.6 1.0 %fusion.11 = bf16[1024,2]{0,1:T(2,128)(2,1)S(1)} fusion(s32[512]{0:T(512)S(1)} %multiply_add_fusion, f32[512,1]{0,1:T(1,128)S(1)} %bitcast.64, f32[512,1]{0,1:T(1,128)S(1)} %bitcast.63), kind=kOutput, calls=%fused_computation.14 | convolution fusion | flops 13110272 | bytes 10240 | tf_op jit(solution)/shard_map/dot_general | solution.py:110
  13.9 0.2 convert_element_type.47
  14.1 3.6 %constant_dynamic-slice_fusion = bf16[1536,1,256]{2,1,0:T(2,128)(2,1)S(1)} fusion(bf16[1536,4,256]{2,1,0:T(4,128)(2,1)} %param.13, s32[]{:T(128)S(6)} %select_n.33), kind=kLoop, calls=%fused_computation.63 | loop fusion | bytes 1572868 | tf_op jit(solution)/shard_map/jit(dynamic_index_in_dim)/dynamic_slice | solution.py:90
  17.7 3.4 %collective-permute-done.1 = bf16[512,256]{0,1:T(8,128)(2,1)S(1)} collective-permute-done((bf16[512,256]{0,1:T(8,128)(2,1)S(1)}, bf16[512,256]{0,1:T(8,128)(2,1)S(1)}, u32[]{:S(2)}, u32[]{:S(2)}) %collective-permute-start.1) | collective-permute-done | bytes 262176 | tf_op jit(solution)/shard_map/ppermute | solution.py:94
  21.1 0.7 convert_add_fusion
  21.8 0.6 fusion.29
  22.4 0.5 fusion.10
  23.2 0.5 broadcast.67
  23.7 1.0 %reduce.4 = bf16[64,4224]{1,0:T(8,128)(2,1)S(1)} reduce(bf16[64,1,4224]{2,0,1:T(8,128)(2,1)S(1)} %fusion.16, bf16[]{:T(256)} %broadcast.67), dimensions={1}, to_apply=%copy.26.reduce_sub_computation | reduce | bytes 1081346 | tf_op jit(solution)/shard_map/all_to_all | solution.py:114
  24.7 1.2 %reshape.67 = bf16[64,2,2112]{2,1,0:T(2,128)(2,1)} reshape(bf16[64,4224]{1,0:T(8,128)(2,1)S(1)} %reduce.4) | data formatting | bytes 1081344
  25.9 13.2 %all-to-all-start = ((bf16[64,2,2112]{2,1,0:T(2,128)(2,1)}), bf16[64,2,2112]{2,1,0:T(2,128)(2,1)S(1)}, u32[]{:S(2)}, u32[]{:S(2)}) async-start(bf16[64,2,2112]{2,1,0:T(2,128)(2,1)} %reshape.67), calls=%async_computation | async-start | bytes 1114112 | tf_op jit(solution)/shard_map/all_to_all | solution.py:114
  39.7 17.4 %all-to-all-done = bf16[64,2,2112]{2,1,0:T(2,128)(2,1)S(1)} async-done(((bf16[64,2,2112]{2,1,0:T(2,128)(2,1)}), bf16[64,2,2112]{2,1,0:T(2,128)(2,1)S(1)}, u32[]{:S(2)}, u32[]{:S(2)}) %all-to-all-start) | async-done | bytes 540704 | tf_op jit(solution)/shard_map/all_to_all | solution.py:114
  57.1 0.6 reshape.68
  58.1 0.3 reshape.62
  58.4 0.4 fusion.18
  58.8 0.7 fusion.1
  59.5 1.9 %fusion.6.kv_ref = bf16[1280,256]{1,0:T(8,128)(2,1)} fusion(bf16[1024,256]{1,0:T(8,128)(2,1)S(1)} %reshape.60, s32[1024]{0:T(1024)S(1)} %fusion.18, bf16[1,1280,1,256]{3,1,2,0:T(8,128)(2,1)S(1)} %copy-done.3, pred[1280]{0:T(1024)(128)(4,1)S(1)} %fusion.1), kind=kOutput, calls=%fused_computation.7 | convolution fusion | flops 673054720 | bytes 1840384 | tf_op jit(solution)/shard_map/dot_general | solution.py:120
  61.4 12.5 %shard_map.73 = bf16[6,1280,128]{2,1,0:T(8,128)(2,1)} custom-call(s32[1]{0:T(128)S(6)} %copy.40.len_ref, bf16[6,1280,128]{2,1,0:T(8,128)(2,1)} %bitcast.61, bf16[1280,256]{1,0:T(8,128)(2,1)} %fusion.6.kv_ref), custom_call_target="tpu_custom_call" | custom-call | tf_op jit(solution)/shard_map/pallas_call | solution.py:72
  (27 shorter events, 1.4 us)
Async XLA Ops:
  0.0 1.4 %copy-start = (bf16[512,1536]{1,0:T(8,128)(2,1)S(1)}, bf16[512,1536]{1,0:T(8,128)(2,1)}, u32[]{:S(2)}) copy-start(bf16[512,1536]{1,0:T(8,128)(2,1)} %param.9) | copy-start | bytes 4718596
  5.1 5.8 %copy-start.2 = (s32[512]{0:T(512)S(1)}, s32[512]{0:T(512)}, u32[]{:S(2)}) copy-start(s32[512]{0:T(512)} %param.11) | copy-start | bytes 6148
  5.2 5.8 %copy-start.1 = (s32[512]{0:T(512)S(1)}, s32[512]{0:T(512)}, u32[]{:S(2)}) copy-start(s32[512]{0:T(512)} %param.10) | copy-start | bytes 6148
  5.2 12.5 %collective-permute-start = (bf16[512,256]{0,1:T(8,128)(2,1)S(1)}, bf16[512,256]{0,1:T(8,128)(2,1)S(1)}, u32[]{:S(2)}, u32[]{:S(2)}) collective-permute-start(bf16[512,256]{0,1:T(8,128)(2,1)S(1)} %get-tuple-element.5), channel_id=1, source_target_pairs={{0,1},{1,2},{2,3},{3,0},{4,5},{5,6},{6,7},{7,4},{8,9},{9,10},{10,1... | collective-permute-start | bytes 786440 | tf_op jit(solution)/shard_map/ppermute | solution.py:94
  7.4 13.8 %collective-permute-start.1 = (bf16[512,256]{0,1:T(8,128)(2,1)S(1)}, bf16[512,256]{0,1:T(8,128)(2,1)S(1)}, u32[]{:S(2)}, u32[]{:S(2)}) collective-permute-start(bf16[512,256]{0,1:T(8,128)(2,1)S(1)} %get-tuple-element.7), channel_id=1, source_target_pairs={{0,2},{1,3},{2,0},{3,1},{4,6},{5,7},{6,4},{7,5},{8,10},{9,11},{10,... | collective-permute-start | bytes 786440 | tf_op jit(solution)/shard_map/ppermute | solution.py:94
  9.8 11.3 %collective-permute-start.2 = (bf16[512,256]{0,1:T(8,128)(2,1)S(1)}, bf16[512,256]{0,1:T(8,128)(2,1)S(1)}, u32[]{:S(2)}, u32[]{:S(2)}) collective-permute-start(bf16[512,256]{0,1:T(8,128)(2,1)S(1)} %get-tuple-element.6), channel_id=1, source_target_pairs={{0,3},{1,0},{2,1},{3,2},{4,7},{5,4},{6,5},{7,6},{8,11},{9,8},{10,9... | collective-permute-start | bytes 786440 | tf_op jit(solution)/shard_map/ppermute | solution.py:94
  25.9 31.3 %all-to-all-start = ((bf16[64,2,2112]{2,1,0:T(2,128)(2,1)}), bf16[64,2,2112]{2,1,0:T(2,128)(2,1)S(1)}, u32[]{:S(2)}, u32[]{:S(2)}) async-start(bf16[64,2,2112]{2,1,0:T(2,128)(2,1)} %reshape.67), calls=%async_computation | async-start | bytes 1114112 | tf_op jit(solution)/shard_map/all_to_all | solution.py:114
  57.9 1.6 %copy-start.3 = (bf16[1,1280,1,256]{3,1,2,0:T(8,128)(2,1)S(1)}, bf16[1,1280,1,256]{3,1,2,0:T(8,128)(2,1)}, u32[]{:S(2)}) copy-start(bf16[1,1280,1,256]{3,1,2,0:T(8,128)(2,1)} %param.8) | copy-start | bytes 1966084

commit v12 on v11

--- a/solution.py
+++ b/solution.py
@@ -108,13 +108,13 @@
     pos_f = row_position.astype(jnp.float32) + 1.0
     digits = jnp.stack([jnp.floor(pos_f / 16.0), pos_f - 16.0 * jnp.floor(pos_f / 16.0)], axis=1)
     send_pos = jnp.dot(pick.astype(jnp.float32), digits, precision=lax.Precision.HIGHEST)
-    tail = send_pos.reshape(groups, 2 * capacity).astype(jnp.bfloat16)
-    tail = jnp.pad(tail, ((0, 0), (0, 128 - 2 * capacity)))
-    packet = jnp.concatenate([send_kv.reshape(groups, capacity * width), tail], axis=1)
+    tail = send_pos.reshape(groups, 2, capacity).astype(jnp.bfloat16)
+    tail = jnp.pad(tail, ((0, 0), (0, 0), (0, 64 - capacity)))
+    packet = jnp.concatenate([send_kv.reshape(groups, 2, capacity * width // 2), tail], axis=2)
     got = lax.all_to_all(packet, "req", split_axis=0, concat_axis=0, tiled=True)
-    got_kv = got[:, : capacity * width].reshape(slots, width)
-    got_digits = got[:, capacity * width : capacity * width + 2 * capacity].astype(jnp.int32)
-    got_digits = got_digits.reshape(slots, 2)
+    got_kv = got[:, :, : capacity * width // 2].reshape(slots, width)
+    got_digits = got[:, :, capacity * width // 2 : capacity * width // 2 + capacity]
+    got_digits = got_digits.astype(jnp.int32).reshape(slots, 2)
     places = got_digits[:, 0] * 16 + got_digits[:, 1] - 1
     match = places[None, :] == jnp.arange(prompt, dtype=jnp.int32)[:, None]
     placed = jnp.dot(match.astype(jnp.bfloat16), got_kv, preferred_element_type=jnp.float32)

time: 74.3 us -> 72.4 us (0.974)
  local copies, waits for them, and re-layouts: 8.96 us -> 6.75 us
    unnamed x11 -> x8, local copies, waits for them, and re-layouts: 3.28 us -> 1.43 us
    concatenate x0 -> x1, other arithmetic: none -> 1.32 us  [per_device(): jnp.concatenate([send_kv.reshape(groups, 2, capacity * width // 2), tail]...]
    all_to_all x2 -> x0, other arithmetic: 1.01 us -> none  [per_device(): got = lax.all_to_all(packet, 'req', split_axis=0, concat_axis=0, tiled=True)]
where the time goes in v12:
time: 72.4 us; the launch traced here: 72.1 us
  waiting for transfers between devices  20.9 us (29%)
  starting transfers between devices  18.9 us (26%)
  Pallas kernels  12.5 us (17%)
  matrix products  7.84 us (11%)
  local copies, waits for them, and re-layouts  6.75 us (9%)
  other arithmetic  4.35 us (6%)
  between operations  0.83 us (1%)
    all_to_all x1, waiting for transfers between devices, per_device(): got = lax.all_to_all(packet, 'req', split_axis=0, concat_axis=0, tiled=True)  17.4 us
    all_to_all x1, starting transfers between devices, per_device(): got = lax.all_to_all(packet, 'req', split_axis=0, concat_axis=0, tiled=True)  13.2 us
    pallas_call x1, Pallas kernels, attend(): pl.pallas_call(functools.partial(attention_kernel, block, head_dim, group...  12.5 us
    ppermute x3, starting transfers between devices, per_device(): lax.ppermute(outgoing, 'tp', perm=[(i, (i + shift) % heads) for i in rang...  5.72 us
    dot_general x1, matrix products, per_device(): jnp.einsum('rd,dhc->hrc', image_rows, kv_weight, preferred_element_type=j...  3.72 us
    dynamic_slice x1, local copies, waits for them, and re-layouts, per_device(): own_weight = lax.dynamic_index_in_dim(kv_weight, me, axis=1, keepdims=False)  3.57 us
    ppermute x3, waiting for transfers between devices, per_device(): lax.ppermute(outgoing, 'tp', perm=[(i, (i + shift) % heads) for i in rang...  3.48 us
    dot_general x1, matrix products, per_device(): jnp.dot(match.astype(jnp.bfloat16), got_kv, preferred_element_type=jnp.fl...  1.93 us
  transfers between devices with their start and end apart: 4, of which 2 were waited for; matrix products, arithmetic and copies ran while one was open for 9% of the time, Pallas kernels for 0%

profile of v12, /device:TPU:1, one launch (start us, length us, event | category | flops | bytes accessed | tf_op | source)
XLA Modules:
  0.0 72.1 jit_solution(2501319120858002352)
XLA Ops:
  0.0 1.4 %copy-done = bf16[512,1536]{1,0:T(8,128)(2,1)S(1)} copy-done((bf16[512,1536]{1,0:T(8,128)(2,1)S(1)}, bf16[512,1536]{1,0:T(8,128)(2,1)}, u32[]{:S(2)}) %copy-start) | copy-done | bytes 1572888
  1.4 3.7 %fusion.2 = bf16[4,256,512]{2,1,0:T(8,128)(2,1)S(1)} fusion(bf16[1536,4,256]{2,1,0:T(4,128)(2,1)} %param.13, bf16[512,1536]{1,0:T(8,128)(2,1)S(1)} %copy-done), kind=kOutput, calls=%fused_computation.3 | convolution fusion | flops 1610612736 | bytes 5767168 | tf_op jit(solution)/shard_map/rd,dhc->hrc/dot_general | solution.py:88
  5.2 2.1 %collective-permute-start = (bf16[512,256]{0,1:T(8,128)(2,1)S(1)}, bf16[512,256]{0,1:T(8,128)(2,1)S(1)}, u32[]{:S(2)}, u32[]{:S(2)}) collective-permute-start(bf16[512,256]{0,1:T(8,128)(2,1)S(1)} %get-tuple-element.5), channel_id=1, source_target_pairs={{0,1},{1,2},{2,3},{3,0},{4,5},{5,6},{6,7},{7,4},{8,9},{9,10},{10,1... | collective-permute-start | bytes 786440 | tf_op jit(solution)/shard_map/ppermute | solution.py:94
  7.4 2.5 %collective-permute-start.1 = (bf16[512,256]{0,1:T(8,128)(2,1)S(1)}, bf16[512,256]{0,1:T(8,128)(2,1)S(1)}, u32[]{:S(2)}, u32[]{:S(2)}) collective-permute-start(bf16[512,256]{0,1:T(8,128)(2,1)S(1)} %get-tuple-element.7), channel_id=1, source_target_pairs={{0,2},{1,3},{2,0},{3,1},{4,6},{5,7},{6,4},{7,5},{8,10},{9,11},{10,... | collective-permute-start | bytes 786440 | tf_op jit(solution)/shard_map/ppermute | solution.py:94
  9.8 1.2 %collective-permute-start.2 = (bf16[512,256]{0,1:T(8,128)(2,1)S(1)}, bf16[512,256]{0,1:T(8,128)(2,1)S(1)}, u32[]{:S(2)}, u32[]{:S(2)}) collective-permute-start(bf16[512,256]{0,1:T(8,128)(2,1)S(1)} %get-tuple-element.6), channel_id=1, source_target_pairs={{0,3},{1,0},{2,1},{3,2},{4,7},{5,4},{6,5},{7,6},{8,11},{9,8},{10,9... | collective-permute-start | bytes 786440 | tf_op jit(solution)/shard_map/ppermute | solution.py:94
  11.0 1.2 %reduce-window.6 = s32[64,4,128]{2,0,1:T(8,128)S(1)} reduce-window(s32[64,4,128]{2,0,1:T(8,128)S(1)} %fusion.33, s32[]{:T(128)} %constant.52.clone.1), window={size=1x1x128 pad=0_0x0_0x127_0}, to_apply=%region_0.1 | reduce-window | flops 4161536 | bytes 262148 | tf_op jit(solution)/shard_map/reduce-window
  12.2 0.2 slice_reduce_fusion
  12.6 1.0 %fusion.11 = bf16[1024,2]{0,1:T(2,128)(2,1)S(1)} fusion(s32[512]{0:T(512)S(1)} %multiply_add_fusion, f32[512,1]{0,1:T(1,128)S(1)} %bitcast.57, f32[512,1]{0,1:T(1,128)S(1)} %bitcast.56), kind=kOutput, calls=%fused_computation.15 | convolution fusion | flops 13110272 | bytes 10240 | tf_op jit(solution)/shard_map/dot_general | solution.py:110
  13.6 0.2 copy.16
  14.1 3.6 %constant_dynamic-slice_fusion = bf16[1536,1,256]{2,1,0:T(2,128)(2,1)S(1)} fusion(bf16[1536,4,256]{2,1,0:T(4,128)(2,1)} %param.13, s32[]{:T(128)S(6)} %select_n.33), kind=kLoop, calls=%fused_computation.60 | loop fusion | bytes 1572868 | tf_op jit(solution)/shard_map/jit(dynamic_index_in_dim)/dynamic_slice | solution.py:90
  17.7 3.5 %collective-permute-done.1 = bf16[512,256]{0,1:T(8,128)(2,1)S(1)} collective-permute-done((bf16[512,256]{0,1:T(8,128)(2,1)S(1)}, bf16[512,256]{0,1:T(8,128)(2,1)S(1)}, u32[]{:S(2)}, u32[]{:S(2)}) %collective-permute-start.1) | collective-permute-done | bytes 262176 | tf_op jit(solution)/shard_map/ppermute | solution.py:94
  21.1 0.7 convert_add_fusion
  21.8 0.6 fusion.27
  22.4 0.5 fusion.10
  23.0 1.3 %fusion.14 = bf16[64,2,2112]{2,1,0:T(2,128)(2,1)} fusion(bf16[64,2,16]{2,1,0:T(2,128)(2,1)S(1)} %convert_element_type.47, bf16[64,2,2048]{2,1,0:T(2,128)(2,1)S(1)} %reshape.55), kind=kLoop, calls=%fused_computation.19 | loop fusion | flops 1622016 | bytes 1069056 | tf_op jit(solution)/shard_map/concatenate | solution.py:113
  24.4 13.2 %all-to-all-start = ((bf16[64,2,2112]{2,1,0:T(2,128)(2,1)}), bf16[64,2,2112]{2,1,0:T(2,128)(2,1)S(1)}, u32[]{:S(2)}, u32[]{:S(2)}) async-start(bf16[64,2,2112]{2,1,0:T(2,128)(2,1)} %fusion.14), calls=%async_computation | async-start | bytes 1114112 | tf_op jit(solution)/shard_map/all_to_all | solution.py:114
  38.2 17.4 %all-to-all-done = bf16[64,2,2112]{2,1,0:T(2,128)(2,1)S(1)} async-done(((bf16[64,2,2112]{2,1,0:T(2,128)(2,1)}), bf16[64,2,2112]{2,1,0:T(2,128)(2,1)S(1)}, u32[]{:S(2)}, u32[]{:S(2)}) %all-to-all-start) | async-done | bytes 540704 | tf_op jit(solution)/shard_map/all_to_all | solution.py:114
  55.6 0.4 slice.44
  56.0 0.3 reshape.58
  56.4 0.2 reshape.60
  56.6 0.4 fusion.16
  57.0 0.7 fusion.1
  57.6 1.9 %fusion.6.kv_ref = bf16[1280,256]{1,0:T(8,128)(2,1)} fusion(bf16[1024,256]{1,0:T(8,128)(2,1)S(1)} %reshape.58, s32[1024]{0:T(1024)S(1)} %fusion.16, bf16[1,1280,1,256]{3,1,2,0:T(8,128)(2,1)S(1)} %copy-done.3, pred[1280]{0:T(1024)(128)(4,1)S(1)} %fusion.1), kind=kOutput, calls=%fused_computation.7 | convolution fusion | flops 673054720 | bytes 1840384 | tf_op jit(solution)/shard_map/dot_general | solution.py:120
  59.6 12.5 %shard_map.73 = bf16[6,1280,128]{2,1,0:T(8,128)(2,1)} custom-call(s32[1]{0:T(128)S(6)} %copy.26.len_ref, bf16[6,1280,128]{2,1,0:T(8,128)(2,1)} %bitcast.54, bf16[1280,256]{1,0:T(8,128)(2,1)} %fusion.6.kv_ref), custom_call_target="tpu_custom_call" | custom-call | tf_op jit(solution)/shard_map/pallas_call | solution.py:72
  (22 shorter events, 0.7 us)
Async XLA Ops:
  0.0 1.4 %copy-start = (bf16[512,1536]{1,0:T(8,128)(2,1)S(1)}, bf16[512,1536]{1,0:T(8,128)(2,1)}, u32[]{:S(2)}) copy-start(bf16[512,1536]{1,0:T(8,128)(2,1)} %param.9) | copy-start | bytes 4718596
  5.1 5.8 %copy-start.2 = (s32[512]{0:T(512)S(1)}, s32[512]{0:T(512)}, u32[]{:S(2)}) copy-start(s32[512]{0:T(512)} %param.11) | copy-start | bytes 6148
  5.2 5.8 %copy-start.1 = (s32[512]{0:T(512)S(1)}, s32[512]{0:T(512)}, u32[]{:S(2)}) copy-start(s32[512]{0:T(512)} %param.10) | copy-start | bytes 6148
  5.2 12.4 %collective-permute-start = (bf16[512,256]{0,1:T(8,128)(2,1)S(1)}, bf16[512,256]{0,1:T(8,128)(2,1)S(1)}, u32[]{:S(2)}, u32[]{:S(2)}) collective-permute-start(bf16[512,256]{0,1:T(8,128)(2,1)S(1)} %get-tuple-element.5), channel_id=1, source_target_pairs={{0,1},{1,2},{2,3},{3,0},{4,5},{5,6},{6,7},{7,4},{8,9},{9,10},{10,1... | collective-permute-start | bytes 786440 | tf_op jit(solution)/shard_map/ppermute | solution.py:94
  7.4 13.8 %collective-permute-start.1 = (bf16[512,256]{0,1:T(8,128)(2,1)S(1)}, bf16[512,256]{0,1:T(8,128)(2,1)S(1)}, u32[]{:S(2)}, u32[]{:S(2)}) collective-permute-start(bf16[512,256]{0,1:T(8,128)(2,1)S(1)} %get-tuple-element.7), channel_id=1, source_target_pairs={{0,2},{1,3},{2,0},{3,1},{4,6},{5,7},{6,4},{7,5},{8,10},{9,11},{10,... | collective-permute-start | bytes 786440 | tf_op jit(solution)/shard_map/ppermute | solution.py:94
  9.8 11.3 %collective-permute-start.2 = (bf16[512,256]{0,1:T(8,128)(2,1)S(1)}, bf16[512,256]{0,1:T(8,128)(2,1)S(1)}, u32[]{:S(2)}, u32[]{:S(2)}) collective-permute-start(bf16[512,256]{0,1:T(8,128)(2,1)S(1)} %get-tuple-element.6), channel_id=1, source_target_pairs={{0,3},{1,0},{2,1},{3,2},{4,7},{5,4},{6,5},{7,6},{8,11},{9,8},{10,9... | collective-permute-start | bytes 786440 | tf_op jit(solution)/shard_map/ppermute | solution.py:94
  24.4 31.3 %all-to-all-start = ((bf16[64,2,2112]{2,1,0:T(2,128)(2,1)}), bf16[64,2,2112]{2,1,0:T(2,128)(2,1)S(1)}, u32[]{:S(2)}, u32[]{:S(2)}) async-start(bf16[64,2,2112]{2,1,0:T(2,128)(2,1)} %fusion.14), calls=%async_computation | async-start | bytes 1114112 | tf_op jit(solution)/shard_map/all_to_all | solution.py:114
  56.3 1.3 %copy-start.3 = (bf16[1,1280,1,256]{3,1,2,0:T(8,128)(2,1)S(1)}, bf16[1,1280,1,256]{3,1,2,0:T(8,128)(2,1)}, u32[]{:S(2)}) copy-start(bf16[1,1280,1,256]{3,1,2,0:T(8,128)(2,1)} %param.8) | copy-start | bytes 1966084

commit v13 on v12

--- a/solution.py
+++ b/solution.py
@@ -25,11 +25,12 @@
 
 
 def attention_kernel(block, head_dim, group, len_ref, q_ref, kv_ref, o_ref, vx_ref):
-    prompt = q_ref.shape[1]
+    prompt = kv_ref.shape[0]
     length = len_ref[0]
     scale = head_dim ** (-0.5)
+    step = pl.program_id(1)
 
-    @pl.when(pl.program_id(0) == 0)
+    @pl.when((pl.program_id(0) == 0) & (step == 0))
     def _():
         vx_ref[:, :head_dim] = kv_ref[:, head_dim:]
         vx_ref[:, head_dim:] = jnp.ones((prompt, head_dim), vx_ref.dtype)
@@ -37,23 +38,26 @@
     for index in range(prompt // block):
         row_start = index * block
         keys_used = row_start + block
-        query = jnp.concatenate([q_ref[g, row_start:keys_used, :] for g in range(group)], axis=0)
-        scores = lax.dot_general(
-            query, kv_ref[0:keys_used, 0:head_dim], (((1,), (1,)), ((), ())),
-            preferred_element_type=jnp.float32,
-        )
-        query_index = row_start + lax.broadcasted_iota(jnp.int32, (group * block, 1), 0) % block
-        limit = jnp.minimum(query_index, length - 1)
-        key_index = row_start + lax.broadcasted_iota(jnp.int32, (1, block), 1)
-        diag = jnp.where(key_index <= limit, scores[:, row_start:], jnp.float32(-1e30))
-        scores = jnp.concatenate([scores[:, :row_start], diag], axis=1) if row_start else diag
-        highest = jnp.max(scores, axis=-1, keepdims=True)
-        weights = jnp.exp((scores - highest) * scale).astype(jnp.bfloat16)
-        both = jnp.dot(weights, vx_ref[0:keys_used, :], preferred_element_type=jnp.float32)
-        result = both[:, :head_dim] / both[:, head_dim : head_dim + 1]
-        result = jnp.where(query_index < length, result, jnp.float32(0.0)).astype(o_ref.dtype)
-        for g in range(group):
-            o_ref[g, row_start:keys_used, :] = result[g * block : (g + 1) * block]
+
+        @pl.when(step == index)
+        def _():
+            query = jnp.concatenate([q_ref[g] for g in range(group)], axis=0)
+            scores = lax.dot_general(
+                query, kv_ref[0:keys_used, 0:head_dim], (((1,), (1,)), ((), ())),
+                preferred_element_type=jnp.float32,
+            )
+            query_index = row_start + lax.broadcasted_iota(jnp.int32, (group * block, 1), 0) % block
+            limit = jnp.minimum(query_index, length - 1)
+            key_index = row_start + lax.broadcasted_iota(jnp.int32, (1, block), 1)
+            diag = jnp.where(key_index <= limit, scores[:, row_start:], jnp.float32(-1e30))
+            scores = jnp.concatenate([scores[:, :row_start], diag], axis=1) if row_start else diag
+            highest = jnp.max(scores, axis=-1, keepdims=True)
+            weights = jnp.exp((scores - highest) * scale).astype(jnp.bfloat16)
+            both = jnp.dot(weights, vx_ref[0:keys_used, :], preferred_element_type=jnp.float32)
+            result = both[:, :head_dim] / both[:, head_dim : head_dim + 1]
+            result = jnp.where(query_index < length, result, jnp.float32(0.0)).astype(o_ref.dtype)
+            for g in range(group):
+                o_ref[g] = result[g * block : (g + 1) * block]
 
 
 def attend(heads_first, prompt_kv, length, head_dim, block=256):
@@ -61,19 +65,19 @@
     group = math.gcd(heads, 3)
     grid_spec = pltpu.PrefetchScalarGridSpec(
         num_scalar_prefetch=1,
-        grid=(heads // group,),
+        grid=(heads // group, prompt // block),
         in_specs=[
-            pl.BlockSpec((group, prompt, head_dim), lambda h, lens: (h, 0, 0)),
-            pl.BlockSpec((prompt, 2 * head_dim), lambda h, lens: (0, 0)),
+            pl.BlockSpec((group, block, head_dim), lambda h, i, lens: (h, i, 0)),
+            pl.BlockSpec((prompt, 2 * head_dim), lambda h, i, lens: (0, 0)),
         ],
-        out_specs=pl.BlockSpec((group, prompt, head_dim), lambda h, lens: (h, 0, 0)),
+        out_specs=pl.BlockSpec((group, block, head_dim), lambda h, i, lens: (h, i, 0)),
         scratch_shapes=[pltpu.VMEM((prompt, 2 * head_dim), jnp.bfloat16)],
     )
     return pl.pallas_call(
         functools.partial(attention_kernel, block, head_dim, group),
         grid_spec=grid_spec,
         out_shape=jax.ShapeDtypeStruct((heads, prompt, head_dim), jnp.bfloat16),
-        compiler_params=pltpu.CompilerParams(dimension_semantics=("arbitrary",)),
+        compiler_params=pltpu.CompilerParams(dimension_semantics=("arbitrary", "arbitrary")),
     )(length, heads_first, prompt_kv)
 
 

time: 72.4 us -> 77.9 us (1.076)
  Pallas kernels: 12.5 us -> 17.9 us
    pallas_call x1, Pallas kernels: 12.5 us -> 17.9 us  [attend(): pl.pallas_call(functools.partial(attention_kernel, block, head_dim, group...]
where the time goes in v13:
time: 77.9 us; the launch traced here: 77.5 us
  waiting for transfers between devices  20.9 us (27%)
  starting transfers between devices  18.9 us (24%)
  Pallas kernels  17.9 us (23%)
  matrix products  7.84 us (10%)
  local copies, waits for them, and re-layouts  6.75 us (9%)
  other arithmetic  4.35 us (6%)
  between operations  0.83 us (1%)
    pallas_call x1, Pallas kernels, attend(): pl.pallas_call(functools.partial(attention_kernel, block, head_dim, group...  17.9 us
    all_to_all x1, waiting for transfers between devices, per_device(): got = lax.all_to_all(packet, 'req', split_axis=0, concat_axis=0, tiled=True)  17.4 us
    all_to_all x1, starting transfers between devices, per_device(): got = lax.all_to_all(packet, 'req', split_axis=0, concat_axis=0, tiled=True)  13.2 us
    ppermute x3, starting transfers between devices, per_device(): lax.ppermute(outgoing, 'tp', perm=[(i, (i + shift) % heads) for i in rang...  5.72 us
    dot_general x1, matrix products, per_device(): jnp.einsum('rd,dhc->hrc', image_rows, kv_weight, preferred_element_type=j...  3.72 us
    dynamic_slice x1, local copies, waits for them, and re-layouts, per_device(): own_weight = lax.dynamic_index_in_dim(kv_weight, me, axis=1, keepdims=False)  3.57 us
    ppermute x3, waiting for transfers between devices, per_device(): lax.ppermute(outgoing, 'tp', perm=[(i, (i + shift) % heads) for i in rang...  3.48 us
    dot_general x1, matrix products, per_device(): jnp.dot(match.astype(jnp.bfloat16), got_kv, preferred_element_type=jnp.fl...  1.93 us
  transfers between devices with their start and end apart: 4, of which 2 were waited for; matrix products, arithmetic and copies ran while one was open for 9% of the time, Pallas kernels for 0%

profile of v13, /device:TPU:1, one launch (start us, length us, event | category | flops | bytes accessed | tf_op | source)
XLA Modules:
  0.0 77.5 jit_solution(15210850699124970581)
XLA Ops:
  0.0 1.4 %copy-done = bf16[512,1536]{1,0:T(8,128)(2,1)S(1)} copy-done((bf16[512,1536]{1,0:T(8,128)(2,1)S(1)}, bf16[512,1536]{1,0:T(8,128)(2,1)}, u32[]{:S(2)}) %copy-start) | copy-done | bytes 1572888
  1.4 3.7 %fusion.2 = bf16[4,256,512]{2,1,0:T(8,128)(2,1)S(1)} fusion(bf16[1536,4,256]{2,1,0:T(4,128)(2,1)} %param.13, bf16[512,1536]{1,0:T(8,128)(2,1)S(1)} %copy-done), kind=kOutput, calls=%fused_computation.3 | convolution fusion | flops 1610612736 | bytes 5767168 | tf_op jit(solution)/shard_map/rd,dhc->hrc/dot_general | solution.py:92
  5.2 2.1 %collective-permute-start = (bf16[512,256]{0,1:T(8,128)(2,1)S(1)}, bf16[512,256]{0,1:T(8,128)(2,1)S(1)}, u32[]{:S(2)}, u32[]{:S(2)}) collective-permute-start(bf16[512,256]{0,1:T(8,128)(2,1)S(1)} %get-tuple-element.5), channel_id=1, source_target_pairs={{0,1},{1,2},{2,3},{3,0},{4,5},{5,6},{6,7},{7,4},{8,9},{9,10},{10,1... | collective-permute-start | bytes 786440 | tf_op jit(solution)/shard_map/ppermute | solution.py:98
  7.4 2.5 %collective-permute-start.1 = (bf16[512,256]{0,1:T(8,128)(2,1)S(1)}, bf16[512,256]{0,1:T(8,128)(2,1)S(1)}, u32[]{:S(2)}, u32[]{:S(2)}) collective-permute-start(bf16[512,256]{0,1:T(8,128)(2,1)S(1)} %get-tuple-element.7), channel_id=1, source_target_pairs={{0,2},{1,3},{2,0},{3,1},{4,6},{5,7},{6,4},{7,5},{8,10},{9,11},{10,... | collective-permute-start | bytes 786440 | tf_op jit(solution)/shard_map/ppermute | solution.py:98
  9.8 1.2 %collective-permute-start.2 = (bf16[512,256]{0,1:T(8,128)(2,1)S(1)}, bf16[512,256]{0,1:T(8,128)(2,1)S(1)}, u32[]{:S(2)}, u32[]{:S(2)}) collective-permute-start(bf16[512,256]{0,1:T(8,128)(2,1)S(1)} %get-tuple-element.6), channel_id=1, source_target_pairs={{0,3},{1,0},{2,1},{3,2},{4,7},{5,4},{6,5},{7,6},{8,11},{9,8},{10,9... | collective-permute-start | bytes 786440 | tf_op jit(solution)/shard_map/ppermute | solution.py:98
  11.0 1.2 %reduce-window.6 = s32[64,4,128]{2,0,1:T(8,128)S(1)} reduce-window(s32[64,4,128]{2,0,1:T(8,128)S(1)} %fusion.33, s32[]{:T(128)} %constant.52.clone.1), window={size=1x1x128 pad=0_0x0_0x127_0}, to_apply=%region_0.1 | reduce-window | flops 4161536 | bytes 262148 | tf_op jit(solution)/shard_map/reduce-window
  12.2 0.2 slice_reduce_fusion
  12.6 1.0 %fusion.11 = bf16[1024,2]{0,1:T(2,128)(2,1)S(1)} fusion(s32[512]{0:T(512)S(1)} %multiply_add_fusion, f32[512,1]{0,1:T(1,128)S(1)} %bitcast.57, f32[512,1]{0,1:T(1,128)S(1)} %bitcast.56), kind=kOutput, calls=%fused_computation.15 | convolution fusion | flops 13110272 | bytes 10240 | tf_op jit(solution)/shard_map/dot_general | solution.py:114
  13.6 0.2 copy.16
  14.1 3.6 %constant_dynamic-slice_fusion = bf16[1536,1,256]{2,1,0:T(2,128)(2,1)S(1)} fusion(bf16[1536,4,256]{2,1,0:T(4,128)(2,1)} %param.13, s32[]{:T(128)S(6)} %select_n.33), kind=kLoop, calls=%fused_computation.60 | loop fusion | bytes 1572868 | tf_op jit(solution)/shard_map/jit(dynamic_index_in_dim)/dynamic_slice | solution.py:94
  17.7 3.5 %collective-permute-done.1 = bf16[512,256]{0,1:T(8,128)(2,1)S(1)} collective-permute-done((bf16[512,256]{0,1:T(8,128)(2,1)S(1)}, bf16[512,256]{0,1:T(8,128)(2,1)S(1)}, u32[]{:S(2)}, u32[]{:S(2)}) %collective-permute-start.1) | collective-permute-done | bytes 262176 | tf_op jit(solution)/shard_map/ppermute | solution.py:98
  21.1 0.7 convert_add_fusion
  21.8 0.6 fusion.27
  22.4 0.5 fusion.10
  23.0 1.3 %fusion.14 = bf16[64,2,2112]{2,1,0:T(2,128)(2,1)} fusion(bf16[64,2,16]{2,1,0:T(2,128)(2,1)S(1)} %convert_element_type.47, bf16[64,2,2048]{2,1,0:T(2,128)(2,1)S(1)} %reshape.55), kind=kLoop, calls=%fused_computation.19 | loop fusion | flops 1622016 | bytes 1069056 | tf_op jit(solution)/shard_map/concatenate | solution.py:117
  24.4 13.2 %all-to-all-start = ((bf16[64,2,2112]{2,1,0:T(2,128)(2,1)}), bf16[64,2,2112]{2,1,0:T(2,128)(2,1)S(1)}, u32[]{:S(2)}, u32[]{:S(2)}) async-start(bf16[64,2,2112]{2,1,0:T(2,128)(2,1)} %fusion.14), calls=%async_computation | async-start | bytes 1114112 | tf_op jit(solution)/shard_map/all_to_all | solution.py:118
  38.2 17.4 %all-to-all-done = bf16[64,2,2112]{2,1,0:T(2,128)(2,1)S(1)} async-done(((bf16[64,2,2112]{2,1,0:T(2,128)(2,1)}), bf16[64,2,2112]{2,1,0:T(2,128)(2,1)S(1)}, u32[]{:S(2)}, u32[]{:S(2)}) %all-to-all-start) | async-done | bytes 540704 | tf_op jit(solution)/shard_map/all_to_all | solution.py:118
  55.6 0.4 slice.44
  56.0 0.3 reshape.58
  56.4 0.2 reshape.60
  56.6 0.4 fusion.16
  57.0 0.7 fusion.1
  57.6 1.9 %fusion.6.kv_ref = bf16[1280,256]{1,0:T(8,128)(2,1)} fusion(bf16[1024,256]{1,0:T(8,128)(2,1)S(1)} %reshape.58, s32[1024]{0:T(1024)S(1)} %fusion.16, bf16[1,1280,1,256]{3,1,2,0:T(8,128)(2,1)S(1)} %copy-done.3, pred[1280]{0:T(1024)(128)(4,1)S(1)} %fusion.1), kind=kOutput, calls=%fused_computation.7 | convolution fusion | flops 673054720 | bytes 1840384 | tf_op jit(solution)/shard_map/dot_general | solution.py:124
  59.6 17.9 %shard_map.73 = bf16[6,1280,128]{2,1,0:T(8,128)(2,1)} custom-call(s32[1]{0:T(128)S(6)} %copy.26.len_ref, bf16[6,1280,128]{2,1,0:T(8,128)(2,1)} %bitcast.54, bf16[1280,256]{1,0:T(8,128)(2,1)} %fusion.6.kv_ref), custom_call_target="tpu_custom_call" | custom-call | tf_op jit(solution)/shard_map/pallas_call | solution.py:76
  (22 shorter events, 0.7 us)
Async XLA Ops:
  0.0 1.4 %copy-start = (bf16[512,1536]{1,0:T(8,128)(2,1)S(1)}, bf16[512,1536]{1,0:T(8,128)(2,1)}, u32[]{:S(2)}) copy-start(bf16[512,1536]{1,0:T(8,128)(2,1)} %param.9) | copy-start | bytes 4718596
  5.1 5.8 %copy-start.2 = (s32[512]{0:T(512)S(1)}, s32[512]{0:T(512)}, u32[]{:S(2)}) copy-start(s32[512]{0:T(512)} %param.11) | copy-start | bytes 6148
  5.2 5.8 %copy-start.1 = (s32[512]{0:T(512)S(1)}, s32[512]{0:T(512)}, u32[]{:S(2)}) copy-start(s32[512]{0:T(512)} %param.10) | copy-start | bytes 6148
  5.2 12.4 %collective-permute-start = (bf16[512,256]{0,1:T(8,128)(2,1)S(1)}, bf16[512,256]{0,1:T(8,128)(2,1)S(1)}, u32[]{:S(2)}, u32[]{:S(2)}) collective-permute-start(bf16[512,256]{0,1:T(8,128)(2,1)S(1)} %get-tuple-element.5), channel_id=1, source_target_pairs={{0,1},{1,2},{2,3},{3,0},{4,5},{5,6},{6,7},{7,4},{8,9},{9,10},{10,1... | collective-permute-start | bytes 786440 | tf_op jit(solution)/shard_map/ppermute | solution.py:98
  7.4 13.8 %collective-permute-start.1 = (bf16[512,256]{0,1:T(8,128)(2,1)S(1)}, bf16[512,256]{0,1:T(8,128)(2,1)S(1)}, u32[]{:S(2)}, u32[]{:S(2)}) collective-permute-start(bf16[512,256]{0,1:T(8,128)(2,1)S(1)} %get-tuple-element.7), channel_id=1, source_target_pairs={{0,2},{1,3},{2,0},{3,1},{4,6},{5,7},{6,4},{7,5},{8,10},{9,11},{10,... | collective-permute-start | bytes 786440 | tf_op jit(solution)/shard_map/ppermute | solution.py:98
  9.8 11.3 %collective-permute-start.2 = (bf16[512,256]{0,1:T(8,128)(2,1)S(1)}, bf16[512,256]{0,1:T(8,128)(2,1)S(1)}, u32[]{:S(2)}, u32[]{:S(2)}) collective-permute-start(bf16[512,256]{0,1:T(8,128)(2,1)S(1)} %get-tuple-element.6), channel_id=1, source_target_pairs={{0,3},{1,0},{2,1},{3,2},{4,7},{5,4},{6,5},{7,6},{8,11},{9,8},{10,9... | collective-permute-start | bytes 786440 | tf_op jit(solution)/shard_map/ppermute | solution.py:98
  24.4 31.3 %all-to-all-start = ((bf16[64,2,2112]{2,1,0:T(2,128)(2,1)}), bf16[64,2,2112]{2,1,0:T(2,128)(2,1)S(1)}, u32[]{:S(2)}, u32[]{:S(2)}) async-start(bf16[64,2,2112]{2,1,0:T(2,128)(2,1)} %fusion.14), calls=%async_computation | async-start | bytes 1114112 | tf_op jit(solution)/shard_map/all_to_all | solution.py:118
  56.3 1.3 %copy-start.3 = (bf16[1,1280,1,256]{3,1,2,0:T(8,128)(2,1)S(1)}, bf16[1,1280,1,256]{3,1,2,0:T(8,128)(2,1)}, u32[]{:S(2)}) copy-start(bf16[1,1280,1,256]{3,1,2,0:T(8,128)(2,1)} %param.8) | copy-start | bytes 1966084

commit v14 on v12

--- a/solution.py
+++ b/solution.py
@@ -50,7 +50,7 @@
         highest = jnp.max(scores, axis=-1, keepdims=True)
         weights = jnp.exp((scores - highest) * scale).astype(jnp.bfloat16)
         both = jnp.dot(weights, vx_ref[0:keys_used, :], preferred_element_type=jnp.float32)
-        result = both[:, :head_dim] / both[:, head_dim : head_dim + 1]
+        result = both[:, :head_dim] * (1.0 / both[:, head_dim : head_dim + 1])
         result = jnp.where(query_index < length, result, jnp.float32(0.0)).astype(o_ref.dtype)
         for g in range(group):
             o_ref[g, row_start:keys_used, :] = result[g * block : (g + 1) * block]

time: 72.4 us -> 72.5 us (level)
  no operation moved by 1% of the time
where the time goes in v14:
time: 72.5 us; the launch traced here: 72.2 us
  waiting for transfers between devices  20.9 us (29%)
  starting transfers between devices  18.9 us (26%)
  Pallas kernels  12.6 us (17%)
  matrix products  7.84 us (11%)
  local copies, waits for them, and re-layouts  6.75 us (9%)
  other arithmetic  4.35 us (6%)
  between operations  0.83 us (1%)
    all_to_all x1, waiting for transfers between devices, per_device(): got = lax.all_to_all(packet, 'req', split_axis=0, concat_axis=0, tiled=True)  17.4 us
    all_to_all x1, starting transfers between devices, per_device(): got = lax.all_to_all(packet, 'req', split_axis=0, concat_axis=0, tiled=True)  13.2 us
    pallas_call x1, Pallas kernels, attend(): pl.pallas_call(functools.partial(attention_kernel, block, head_dim, group...  12.6 us
    ppermute x3, starting transfers between devices, per_device(): lax.ppermute(outgoing, 'tp', perm=[(i, (i + shift) % heads) for i in rang...  5.72 us
    dot_general x1, matrix products, per_device(): jnp.einsum('rd,dhc->hrc', image_rows, kv_weight, preferred_element_type=j...  3.72 us
    dynamic_slice x1, local copies, waits for them, and re-layouts, per_device(): own_weight = lax.dynamic_index_in_dim(kv_weight, me, axis=1, keepdims=False)  3.57 us
    ppermute x3, waiting for transfers between devices, per_device(): lax.ppermute(outgoing, 'tp', perm=[(i, (i + shift) % heads) for i in rang...  3.48 us
    dot_general x1, matrix products, per_device(): jnp.dot(match.astype(jnp.bfloat16), got_kv, preferred_element_type=jnp.fl...  1.93 us
  transfers between devices with their start and end apart: 4, of which 2 were waited for; matrix products, arithmetic and copies ran while one was open for 9% of the time, Pallas kernels for 0%

profile of v14, /device:TPU:1, one launch (start us, length us, event | category | flops | bytes accessed | tf_op | source)
XLA Modules:
  0.0 72.2 jit_solution(8266711516862804553)
XLA Ops:
  0.0 1.4 %copy-done = bf16[512,1536]{1,0:T(8,128)(2,1)S(1)} copy-done((bf16[512,1536]{1,0:T(8,128)(2,1)S(1)}, bf16[512,1536]{1,0:T(8,128)(2,1)}, u32[]{:S(2)}) %copy-start) | copy-done | bytes 1572888
  1.4 3.7 %fusion.2 = bf16[4,256,512]{2,1,0:T(8,128)(2,1)S(1)} fusion(bf16[1536,4,256]{2,1,0:T(4,128)(2,1)} %param.13, bf16[512,1536]{1,0:T(8,128)(2,1)S(1)} %copy-done), kind=kOutput, calls=%fused_computation.3 | convolution fusion | flops 1610612736 | bytes 5767168 | tf_op jit(solution)/shard_map/rd,dhc->hrc/dot_general | solution.py:88
  5.2 2.1 %collective-permute-start = (bf16[512,256]{0,1:T(8,128)(2,1)S(1)}, bf16[512,256]{0,1:T(8,128)(2,1)S(1)}, u32[]{:S(2)}, u32[]{:S(2)}) collective-permute-start(bf16[512,256]{0,1:T(8,128)(2,1)S(1)} %get-tuple-element.5), channel_id=1, source_target_pairs={{0,1},{1,2},{2,3},{3,0},{4,5},{5,6},{6,7},{7,4},{8,9},{9,10},{10,1... | collective-permute-start | bytes 786440 | tf_op jit(solution)/shard_map/ppermute | solution.py:94
  7.4 2.5 %collective-permute-start.1 = (bf16[512,256]{0,1:T(8,128)(2,1)S(1)}, bf16[512,256]{0,1:T(8,128)(2,1)S(1)}, u32[]{:S(2)}, u32[]{:S(2)}) collective-permute-start(bf16[512,256]{0,1:T(8,128)(2,1)S(1)} %get-tuple-element.7), channel_id=1, source_target_pairs={{0,2},{1,3},{2,0},{3,1},{4,6},{5,7},{6,4},{7,5},{8,10},{9,11},{10,... | collective-permute-start | bytes 786440 | tf_op jit(solution)/shard_map/ppermute | solution.py:94
  9.8 1.2 %collective-permute-start.2 = (bf16[512,256]{0,1:T(8,128)(2,1)S(1)}, bf16[512,256]{0,1:T(8,128)(2,1)S(1)}, u32[]{:S(2)}, u32[]{:S(2)}) collective-permute-start(bf16[512,256]{0,1:T(8,128)(2,1)S(1)} %get-tuple-element.6), channel_id=1, source_target_pairs={{0,3},{1,0},{2,1},{3,2},{4,7},{5,4},{6,5},{7,6},{8,11},{9,8},{10,9... | collective-permute-start | bytes 786440 | tf_op jit(solution)/shard_map/ppermute | solution.py:94
  11.0 1.2 %reduce-window.6 = s32[64,4,128]{2,0,1:T(8,128)S(1)} reduce-window(s32[64,4,128]{2,0,1:T(8,128)S(1)} %fusion.33, s32[]{:T(128)} %constant.52.clone.1), window={size=1x1x128 pad=0_0x0_0x127_0}, to_apply=%region_0.1 | reduce-window | flops 4161536 | bytes 262148 | tf_op jit(solution)/shard_map/reduce-window
  12.2 0.2 slice_reduce_fusion
  12.6 1.0 %fusion.11 = bf16[1024,2]{0,1:T(2,128)(2,1)S(1)} fusion(s32[512]{0:T(512)S(1)} %multiply_add_fusion, f32[512,1]{0,1:T(1,128)S(1)} %bitcast.57, f32[512,1]{0,1:T(1,128)S(1)} %bitcast.56), kind=kOutput, calls=%fused_computation.15 | convolution fusion | flops 13110272 | bytes 10240 | tf_op jit(solution)/shard_map/dot_general | solution.py:110
  13.6 0.2 copy.16
  14.1 3.6 %constant_dynamic-slice_fusion = bf16[1536,1,256]{2,1,0:T(2,128)(2,1)S(1)} fusion(bf16[1536,4,256]{2,1,0:T(4,128)(2,1)} %param.13, s32[]{:T(128)S(6)} %select_n.33), kind=kLoop, calls=%fused_computation.60 | loop fusion | bytes 1572868 | tf_op jit(solution)/shard_map/jit(dynamic_index_in_dim)/dynamic_slice | solution.py:90
  17.7 3.5 %collective-permute-done.1 = bf16[512,256]{0,1:T(8,128)(2,1)S(1)} collective-permute-done((bf16[512,256]{0,1:T(8,128)(2,1)S(1)}, bf16[512,256]{0,1:T(8,128)(2,1)S(1)}, u32[]{:S(2)}, u32[]{:S(2)}) %collective-permute-start.1) | collective-permute-done | bytes 262176 | tf_op jit(solution)/shard_map/ppermute | solution.py:94
  21.1 0.7 convert_add_fusion
  21.8 0.6 fusion.27
  22.4 0.5 fusion.10
  23.0 1.3 %fusion.14 = bf16[64,2,2112]{2,1,0:T(2,128)(2,1)} fusion(bf16[64,2,16]{2,1,0:T(2,128)(2,1)S(1)} %convert_element_type.47, bf16[64,2,2048]{2,1,0:T(2,128)(2,1)S(1)} %reshape.55), kind=kLoop, calls=%fused_computation.19 | loop fusion | flops 1622016 | bytes 1069056 | tf_op jit(solution)/shard_map/concatenate | solution.py:113
  24.4 13.2 %all-to-all-start = ((bf16[64,2,2112]{2,1,0:T(2,128)(2,1)}), bf16[64,2,2112]{2,1,0:T(2,128)(2,1)S(1)}, u32[]{:S(2)}, u32[]{:S(2)}) async-start(bf16[64,2,2112]{2,1,0:T(2,128)(2,1)} %fusion.14), calls=%async_computation | async-start | bytes 1114112 | tf_op jit(solution)/shard_map/all_to_all | solution.py:114
  38.2 17.4 %all-to-all-done = bf16[64,2,2112]{2,1,0:T(2,128)(2,1)S(1)} async-done(((bf16[64,2,2112]{2,1,0:T(2,128)(2,1)}), bf16[64,2,2112]{2,1,0:T(2,128)(2,1)S(1)}, u32[]{:S(2)}, u32[]{:S(2)}) %all-to-all-start) | async-done | bytes 540704 | tf_op jit(solution)/shard_map/all_to_all | solution.py:114
  55.6 0.4 slice.44
  56.0 0.3 reshape.58
  56.4 0.2 reshape.60
  56.6 0.4 fusion.16
  57.0 0.7 fusion.1
  57.6 1.9 %fusion.6.kv_ref = bf16[1280,256]{1,0:T(8,128)(2,1)} fusion(bf16[1024,256]{1,0:T(8,128)(2,1)S(1)} %reshape.58, s32[1024]{0:T(1024)S(1)} %fusion.16, bf16[1,1280,1,256]{3,1,2,0:T(8,128)(2,1)S(1)} %copy-done.3, pred[1280]{0:T(1024)(128)(4,1)S(1)} %fusion.1), kind=kOutput, calls=%fused_computation.7 | convolution fusion | flops 673054720 | bytes 1840384 | tf_op jit(solution)/shard_map/dot_general | solution.py:120
  59.6 12.6 %shard_map.73 = bf16[6,1280,128]{2,1,0:T(8,128)(2,1)} custom-call(s32[1]{0:T(128)S(6)} %copy.26.len_ref, bf16[6,1280,128]{2,1,0:T(8,128)(2,1)} %bitcast.54, bf16[1280,256]{1,0:T(8,128)(2,1)} %fusion.6.kv_ref), custom_call_target="tpu_custom_call" | custom-call | tf_op jit(solution)/shard_map/pallas_call | solution.py:72
  (22 shorter events, 0.7 us)
Async XLA Ops:
  0.0 1.4 %copy-start = (bf16[512,1536]{1,0:T(8,128)(2,1)S(1)}, bf16[512,1536]{1,0:T(8,128)(2,1)}, u32[]{:S(2)}) copy-start(bf16[512,1536]{1,0:T(8,128)(2,1)} %param.9) | copy-start | bytes 4718596
  5.1 5.8 %copy-start.2 = (s32[512]{0:T(512)S(1)}, s32[512]{0:T(512)}, u32[]{:S(2)}) copy-start(s32[512]{0:T(512)} %param.11) | copy-start | bytes 6148
  5.2 5.8 %copy-start.1 = (s32[512]{0:T(512)S(1)}, s32[512]{0:T(512)}, u32[]{:S(2)}) copy-start(s32[512]{0:T(512)} %param.10) | copy-start | bytes 6148
  5.2 12.4 %collective-permute-start = (bf16[512,256]{0,1:T(8,128)(2,1)S(1)}, bf16[512,256]{0,1:T(8,128)(2,1)S(1)}, u32[]{:S(2)}, u32[]{:S(2)}) collective-permute-start(bf16[512,256]{0,1:T(8,128)(2,1)S(1)} %get-tuple-element.5), channel_id=1, source_target_pairs={{0,1},{1,2},{2,3},{3,0},{4,5},{5,6},{6,7},{7,4},{8,9},{9,10},{10,1... | collective-permute-start | bytes 786440 | tf_op jit(solution)/shard_map/ppermute | solution.py:94
  7.4 13.8 %collective-permute-start.1 = (bf16[512,256]{0,1:T(8,128)(2,1)S(1)}, bf16[512,256]{0,1:T(8,128)(2,1)S(1)}, u32[]{:S(2)}, u32[]{:S(2)}) collective-permute-start(bf16[512,256]{0,1:T(8,128)(2,1)S(1)} %get-tuple-element.7), channel_id=1, source_target_pairs={{0,2},{1,3},{2,0},{3,1},{4,6},{5,7},{6,4},{7,5},{8,10},{9,11},{10,... | collective-permute-start | bytes 786440 | tf_op jit(solution)/shard_map/ppermute | solution.py:94
  9.8 11.3 %collective-permute-start.2 = (bf16[512,256]{0,1:T(8,128)(2,1)S(1)}, bf16[512,256]{0,1:T(8,128)(2,1)S(1)}, u32[]{:S(2)}, u32[]{:S(2)}) collective-permute-start(bf16[512,256]{0,1:T(8,128)(2,1)S(1)} %get-tuple-element.6), channel_id=1, source_target_pairs={{0,3},{1,0},{2,1},{3,2},{4,7},{5,4},{6,5},{7,6},{8,11},{9,8},{10,9... | collective-permute-start | bytes 786440 | tf_op jit(solution)/shard_map/ppermute | solution.py:94
  24.4 31.3 %all-to-all-start = ((bf16[64,2,2112]{2,1,0:T(2,128)(2,1)}), bf16[64,2,2112]{2,1,0:T(2,128)(2,1)S(1)}, u32[]{:S(2)}, u32[]{:S(2)}) async-start(bf16[64,2,2112]{2,1,0:T(2,128)(2,1)} %fusion.14), calls=%async_computation | async-start | bytes 1114112 | tf_op jit(solution)/shard_map/all_to_all | solution.py:114
  56.3 1.3 %copy-start.3 = (bf16[1,1280,1,256]{3,1,2,0:T(8,128)(2,1)S(1)}, bf16[1,1280,1,256]{3,1,2,0:T(8,128)(2,1)}, u32[]{:S(2)}) copy-start(bf16[1,1280,1,256]{3,1,2,0:T(8,128)(2,1)} %param.8) | copy-start | bytes 1966084

commit v15 on v12

--- a/solution.py
+++ b/solution.py
@@ -118,7 +118,10 @@
     places = got_digits[:, 0] * 16 + got_digits[:, 1] - 1
     match = places[None, :] == jnp.arange(prompt, dtype=jnp.int32)[:, None]
     placed = jnp.dot(match.astype(jnp.bfloat16), got_kv, preferred_element_type=jnp.float32)
-    hit = jnp.any(match, axis=1)
+    first = jnp.min(jnp.where(places >= 0, places, prompt))
+    last = jnp.max(places)
+    spot = jnp.arange(prompt, dtype=jnp.int32)
+    hit = (spot >= first) & (spot <= last)
     prompt_kv = jnp.where(hit[:, None], placed.astype(jnp.bfloat16), text_kv[0, :, 0, :])
     heads_first = jnp.transpose(queries[0], (1, 0, 2))
     out = attend(heads_first, prompt_kv, prompt_lengths, head_dim)

time: 72.4 us -> 74.4 us (1.028)
  other arithmetic: 4.35 us -> 6.26 us
    and x0 -> x1, other arithmetic: none -> 1.34 us  [per_device(): hit = (spot >= first) & (spot <= last)]
    reduce_max x0 -> x1, other arithmetic: none -> 0.89 us  [per_device(): last = jnp.max(places)]
where the time goes in v15:
time: 74.4 us; the launch traced here: 74 us
  waiting for transfers between devices  20.9 us (28%)
  starting transfers between devices  18.9 us (25%)
  Pallas kernels  12.5 us (17%)
  matrix products  7.85 us (11%)
  local copies, waits for them, and re-layouts  6.75 us (9%)
  other arithmetic  6.26 us (8%)
  between operations  0.83 us (1%)
    all_to_all x1, waiting for transfers between devices, per_device(): got = lax.all_to_all(packet, 'req', split_axis=0, concat_axis=0, tiled=True)  17.4 us
    all_to_all x1, starting transfers between devices, per_device(): got = lax.all_to_all(packet, 'req', split_axis=0, concat_axis=0, tiled=True)  13.2 us
    pallas_call x1, Pallas kernels, attend(): pl.pallas_call(functools.partial(attention_kernel, block, head_dim, group...  12.5 us
    ppermute x3, starting transfers between devices, per_device(): lax.ppermute(outgoing, 'tp', perm=[(i, (i + shift) % heads) for i in rang...  5.72 us
    dot_general x1, matrix products, per_device(): jnp.einsum('rd,dhc->hrc', image_rows, kv_weight, preferred_element_type=j...  3.72 us
    dynamic_slice x1, local copies, waits for them, and re-layouts, per_device(): own_weight = lax.dynamic_index_in_dim(kv_weight, me, axis=1, keepdims=False)  3.57 us
    ppermute x3, waiting for transfers between devices, per_device(): lax.ppermute(outgoing, 'tp', perm=[(i, (i + shift) % heads) for i in rang...  3.48 us
    dot_general x1, matrix products, per_device(): jnp.dot(match.astype(jnp.bfloat16), got_kv, preferred_element_type=jnp.fl...  1.93 us
  transfers between devices with their start and end apart: 4, of which 2 were waited for; matrix products, arithmetic and copies ran while one was open for 9% of the time, Pallas kernels for 0%

profile of v15, /device:TPU:1, one launch (start us, length us, event | category | flops | bytes accessed | tf_op | source)
XLA Modules:
  0.0 74.0 jit_solution(9561858813817041601)
XLA Ops:
  0.0 1.4 %copy-done = bf16[512,1536]{1,0:T(8,128)(2,1)S(1)} copy-done((bf16[512,1536]{1,0:T(8,128)(2,1)S(1)}, bf16[512,1536]{1,0:T(8,128)(2,1)}, u32[]{:S(2)}) %copy-start) | copy-done | bytes 1572888
  1.4 3.7 %fusion.1 = bf16[4,256,512]{2,1,0:T(8,128)(2,1)S(1)} fusion(bf16[1536,4,256]{2,1,0:T(4,128)(2,1)} %param.13, bf16[512,1536]{1,0:T(8,128)(2,1)S(1)} %copy-done), kind=kOutput, calls=%fused_computation.2 | convolution fusion | flops 1610612736 | bytes 5767168 | tf_op jit(solution)/shard_map/rd,dhc->hrc/dot_general | solution.py:88
  5.2 2.1 %collective-permute-start = (bf16[512,256]{0,1:T(8,128)(2,1)S(1)}, bf16[512,256]{0,1:T(8,128)(2,1)S(1)}, u32[]{:S(2)}, u32[]{:S(2)}) collective-permute-start(bf16[512,256]{0,1:T(8,128)(2,1)S(1)} %get-tuple-element.7), channel_id=1, source_target_pairs={{0,1},{1,2},{2,3},{3,0},{4,5},{5,6},{6,7},{7,4},{8,9},{9,10},{10,1... | collective-permute-start | bytes 786440 | tf_op jit(solution)/shard_map/ppermute | solution.py:94
  7.4 2.5 %collective-permute-start.1 = (bf16[512,256]{0,1:T(8,128)(2,1)S(1)}, bf16[512,256]{0,1:T(8,128)(2,1)S(1)}, u32[]{:S(2)}, u32[]{:S(2)}) collective-permute-start(bf16[512,256]{0,1:T(8,128)(2,1)S(1)} %get-tuple-element.9), channel_id=1, source_target_pairs={{0,2},{1,3},{2,0},{3,1},{4,6},{5,7},{6,4},{7,5},{8,10},{9,11},{10,... | collective-permute-start | bytes 786440 | tf_op jit(solution)/shard_map/ppermute | solution.py:94
  9.8 1.2 %collective-permute-start.2 = (bf16[512,256]{0,1:T(8,128)(2,1)S(1)}, bf16[512,256]{0,1:T(8,128)(2,1)S(1)}, u32[]{:S(2)}, u32[]{:S(2)}) collective-permute-start(bf16[512,256]{0,1:T(8,128)(2,1)S(1)} %get-tuple-element.8), channel_id=1, source_target_pairs={{0,3},{1,0},{2,1},{3,2},{4,7},{5,4},{6,5},{7,6},{8,11},{9,8},{10,9... | collective-permute-start | bytes 786440 | tf_op jit(solution)/shard_map/ppermute | solution.py:94
  11.0 1.2 %reduce-window.6 = s32[64,4,128]{2,0,1:T(8,128)S(1)} reduce-window(s32[64,4,128]{2,0,1:T(8,128)S(1)} %fusion.31, s32[]{:T(128)} %constant.55.clone.1), window={size=1x1x128 pad=0_0x0_0x127_0}, to_apply=%region_0.1 | reduce-window | flops 4161536 | bytes 262148 | tf_op jit(solution)/shard_map/reduce-window
  12.2 0.2 slice_reduce_fusion
  12.6 1.0 %fusion.10 = bf16[1024,2]{0,1:T(2,128)(2,1)S(1)} fusion(s32[512]{0:T(512)S(1)} %multiply_add_fusion, f32[512,1]{0,1:T(1,128)S(1)} %bitcast.57, f32[512,1]{0,1:T(1,128)S(1)} %bitcast.56), kind=kOutput, calls=%fused_computation.14 | convolution fusion | flops 13110272 | bytes 10240 | tf_op jit(solution)/shard_map/dot_general | solution.py:110
  13.6 0.2 copy.12
  14.1 3.6 %constant_dynamic-slice_fusion = bf16[1536,1,256]{2,1,0:T(2,128)(2,1)S(1)} fusion(bf16[1536,4,256]{2,1,0:T(4,128)(2,1)} %param.13, s32[]{:T(128)S(6)} %select_n.37), kind=kLoop, calls=%fused_computation.65 | loop fusion | bytes 1572868 | tf_op jit(solution)/shard_map/jit(dynamic_index_in_dim)/dynamic_slice | solution.py:90
  17.7 3.5 %collective-permute-done.1 = bf16[512,256]{0,1:T(8,128)(2,1)S(1)} collective-permute-done((bf16[512,256]{0,1:T(8,128)(2,1)S(1)}, bf16[512,256]{0,1:T(8,128)(2,1)S(1)}, u32[]{:S(2)}, u32[]{:S(2)}) %collective-permute-start.1) | collective-permute-done | bytes 262176 | tf_op jit(solution)/shard_map/ppermute | solution.py:94
  21.1 0.7 convert_add_fusion
  21.8 0.6 fusion.25
  22.4 0.5 fusion.9
  23.0 1.3 %fusion.13 = bf16[64,2,2112]{2,1,0:T(2,128)(2,1)} fusion(bf16[64,2,16]{2,1,0:T(2,128)(2,1)S(1)} %convert_element_type.47, bf16[64,2,2048]{2,1,0:T(2,128)(2,1)S(1)} %reshape.61), kind=kLoop, calls=%fused_computation.18 | loop fusion | flops 1622016 | bytes 1069056 | tf_op jit(solution)/shard_map/concatenate | solution.py:113
  24.4 13.2 %all-to-all-start = ((bf16[64,2,2112]{2,1,0:T(2,128)(2,1)}), bf16[64,2,2112]{2,1,0:T(2,128)(2,1)S(1)}, u32[]{:S(2)}, u32[]{:S(2)}) async-start(bf16[64,2,2112]{2,1,0:T(2,128)(2,1)} %fusion.13), calls=%async_computation | async-start | bytes 1114112 | tf_op jit(solution)/shard_map/all_to_all | solution.py:114
  38.2 17.4 %all-to-all-done = bf16[64,2,2112]{2,1,0:T(2,128)(2,1)S(1)} async-done(((bf16[64,2,2112]{2,1,0:T(2,128)(2,1)}), bf16[64,2,2112]{2,1,0:T(2,128)(2,1)S(1)}, u32[]{:S(2)}, u32[]{:S(2)}) %all-to-all-start) | async-done | bytes 540704 | tf_op jit(solution)/shard_map/all_to_all | solution.py:114
  55.9 0.9 %fusion.32 = (s32[]{:T(128)}, s32[1024]{0:T(1024)S(1)}) fusion(s32[1024,2]{1,0:T(8,128)S(1)} %reshape.66), kind=kLoop, calls=%fused_computation.51 | loop fusion | flops 4095 | bytes 12292 | tf_op jit(solution)/shard_map/reduce_max | solution.py:122
  56.8 0.7 fusion.35
  57.5 0.4 slice.44
  57.9 0.3 reshape.64
  58.2 1.3 %fusion.34 = pred[1280]{0:T(1024)(128)(4,1)S(1)} fusion(s32[]{:T(128)} %get-tuple-element.5, s32[]{:T(128)} %fusion.35), kind=kLoop, calls=%fused_computation.57 | loop fusion | flops 3840 | bytes 1288 | tf_op jit(solution)/shard_map/and | solution.py:124
  59.6 1.9 %fusion.5.kv_ref = bf16[1280,256]{1,0:T(8,128)(2,1)} fusion(bf16[1024,256]{1,0:T(8,128)(2,1)S(1)} %reshape.64, s32[1024]{0:T(1024)S(1)} %get-tuple-element.6, bf16[1,1280,1,256]{3,1,2,0:T(8,128)(2,1)S(1)} %copy-done.3, pred[1280]{0:T(1024)(128)(4,1)S(1)} %fusion.34), kind=kOutput, calls=%fused_computation.6 | convolution fusion | flops 673054720 | bytes 1840384 | tf_op jit(solution)/shard_map/dot_general | solution.py:120
  61.5 12.5 %shard_map.73 = bf16[6,1280,128]{2,1,0:T(8,128)(2,1)} custom-call(s32[1]{0:T(128)S(6)} %copy.22.len_ref, bf16[6,1280,128]{2,1,0:T(8,128)(2,1)} %bitcast.54, bf16[1280,256]{1,0:T(8,128)(2,1)} %fusion.5.kv_ref), custom_call_target="tpu_custom_call" | custom-call | tf_op jit(solution)/shard_map/pallas_call | solution.py:72
  (23 shorter events, 0.9 us)
Async XLA Ops:
  0.0 1.4 %copy-start = (bf16[512,1536]{1,0:T(8,128)(2,1)S(1)}, bf16[512,1536]{1,0:T(8,128)(2,1)}, u32[]{:S(2)}) copy-start(bf16[512,1536]{1,0:T(8,128)(2,1)} %param.9) | copy-start | bytes 4718596
  5.1 5.8 %copy-start.2 = (s32[512]{0:T(512)S(1)}, s32[512]{0:T(512)}, u32[]{:S(2)}) copy-start(s32[512]{0:T(512)} %param.11) | copy-start | bytes 6148
  5.2 5.8 %copy-start.1 = (s32[512]{0:T(512)S(1)}, s32[512]{0:T(512)}, u32[]{:S(2)}) copy-start(s32[512]{0:T(512)} %param.10) | copy-start | bytes 6148
  5.2 12.4 %collective-permute-start = (bf16[512,256]{0,1:T(8,128)(2,1)S(1)}, bf16[512,256]{0,1:T(8,128)(2,1)S(1)}, u32[]{:S(2)}, u32[]{:S(2)}) collective-permute-start(bf16[512,256]{0,1:T(8,128)(2,1)S(1)} %get-tuple-element.7), channel_id=1, source_target_pairs={{0,1},{1,2},{2,3},{3,0},{4,5},{5,6},{6,7},{7,4},{8,9},{9,10},{10,1... | collective-permute-start | bytes 786440 | tf_op jit(solution)/shard_map/ppermute | solution.py:94
  7.4 13.8 %collective-permute-start.1 = (bf16[512,256]{0,1:T(8,128)(2,1)S(1)}, bf16[512,256]{0,1:T(8,128)(2,1)S(1)}, u32[]{:S(2)}, u32[]{:S(2)}) collective-permute-start(bf16[512,256]{0,1:T(8,128)(2,1)S(1)} %get-tuple-element.9), channel_id=1, source_target_pairs={{0,2},{1,3},{2,0},{3,1},{4,6},{5,7},{6,4},{7,5},{8,10},{9,11},{10,... | collective-permute-start | bytes 786440 | tf_op jit(solution)/shard_map/ppermute | solution.py:94
  9.8 11.3 %collective-permute-start.2 = (bf16[512,256]{0,1:T(8,128)(2,1)S(1)}, bf16[512,256]{0,1:T(8,128)(2,1)S(1)}, u32[]{:S(2)}, u32[]{:S(2)}) collective-permute-start(bf16[512,256]{0,1:T(8,128)(2,1)S(1)} %get-tuple-element.8), channel_id=1, source_target_pairs={{0,3},{1,0},{2,1},{3,2},{4,7},{5,4},{6,5},{7,6},{8,11},{9,8},{10,9... | collective-permute-start | bytes 786440 | tf_op jit(solution)/shard_map/ppermute | solution.py:94
  24.4 31.3 %all-to-all-start = ((bf16[64,2,2112]{2,1,0:T(2,128)(2,1)}), bf16[64,2,2112]{2,1,0:T(2,128)(2,1)S(1)}, u32[]{:S(2)}, u32[]{:S(2)}) async-start(bf16[64,2,2112]{2,1,0:T(2,128)(2,1)} %fusion.13), calls=%async_computation | async-start | bytes 1114112 | tf_op jit(solution)/shard_map/all_to_all | solution.py:114
  55.9 3.7 %copy-start.3 = (bf16[1,1280,1,256]{3,1,2,0:T(8,128)(2,1)S(1)}, bf16[1,1280,1,256]{3,1,2,0:T(8,128)(2,1)}, u32[]{:S(2)}) copy-start(bf16[1,1280,1,256]{3,1,2,0:T(8,128)(2,1)} %param.8) | copy-start | bytes 1966084

commit v16 on v12

--- a/solution.py
+++ b/solution.py
@@ -46,9 +46,15 @@
         limit = jnp.minimum(query_index, length - 1)
         key_index = row_start + lax.broadcasted_iota(jnp.int32, (1, block), 1)
         diag = jnp.where(key_index <= limit, scores[:, row_start:], jnp.float32(-1e30))
-        scores = jnp.concatenate([scores[:, :row_start], diag], axis=1) if row_start else diag
-        highest = jnp.max(scores, axis=-1, keepdims=True)
-        weights = jnp.exp((scores - highest) * scale).astype(jnp.bfloat16)
+        highest = jnp.max(diag, axis=-1, keepdims=True)
+        if row_start:
+            off = scores[:, :row_start]
+            highest = jnp.maximum(highest, jnp.max(off, axis=-1, keepdims=True))
+        weights = jnp.exp((diag - highest) * scale).astype(jnp.bfloat16)
+        if row_start:
+            weights = jnp.concatenate(
+                [jnp.exp((off - highest) * scale).astype(jnp.bfloat16), weights], axis=1
+            )
         both = jnp.dot(weights, vx_ref[0:keys_used, :], preferred_element_type=jnp.float32)
         result = both[:, :head_dim] / both[:, head_dim : head_dim + 1]
         result = jnp.where(query_index < length, result, jnp.float32(0.0)).astype(o_ref.dtype)

time: 72.4 us -> 72.4 us (level)
  no operation moved by 1% of the time
where the time goes in v16:
time: 72.4 us; the launch traced here: 72.1 us
  waiting for transfers between devices  20.9 us (29%)
  starting transfers between devices  18.9 us (26%)
  Pallas kernels  12.5 us (17%)
  matrix products  7.84 us (11%)
  local copies, waits for them, and re-layouts  6.75 us (9%)
  other arithmetic  4.35 us (6%)
  between operations  0.83 us (1%)
    all_to_all x1, waiting for transfers between devices, per_device(): got = lax.all_to_all(packet, 'req', split_axis=0, concat_axis=0, tiled=True)  17.4 us
    all_to_all x1, starting transfers between devices, per_device(): got = lax.all_to_all(packet, 'req', split_axis=0, concat_axis=0, tiled=True)  13.2 us
    pallas_call x1, Pallas kernels, attend(): pl.pallas_call(functools.partial(attention_kernel, block, head_dim, group...  12.5 us
    ppermute x3, starting transfers between devices, per_device(): lax.ppermute(outgoing, 'tp', perm=[(i, (i + shift) % heads) for i in rang...  5.72 us
    dot_general x1, matrix products, per_device(): jnp.einsum('rd,dhc->hrc', image_rows, kv_weight, preferred_element_type=j...  3.72 us
    dynamic_slice x1, local copies, waits for them, and re-layouts, per_device(): own_weight = lax.dynamic_index_in_dim(kv_weight, me, axis=1, keepdims=False)  3.57 us
    ppermute x3, waiting for transfers between devices, per_device(): lax.ppermute(outgoing, 'tp', perm=[(i, (i + shift) % heads) for i in rang...  3.48 us
    dot_general x1, matrix products, per_device(): jnp.dot(match.astype(jnp.bfloat16), got_kv, preferred_element_type=jnp.fl...  1.93 us
  transfers between devices with their start and end apart: 4, of which 2 were waited for; matrix products, arithmetic and copies ran while one was open for 9% of the time, Pallas kernels for 0%

profile of v16, /device:TPU:1, one launch (start us, length us, event | category | flops | bytes accessed | tf_op | source)
XLA Modules:
  0.0 72.1 jit_solution(14040199415267758183)
XLA Ops:
  0.0 1.4 %copy-done = bf16[512,1536]{1,0:T(8,128)(2,1)S(1)} copy-done((bf16[512,1536]{1,0:T(8,128)(2,1)S(1)}, bf16[512,1536]{1,0:T(8,128)(2,1)}, u32[]{:S(2)}) %copy-start) | copy-done | bytes 1572888
  1.4 3.7 %fusion.2 = bf16[4,256,512]{2,1,0:T(8,128)(2,1)S(1)} fusion(bf16[1536,4,256]{2,1,0:T(4,128)(2,1)} %param.13, bf16[512,1536]{1,0:T(8,128)(2,1)S(1)} %copy-done), kind=kOutput, calls=%fused_computation.3 | convolution fusion | flops 1610612736 | bytes 5767168 | tf_op jit(solution)/shard_map/rd,dhc->hrc/dot_general | solution.py:94
  5.2 2.1 %collective-permute-start = (bf16[512,256]{0,1:T(8,128)(2,1)S(1)}, bf16[512,256]{0,1:T(8,128)(2,1)S(1)}, u32[]{:S(2)}, u32[]{:S(2)}) collective-permute-start(bf16[512,256]{0,1:T(8,128)(2,1)S(1)} %get-tuple-element.5), channel_id=1, source_target_pairs={{0,1},{1,2},{2,3},{3,0},{4,5},{5,6},{6,7},{7,4},{8,9},{9,10},{10,1... | collective-permute-start | bytes 786440 | tf_op jit(solution)/shard_map/ppermute | solution.py:100
  7.4 2.5 %collective-permute-start.1 = (bf16[512,256]{0,1:T(8,128)(2,1)S(1)}, bf16[512,256]{0,1:T(8,128)(2,1)S(1)}, u32[]{:S(2)}, u32[]{:S(2)}) collective-permute-start(bf16[512,256]{0,1:T(8,128)(2,1)S(1)} %get-tuple-element.7), channel_id=1, source_target_pairs={{0,2},{1,3},{2,0},{3,1},{4,6},{5,7},{6,4},{7,5},{8,10},{9,11},{10,... | collective-permute-start | bytes 786440 | tf_op jit(solution)/shard_map/ppermute | solution.py:100
  9.8 1.2 %collective-permute-start.2 = (bf16[512,256]{0,1:T(8,128)(2,1)S(1)}, bf16[512,256]{0,1:T(8,128)(2,1)S(1)}, u32[]{:S(2)}, u32[]{:S(2)}) collective-permute-start(bf16[512,256]{0,1:T(8,128)(2,1)S(1)} %get-tuple-element.6), channel_id=1, source_target_pairs={{0,3},{1,0},{2,1},{3,2},{4,7},{5,4},{6,5},{7,6},{8,11},{9,8},{10,9... | collective-permute-start | bytes 786440 | tf_op jit(solution)/shard_map/ppermute | solution.py:100
  11.0 1.2 %reduce-window.6 = s32[64,4,128]{2,0,1:T(8,128)S(1)} reduce-window(s32[64,4,128]{2,0,1:T(8,128)S(1)} %fusion.33, s32[]{:T(128)} %constant.52.clone.1), window={size=1x1x128 pad=0_0x0_0x127_0}, to_apply=%region_0.1 | reduce-window | flops 4161536 | bytes 262148 | tf_op jit(solution)/shard_map/reduce-window
  12.2 0.2 slice_reduce_fusion
  12.6 1.0 %fusion.11 = bf16[1024,2]{0,1:T(2,128)(2,1)S(1)} fusion(s32[512]{0:T(512)S(1)} %multiply_add_fusion, f32[512,1]{0,1:T(1,128)S(1)} %bitcast.57, f32[512,1]{0,1:T(1,128)S(1)} %bitcast.56), kind=kOutput, calls=%fused_computation.15 | convolution fusion | flops 13110272 | bytes 10240 | tf_op jit(solution)/shard_map/dot_general | solution.py:116
  13.6 0.2 copy.16
  14.1 3.6 %constant_dynamic-slice_fusion = bf16[1536,1,256]{2,1,0:T(2,128)(2,1)S(1)} fusion(bf16[1536,4,256]{2,1,0:T(4,128)(2,1)} %param.13, s32[]{:T(128)S(6)} %select_n.33), kind=kLoop, calls=%fused_computation.60 | loop fusion | bytes 1572868 | tf_op jit(solution)/shard_map/jit(dynamic_index_in_dim)/dynamic_slice | solution.py:96
  17.7 3.5 %collective-permute-done.1 = bf16[512,256]{0,1:T(8,128)(2,1)S(1)} collective-permute-done((bf16[512,256]{0,1:T(8,128)(2,1)S(1)}, bf16[512,256]{0,1:T(8,128)(2,1)S(1)}, u32[]{:S(2)}, u32[]{:S(2)}) %collective-permute-start.1) | collective-permute-done | bytes 262176 | tf_op jit(solution)/shard_map/ppermute | solution.py:100
  21.1 0.7 convert_add_fusion
  21.8 0.6 fusion.27
  22.4 0.5 fusion.10
  23.0 1.3 %fusion.14 = bf16[64,2,2112]{2,1,0:T(2,128)(2,1)} fusion(bf16[64,2,16]{2,1,0:T(2,128)(2,1)S(1)} %convert_element_type.47, bf16[64,2,2048]{2,1,0:T(2,128)(2,1)S(1)} %reshape.55), kind=kLoop, calls=%fused_computation.19 | loop fusion | flops 1622016 | bytes 1069056 | tf_op jit(solution)/shard_map/concatenate | solution.py:119
  24.4 13.2 %all-to-all-start = ((bf16[64,2,2112]{2,1,0:T(2,128)(2,1)}), bf16[64,2,2112]{2,1,0:T(2,128)(2,1)S(1)}, u32[]{:S(2)}, u32[]{:S(2)}) async-start(bf16[64,2,2112]{2,1,0:T(2,128)(2,1)} %fusion.14), calls=%async_computation | async-start | bytes 1114112 | tf_op jit(solution)/shard_map/all_to_all | solution.py:120
  38.2 17.4 %all-to-all-done = bf16[64,2,2112]{2,1,0:T(2,128)(2,1)S(1)} async-done(((bf16[64,2,2112]{2,1,0:T(2,128)(2,1)}), bf16[64,2,2112]{2,1,0:T(2,128)(2,1)S(1)}, u32[]{:S(2)}, u32[]{:S(2)}) %all-to-all-start) | async-done | bytes 540704 | tf_op jit(solution)/shard_map/all_to_all | solution.py:120
  55.6 0.4 slice.44
  56.0 0.3 reshape.58
  56.4 0.2 reshape.60
  56.6 0.4 fusion.16
  57.0 0.7 fusion.1
  57.6 1.9 %fusion.6.kv_ref = bf16[1280,256]{1,0:T(8,128)(2,1)} fusion(bf16[1024,256]{1,0:T(8,128)(2,1)S(1)} %reshape.58, s32[1024]{0:T(1024)S(1)} %fusion.16, bf16[1,1280,1,256]{3,1,2,0:T(8,128)(2,1)S(1)} %copy-done.3, pred[1280]{0:T(1024)(128)(4,1)S(1)} %fusion.1), kind=kOutput, calls=%fused_computation.7 | convolution fusion | flops 673054720 | bytes 1840384 | tf_op jit(solution)/shard_map/dot_general | solution.py:126
  59.6 12.5 %shard_map.73 = bf16[6,1280,128]{2,1,0:T(8,128)(2,1)} custom-call(s32[1]{0:T(128)S(6)} %copy.26.len_ref, bf16[6,1280,128]{2,1,0:T(8,128)(2,1)} %bitcast.54, bf16[1280,256]{1,0:T(8,128)(2,1)} %fusion.6.kv_ref), custom_call_target="tpu_custom_call" | custom-call | tf_op jit(solution)/shard_map/pallas_call | solution.py:78
  (22 shorter events, 0.7 us)
Async XLA Ops:
  0.0 1.4 %copy-start = (bf16[512,1536]{1,0:T(8,128)(2,1)S(1)}, bf16[512,1536]{1,0:T(8,128)(2,1)}, u32[]{:S(2)}) copy-start(bf16[512,1536]{1,0:T(8,128)(2,1)} %param.9) | copy-start | bytes 4718596
  5.1 5.8 %copy-start.2 = (s32[512]{0:T(512)S(1)}, s32[512]{0:T(512)}, u32[]{:S(2)}) copy-start(s32[512]{0:T(512)} %param.11) | copy-start | bytes 6148
  5.2 5.8 %copy-start.1 = (s32[512]{0:T(512)S(1)}, s32[512]{0:T(512)}, u32[]{:S(2)}) copy-start(s32[512]{0:T(512)} %param.10) | copy-start | bytes 6148
  5.2 12.4 %collective-permute-start = (bf16[512,256]{0,1:T(8,128)(2,1)S(1)}, bf16[512,256]{0,1:T(8,128)(2,1)S(1)}, u32[]{:S(2)}, u32[]{:S(2)}) collective-permute-start(bf16[512,256]{0,1:T(8,128)(2,1)S(1)} %get-tuple-element.5), channel_id=1, source_target_pairs={{0,1},{1,2},{2,3},{3,0},{4,5},{5,6},{6,7},{7,4},{8,9},{9,10},{10,1... | collective-permute-start | bytes 786440 | tf_op jit(solution)/shard_map/ppermute | solution.py:100
  7.4 13.8 %collective-permute-start.1 = (bf16[512,256]{0,1:T(8,128)(2,1)S(1)}, bf16[512,256]{0,1:T(8,128)(2,1)S(1)}, u32[]{:S(2)}, u32[]{:S(2)}) collective-permute-start(bf16[512,256]{0,1:T(8,128)(2,1)S(1)} %get-tuple-element.7), channel_id=1, source_target_pairs={{0,2},{1,3},{2,0},{3,1},{4,6},{5,7},{6,4},{7,5},{8,10},{9,11},{10,... | collective-permute-start | bytes 786440 | tf_op jit(solution)/shard_map/ppermute | solution.py:100
  9.8 11.3 %collective-permute-start.2 = (bf16[512,256]{0,1:T(8,128)(2,1)S(1)}, bf16[512,256]{0,1:T(8,128)(2,1)S(1)}, u32[]{:S(2)}, u32[]{:S(2)}) collective-permute-start(bf16[512,256]{0,1:T(8,128)(2,1)S(1)} %get-tuple-element.6), channel_id=1, source_target_pairs={{0,3},{1,0},{2,1},{3,2},{4,7},{5,4},{6,5},{7,6},{8,11},{9,8},{10,9... | collective-permute-start | bytes 786440 | tf_op jit(solution)/shard_map/ppermute | solution.py:100
  24.4 31.3 %all-to-all-start = ((bf16[64,2,2112]{2,1,0:T(2,128)(2,1)}), bf16[64,2,2112]{2,1,0:T(2,128)(2,1)S(1)}, u32[]{:S(2)}, u32[]{:S(2)}) async-start(bf16[64,2,2112]{2,1,0:T(2,128)(2,1)} %fusion.14), calls=%async_computation | async-start | bytes 1114112 | tf_op jit(solution)/shard_map/all_to_all | solution.py:120
  56.3 1.3 %copy-start.3 = (bf16[1,1280,1,256]{3,1,2,0:T(8,128)(2,1)S(1)}, bf16[1,1280,1,256]{3,1,2,0:T(8,128)(2,1)}, u32[]{:S(2)}) copy-start(bf16[1,1280,1,256]{3,1,2,0:T(8,128)(2,1)} %param.8) | copy-start | bytes 1966084

commit v17 on v16

--- a/solution.py
+++ b/solution.py
@@ -56,7 +56,7 @@
                 [jnp.exp((off - highest) * scale).astype(jnp.bfloat16), weights], axis=1
             )
         both = jnp.dot(weights, vx_ref[0:keys_used, :], preferred_element_type=jnp.float32)
-        result = both[:, :head_dim] / both[:, head_dim : head_dim + 1]
+        result = both[:, :head_dim] * (1.0 / both[:, head_dim : head_dim + 1])
         result = jnp.where(query_index < length, result, jnp.float32(0.0)).astype(o_ref.dtype)
         for g in range(group):
             o_ref[g, row_start:keys_used, :] = result[g * block : (g + 1) * block]

time: 72.4 us -> 72.4 us (level)
  no operation moved by 1% of the time
where the time goes in v17:
time: 72.4 us; the launch traced here: 72.1 us
  waiting for transfers between devices  20.9 us (29%)
  starting transfers between devices  18.9 us (26%)
  Pallas kernels  12.5 us (17%)
  matrix products  7.84 us (11%)
  local copies, waits for them, and re-layouts  6.75 us (9%)
  other arithmetic  4.35 us (6%)
  between operations  0.83 us (1%)
    all_to_all x1, waiting for transfers between devices, per_device(): got = lax.all_to_all(packet, 'req', split_axis=0, concat_axis=0, tiled=True)  17.4 us
    all_to_all x1, starting transfers between devices, per_device(): got = lax.all_to_all(packet, 'req', split_axis=0, concat_axis=0, tiled=True)  13.2 us
    pallas_call x1, Pallas kernels, attend(): pl.pallas_call(functools.partial(attention_kernel, block, head_dim, group...  12.5 us
    ppermute x3, starting transfers between devices, per_device(): lax.ppermute(outgoing, 'tp', perm=[(i, (i + shift) % heads) for i in rang...  5.72 us
    dot_general x1, matrix products, per_device(): jnp.einsum('rd,dhc->hrc', image_rows, kv_weight, preferred_element_type=j...  3.72 us
    dynamic_slice x1, local copies, waits for them, and re-layouts, per_device(): own_weight = lax.dynamic_index_in_dim(kv_weight, me, axis=1, keepdims=False)  3.57 us
    ppermute x3, waiting for transfers between devices, per_device(): lax.ppermute(outgoing, 'tp', perm=[(i, (i + shift) % heads) for i in rang...  3.48 us
    dot_general x1, matrix products, per_device(): jnp.dot(match.astype(jnp.bfloat16), got_kv, preferred_element_type=jnp.fl...  1.93 us
  transfers between devices with their start and end apart: 4, of which 2 were waited for; matrix products, arithmetic and copies ran while one was open for 9% of the time, Pallas kernels for 0%

profile of v17, /device:TPU:1, one launch (start us, length us, event | category | flops | bytes accessed | tf_op | source)
XLA Modules:
  0.0 72.1 jit_solution(23565395527734167)
XLA Ops:
  0.0 1.4 %copy-done = bf16[512,1536]{1,0:T(8,128)(2,1)S(1)} copy-done((bf16[512,1536]{1,0:T(8,128)(2,1)S(1)}, bf16[512,1536]{1,0:T(8,128)(2,1)}, u32[]{:S(2)}) %copy-start) | copy-done | bytes 1572888
  1.4 3.7 %fusion.2 = bf16[4,256,512]{2,1,0:T(8,128)(2,1)S(1)} fusion(bf16[1536,4,256]{2,1,0:T(4,128)(2,1)} %param.13, bf16[512,1536]{1,0:T(8,128)(2,1)S(1)} %copy-done), kind=kOutput, calls=%fused_computation.3 | convolution fusion | flops 1610612736 | bytes 5767168 | tf_op jit(solution)/shard_map/rd,dhc->hrc/dot_general | solution.py:94
  5.2 2.1 %collective-permute-start = (bf16[512,256]{0,1:T(8,128)(2,1)S(1)}, bf16[512,256]{0,1:T(8,128)(2,1)S(1)}, u32[]{:S(2)}, u32[]{:S(2)}) collective-permute-start(bf16[512,256]{0,1:T(8,128)(2,1)S(1)} %get-tuple-element.5), channel_id=1, source_target_pairs={{0,1},{1,2},{2,3},{3,0},{4,5},{5,6},{6,7},{7,4},{8,9},{9,10},{10,1... | collective-permute-start | bytes 786440 | tf_op jit(solution)/shard_map/ppermute | solution.py:100
  7.4 2.5 %collective-permute-start.1 = (bf16[512,256]{0,1:T(8,128)(2,1)S(1)}, bf16[512,256]{0,1:T(8,128)(2,1)S(1)}, u32[]{:S(2)}, u32[]{:S(2)}) collective-permute-start(bf16[512,256]{0,1:T(8,128)(2,1)S(1)} %get-tuple-element.7), channel_id=1, source_target_pairs={{0,2},{1,3},{2,0},{3,1},{4,6},{5,7},{6,4},{7,5},{8,10},{9,11},{10,... | collective-permute-start | bytes 786440 | tf_op jit(solution)/shard_map/ppermute | solution.py:100
  9.8 1.2 %collective-permute-start.2 = (bf16[512,256]{0,1:T(8,128)(2,1)S(1)}, bf16[512,256]{0,1:T(8,128)(2,1)S(1)}, u32[]{:S(2)}, u32[]{:S(2)}) collective-permute-start(bf16[512,256]{0,1:T(8,128)(2,1)S(1)} %get-tuple-element.6), channel_id=1, source_target_pairs={{0,3},{1,0},{2,1},{3,2},{4,7},{5,4},{6,5},{7,6},{8,11},{9,8},{10,9... | collective-permute-start | bytes 786440 | tf_op jit(solution)/shard_map/ppermute | solution.py:100
  11.0 1.2 %reduce-window.6 = s32[64,4,128]{2,0,1:T(8,128)S(1)} reduce-window(s32[64,4,128]{2,0,1:T(8,128)S(1)} %fusion.33, s32[]{:T(128)} %constant.52.clone.1), window={size=1x1x128 pad=0_0x0_0x127_0}, to_apply=%region_0.1 | reduce-window | flops 4161536 | bytes 262148 | tf_op jit(solution)/shard_map/reduce-window
  12.2 0.2 slice_reduce_fusion
  12.6 1.0 %fusion.11 = bf16[1024,2]{0,1:T(2,128)(2,1)S(1)} fusion(s32[512]{0:T(512)S(1)} %multiply_add_fusion, f32[512,1]{0,1:T(1,128)S(1)} %bitcast.57, f32[512,1]{0,1:T(1,128)S(1)} %bitcast.56), kind=kOutput, calls=%fused_computation.15 | convolution fusion | flops 13110272 | bytes 10240 | tf_op jit(solution)/shard_map/dot_general | solution.py:116
  13.6 0.2 copy.16
  14.1 3.6 %constant_dynamic-slice_fusion = bf16[1536,1,256]{2,1,0:T(2,128)(2,1)S(1)} fusion(bf16[1536,4,256]{2,1,0:T(4,128)(2,1)} %param.13, s32[]{:T(128)S(6)} %select_n.33), kind=kLoop, calls=%fused_computation.60 | loop fusion | bytes 1572868 | tf_op jit(solution)/shard_map/jit(dynamic_index_in_dim)/dynamic_slice | solution.py:96
  17.7 3.5 %collective-permute-done.1 = bf16[512,256]{0,1:T(8,128)(2,1)S(1)} collective-permute-done((bf16[512,256]{0,1:T(8,128)(2,1)S(1)}, bf16[512,256]{0,1:T(8,128)(2,1)S(1)}, u32[]{:S(2)}, u32[]{:S(2)}) %collective-permute-start.1) | collective-permute-done | bytes 262176 | tf_op jit(solution)/shard_map/ppermute | solution.py:100
  21.1 0.7 convert_add_fusion
  21.8 0.6 fusion.27
  22.4 0.5 fusion.10
  23.0 1.3 %fusion.14 = bf16[64,2,2112]{2,1,0:T(2,128)(2,1)} fusion(bf16[64,2,16]{2,1,0:T(2,128)(2,1)S(1)} %convert_element_type.47, bf16[64,2,2048]{2,1,0:T(2,128)(2,1)S(1)} %reshape.55), kind=kLoop, calls=%fused_computation.19 | loop fusion | flops 1622016 | bytes 1069056 | tf_op jit(solution)/shard_map/concatenate | solution.py:119
  24.4 13.2 %all-to-all-start = ((bf16[64,2,2112]{2,1,0:T(2,128)(2,1)}), bf16[64,2,2112]{2,1,0:T(2,128)(2,1)S(1)}, u32[]{:S(2)}, u32[]{:S(2)}) async-start(bf16[64,2,2112]{2,1,0:T(2,128)(2,1)} %fusion.14), calls=%async_computation | async-start | bytes 1114112 | tf_op jit(solution)/shard_map/all_to_all | solution.py:120
  38.2 17.4 %all-to-all-done = bf16[64,2,2112]{2,1,0:T(2,128)(2,1)S(1)} async-done(((bf16[64,2,2112]{2,1,0:T(2,128)(2,1)}), bf16[64,2,2112]{2,1,0:T(2,128)(2,1)S(1)}, u32[]{:S(2)}, u32[]{:S(2)}) %all-to-all-start) | async-done | bytes 540704 | tf_op jit(solution)/shard_map/all_to_all | solution.py:120
  55.6 0.4 slice.44
  56.0 0.3 reshape.58
  56.4 0.2 reshape.60
  56.6 0.4 fusion.16
  57.0 0.7 fusion.1
  57.6 1.9 %fusion.6.kv_ref = bf16[1280,256]{1,0:T(8,128)(2,1)} fusion(bf16[1024,256]{1,0:T(8,128)(2,1)S(1)} %reshape.58, s32[1024]{0:T(1024)S(1)} %fusion.16, bf16[1,1280,1,256]{3,1,2,0:T(8,128)(2,1)S(1)} %copy-done.3, pred[1280]{0:T(1024)(128)(4,1)S(1)} %fusion.1), kind=kOutput, calls=%fused_computation.7 | convolution fusion | flops 673054720 | bytes 1840384 | tf_op jit(solution)/shard_map/dot_general | solution.py:126
  59.6 12.5 %shard_map.73 = bf16[6,1280,128]{2,1,0:T(8,128)(2,1)} custom-call(s32[1]{0:T(128)S(6)} %copy.26.len_ref, bf16[6,1280,128]{2,1,0:T(8,128)(2,1)} %bitcast.54, bf16[1280,256]{1,0:T(8,128)(2,1)} %fusion.6.kv_ref), custom_call_target="tpu_custom_call" | custom-call | tf_op jit(solution)/shard_map/pallas_call | solution.py:78
  (22 shorter events, 0.7 us)
Async XLA Ops:
  0.0 1.4 %copy-start = (bf16[512,1536]{1,0:T(8,128)(2,1)S(1)}, bf16[512,1536]{1,0:T(8,128)(2,1)}, u32[]{:S(2)}) copy-start(bf16[512,1536]{1,0:T(8,128)(2,1)} %param.9) | copy-start | bytes 4718596
  5.1 5.8 %copy-start.2 = (s32[512]{0:T(512)S(1)}, s32[512]{0:T(512)}, u32[]{:S(2)}) copy-start(s32[512]{0:T(512)} %param.11) | copy-start | bytes 6148
  5.2 5.8 %copy-start.1 = (s32[512]{0:T(512)S(1)}, s32[512]{0:T(512)}, u32[]{:S(2)}) copy-start(s32[512]{0:T(512)} %param.10) | copy-start | bytes 6148
  5.2 12.4 %collective-permute-start = (bf16[512,256]{0,1:T(8,128)(2,1)S(1)}, bf16[512,256]{0,1:T(8,128)(2,1)S(1)}, u32[]{:S(2)}, u32[]{:S(2)}) collective-permute-start(bf16[512,256]{0,1:T(8,128)(2,1)S(1)} %get-tuple-element.5), channel_id=1, source_target_pairs={{0,1},{1,2},{2,3},{3,0},{4,5},{5,6},{6,7},{7,4},{8,9},{9,10},{10,1... | collective-permute-start | bytes 786440 | tf_op jit(solution)/shard_map/ppermute | solution.py:100
  7.4 13.8 %collective-permute-start.1 = (bf16[512,256]{0,1:T(8,128)(2,1)S(1)}, bf16[512,256]{0,1:T(8,128)(2,1)S(1)}, u32[]{:S(2)}, u32[]{:S(2)}) collective-permute-start(bf16[512,256]{0,1:T(8,128)(2,1)S(1)} %get-tuple-element.7), channel_id=1, source_target_pairs={{0,2},{1,3},{2,0},{3,1},{4,6},{5,7},{6,4},{7,5},{8,10},{9,11},{10,... | collective-permute-start | bytes 786440 | tf_op jit(solution)/shard_map/ppermute | solution.py:100
  9.8 11.3 %collective-permute-start.2 = (bf16[512,256]{0,1:T(8,128)(2,1)S(1)}, bf16[512,256]{0,1:T(8,128)(2,1)S(1)}, u32[]{:S(2)}, u32[]{:S(2)}) collective-permute-start(bf16[512,256]{0,1:T(8,128)(2,1)S(1)} %get-tuple-element.6), channel_id=1, source_target_pairs={{0,3},{1,0},{2,1},{3,2},{4,7},{5,4},{6,5},{7,6},{8,11},{9,8},{10,9... | collective-permute-start | bytes 786440 | tf_op jit(solution)/shard_map/ppermute | solution.py:100
  24.4 31.3 %all-to-all-start = ((bf16[64,2,2112]{2,1,0:T(2,128)(2,1)}), bf16[64,2,2112]{2,1,0:T(2,128)(2,1)S(1)}, u32[]{:S(2)}, u32[]{:S(2)}) async-start(bf16[64,2,2112]{2,1,0:T(2,128)(2,1)} %fusion.14), calls=%async_computation | async-start | bytes 1114112 | tf_op jit(solution)/shard_map/all_to_all | solution.py:120
  56.3 1.3 %copy-start.3 = (bf16[1,1280,1,256]{3,1,2,0:T(8,128)(2,1)S(1)}, bf16[1,1280,1,256]{3,1,2,0:T(8,128)(2,1)}, u32[]{:S(2)}) copy-start(bf16[1,1280,1,256]{3,1,2,0:T(8,128)(2,1)} %param.8) | copy-start | bytes 1966084

commit v18 on v12

--- a/solution.py
+++ b/solution.py
@@ -58,7 +58,7 @@
 
 def attend(heads_first, prompt_kv, length, head_dim, block=256):
     heads, prompt, _ = heads_first.shape
-    group = math.gcd(heads, 3)
+    group = math.gcd(heads, 6)
     grid_spec = pltpu.PrefetchScalarGridSpec(
         num_scalar_prefetch=1,
         grid=(heads // group,),

time: 72.4 us -> 72.6 us (level)
  no operation moved by 1% of the time
where the time goes in v18:
time: 72.6 us; the launch traced here: 72.3 us
  waiting for transfers between devices  20.7 us (29%)
  starting transfers between devices  19.1 us (26%)
  Pallas kernels  12.7 us (17%)
  matrix products  7.84 us (11%)
  local copies, waits for them, and re-layouts  6.75 us (9%)
  other arithmetic  4.35 us (6%)
  between operations  0.83 us (1%)
    all_to_all x1, waiting for transfers between devices, per_device(): got = lax.all_to_all(packet, 'req', split_axis=0, concat_axis=0, tiled=True)  17.2 us
    all_to_all x1, starting transfers between devices, per_device(): got = lax.all_to_all(packet, 'req', split_axis=0, concat_axis=0, tiled=True)  13.4 us
    pallas_call x1, Pallas kernels, attend(): pl.pallas_call(functools.partial(attention_kernel, block, head_dim, group...  12.7 us
    ppermute x3, starting transfers between devices, per_device(): lax.ppermute(outgoing, 'tp', perm=[(i, (i + shift) % heads) for i in rang...  5.72 us
    dot_general x1, matrix products, per_device(): jnp.einsum('rd,dhc->hrc', image_rows, kv_weight, preferred_element_type=j...  3.72 us
    dynamic_slice x1, local copies, waits for them, and re-layouts, per_device(): own_weight = lax.dynamic_index_in_dim(kv_weight, me, axis=1, keepdims=False)  3.57 us
    ppermute x3, waiting for transfers between devices, per_device(): lax.ppermute(outgoing, 'tp', perm=[(i, (i + shift) % heads) for i in rang...  3.48 us
    dot_general x1, matrix products, per_device(): jnp.dot(match.astype(jnp.bfloat16), got_kv, preferred_element_type=jnp.fl...  1.93 us
  transfers between devices with their start and end apart: 4, of which 2 were waited for; matrix products, arithmetic and copies ran while one was open for 9% of the time, Pallas kernels for 0%

profile of v18, /device:TPU:1, one launch (start us, length us, event | category | flops | bytes accessed | tf_op | source)
XLA Modules:
  0.0 72.3 jit_solution(16427596118665616501)
XLA Ops:
  0.0 1.4 %copy-done = bf16[512,1536]{1,0:T(8,128)(2,1)S(1)} copy-done((bf16[512,1536]{1,0:T(8,128)(2,1)S(1)}, bf16[512,1536]{1,0:T(8,128)(2,1)}, u32[]{:S(2)}) %copy-start) | copy-done | bytes 1572888
  1.4 3.7 %fusion.2 = bf16[4,256,512]{2,1,0:T(8,128)(2,1)S(1)} fusion(bf16[1536,4,256]{2,1,0:T(4,128)(2,1)} %param.13, bf16[512,1536]{1,0:T(8,128)(2,1)S(1)} %copy-done), kind=kOutput, calls=%fused_computation.3 | convolution fusion | flops 1610612736 | bytes 5767168 | tf_op jit(solution)/shard_map/rd,dhc->hrc/dot_general | solution.py:88
  5.2 2.1 %collective-permute-start = (bf16[512,256]{0,1:T(8,128)(2,1)S(1)}, bf16[512,256]{0,1:T(8,128)(2,1)S(1)}, u32[]{:S(2)}, u32[]{:S(2)}) collective-permute-start(bf16[512,256]{0,1:T(8,128)(2,1)S(1)} %get-tuple-element.5), channel_id=1, source_target_pairs={{0,1},{1,2},{2,3},{3,0},{4,5},{5,6},{6,7},{7,4},{8,9},{9,10},{10,1... | collective-permute-start | bytes 786440 | tf_op jit(solution)/shard_map/ppermute | solution.py:94
  7.4 2.5 %collective-permute-start.1 = (bf16[512,256]{0,1:T(8,128)(2,1)S(1)}, bf16[512,256]{0,1:T(8,128)(2,1)S(1)}, u32[]{:S(2)}, u32[]{:S(2)}) collective-permute-start(bf16[512,256]{0,1:T(8,128)(2,1)S(1)} %get-tuple-element.7), channel_id=1, source_target_pairs={{0,2},{1,3},{2,0},{3,1},{4,6},{5,7},{6,4},{7,5},{8,10},{9,11},{10,... | collective-permute-start | bytes 786440 | tf_op jit(solution)/shard_map/ppermute | solution.py:94
  9.8 1.2 %collective-permute-start.2 = (bf16[512,256]{0,1:T(8,128)(2,1)S(1)}, bf16[512,256]{0,1:T(8,128)(2,1)S(1)}, u32[]{:S(2)}, u32[]{:S(2)}) collective-permute-start(bf16[512,256]{0,1:T(8,128)(2,1)S(1)} %get-tuple-element.6), channel_id=1, source_target_pairs={{0,3},{1,0},{2,1},{3,2},{4,7},{5,4},{6,5},{7,6},{8,11},{9,8},{10,9... | collective-permute-start | bytes 786440 | tf_op jit(solution)/shard_map/ppermute | solution.py:94
  11.0 1.2 %reduce-window.6 = s32[64,4,128]{2,0,1:T(8,128)S(1)} reduce-window(s32[64,4,128]{2,0,1:T(8,128)S(1)} %fusion.33, s32[]{:T(128)} %constant.52.clone.1), window={size=1x1x128 pad=0_0x0_0x127_0}, to_apply=%region_0.1 | reduce-window | flops 4161536 | bytes 262148 | tf_op jit(solution)/shard_map/reduce-window
  12.2 0.2 slice_reduce_fusion
  12.6 1.0 %fusion.11 = bf16[1024,2]{0,1:T(2,128)(2,1)S(1)} fusion(s32[512]{0:T(512)S(1)} %multiply_add_fusion, f32[512,1]{0,1:T(1,128)S(1)} %bitcast.57, f32[512,1]{0,1:T(1,128)S(1)} %bitcast.56), kind=kOutput, calls=%fused_computation.15 | convolution fusion | flops 13110272 | bytes 10240 | tf_op jit(solution)/shard_map/dot_general | solution.py:110
  13.6 0.2 copy.16
  14.1 3.6 %constant_dynamic-slice_fusion = bf16[1536,1,256]{2,1,0:T(2,128)(2,1)S(1)} fusion(bf16[1536,4,256]{2,1,0:T(4,128)(2,1)} %param.13, s32[]{:T(128)S(6)} %select_n.33), kind=kLoop, calls=%fused_computation.60 | loop fusion | bytes 1572868 | tf_op jit(solution)/shard_map/jit(dynamic_index_in_dim)/dynamic_slice | solution.py:90
  17.7 3.5 %collective-permute-done.1 = bf16[512,256]{0,1:T(8,128)(2,1)S(1)} collective-permute-done((bf16[512,256]{0,1:T(8,128)(2,1)S(1)}, bf16[512,256]{0,1:T(8,128)(2,1)S(1)}, u32[]{:S(2)}, u32[]{:S(2)}) %collective-permute-start.1) | collective-permute-done | bytes 262176 | tf_op jit(solution)/shard_map/ppermute | solution.py:94
  21.1 0.7 convert_add_fusion
  21.8 0.6 fusion.27
  22.4 0.5 fusion.10
  23.0 1.3 %fusion.14 = bf16[64,2,2112]{2,1,0:T(2,128)(2,1)} fusion(bf16[64,2,16]{2,1,0:T(2,128)(2,1)S(1)} %convert_element_type.47, bf16[64,2,2048]{2,1,0:T(2,128)(2,1)S(1)} %reshape.55), kind=kLoop, calls=%fused_computation.19 | loop fusion | flops 1622016 | bytes 1069056 | tf_op jit(solution)/shard_map/concatenate | solution.py:113
  24.4 13.4 %all-to-all-start = ((bf16[64,2,2112]{2,1,0:T(2,128)(2,1)}), bf16[64,2,2112]{2,1,0:T(2,128)(2,1)S(1)}, u32[]{:S(2)}, u32[]{:S(2)}) async-start(bf16[64,2,2112]{2,1,0:T(2,128)(2,1)} %fusion.14), calls=%async_computation | async-start | bytes 1114112 | tf_op jit(solution)/shard_map/all_to_all | solution.py:114
  38.4 17.2 %all-to-all-done = bf16[64,2,2112]{2,1,0:T(2,128)(2,1)S(1)} async-done(((bf16[64,2,2112]{2,1,0:T(2,128)(2,1)}), bf16[64,2,2112]{2,1,0:T(2,128)(2,1)S(1)}, u32[]{:S(2)}, u32[]{:S(2)}) %all-to-all-start) | async-done | bytes 540704 | tf_op jit(solution)/shard_map/all_to_all | solution.py:114
  55.6 0.4 slice.44
  56.0 0.3 reshape.58
  56.4 0.2 reshape.60
  56.6 0.4 fusion.16
  57.0 0.7 fusion.1
  57.6 1.9 %fusion.6.kv_ref = bf16[1280,256]{1,0:T(8,128)(2,1)} fusion(bf16[1024,256]{1,0:T(8,128)(2,1)S(1)} %reshape.58, s32[1024]{0:T(1024)S(1)} %fusion.16, bf16[1,1280,1,256]{3,1,2,0:T(8,128)(2,1)S(1)} %copy-done.3, pred[1280]{0:T(1024)(128)(4,1)S(1)} %fusion.1), kind=kOutput, calls=%fused_computation.7 | convolution fusion | flops 673054720 | bytes 1840384 | tf_op jit(solution)/shard_map/dot_general | solution.py:120
  59.6 12.7 %shard_map.73 = bf16[6,1280,128]{2,1,0:T(8,128)(2,1)} custom-call(s32[1]{0:T(128)S(6)} %copy.26.len_ref, bf16[6,1280,128]{2,1,0:T(8,128)(2,1)} %bitcast.54, bf16[1280,256]{1,0:T(8,128)(2,1)} %fusion.6.kv_ref), custom_call_target="tpu_custom_call" | custom-call | tf_op jit(solution)/shard_map/pallas_call | solution.py:72
  (22 shorter events, 0.7 us)
Async XLA Ops:
  0.0 1.4 %copy-start = (bf16[512,1536]{1,0:T(8,128)(2,1)S(1)}, bf16[512,1536]{1,0:T(8,128)(2,1)}, u32[]{:S(2)}) copy-start(bf16[512,1536]{1,0:T(8,128)(2,1)} %param.9) | copy-start | bytes 4718596
  5.1 5.8 %copy-start.2 = (s32[512]{0:T(512)S(1)}, s32[512]{0:T(512)}, u32[]{:S(2)}) copy-start(s32[512]{0:T(512)} %param.11) | copy-start | bytes 6148
  5.2 5.8 %copy-start.1 = (s32[512]{0:T(512)S(1)}, s32[512]{0:T(512)}, u32[]{:S(2)}) copy-start(s32[512]{0:T(512)} %param.10) | copy-start | bytes 6148
  5.2 12.4 %collective-permute-start = (bf16[512,256]{0,1:T(8,128)(2,1)S(1)}, bf16[512,256]{0,1:T(8,128)(2,1)S(1)}, u32[]{:S(2)}, u32[]{:S(2)}) collective-permute-start(bf16[512,256]{0,1:T(8,128)(2,1)S(1)} %get-tuple-element.5), channel_id=1, source_target_pairs={{0,1},{1,2},{2,3},{3,0},{4,5},{5,6},{6,7},{7,4},{8,9},{9,10},{10,1... | collective-permute-start | bytes 786440 | tf_op jit(solution)/shard_map/ppermute | solution.py:94
  7.4 13.8 %collective-permute-start.1 = (bf16[512,256]{0,1:T(8,128)(2,1)S(1)}, bf16[512,256]{0,1:T(8,128)(2,1)S(1)}, u32[]{:S(2)}, u32[]{:S(2)}) collective-permute-start(bf16[512,256]{0,1:T(8,128)(2,1)S(1)} %get-tuple-element.7), channel_id=1, source_target_pairs={{0,2},{1,3},{2,0},{3,1},{4,6},{5,7},{6,4},{7,5},{8,10},{9,11},{10,... | collective-permute-start | bytes 786440 | tf_op jit(solution)/shard_map/ppermute | solution.py:94
  9.8 11.3 %collective-permute-start.2 = (bf16[512,256]{0,1:T(8,128)(2,1)S(1)}, bf16[512,256]{0,1:T(8,128)(2,1)S(1)}, u32[]{:S(2)}, u32[]{:S(2)}) collective-permute-start(bf16[512,256]{0,1:T(8,128)(2,1)S(1)} %get-tuple-element.6), channel_id=1, source_target_pairs={{0,3},{1,0},{2,1},{3,2},{4,7},{5,4},{6,5},{7,6},{8,11},{9,8},{10,9... | collective-permute-start | bytes 786440 | tf_op jit(solution)/shard_map/ppermute | solution.py:94
  24.4 31.3 %all-to-all-start = ((bf16[64,2,2112]{2,1,0:T(2,128)(2,1)}), bf16[64,2,2112]{2,1,0:T(2,128)(2,1)S(1)}, u32[]{:S(2)}, u32[]{:S(2)}) async-start(bf16[64,2,2112]{2,1,0:T(2,128)(2,1)} %fusion.14), calls=%async_computation | async-start | bytes 1114112 | tf_op jit(solution)/shard_map/all_to_all | solution.py:114
  56.3 1.3 %copy-start.3 = (bf16[1,1280,1,256]{3,1,2,0:T(8,128)(2,1)S(1)}, bf16[1,1280,1,256]{3,1,2,0:T(8,128)(2,1)}, u32[]{:S(2)}) copy-start(bf16[1,1280,1,256]{3,1,2,0:T(8,128)(2,1)} %param.8) | copy-start | bytes 1966084
